TPU v7x, 32 devices: a whole 2x2x4 slice. The times are simulated.
32 devices in a mesh: row: 8 (over y, x, core), col: 4 (over z).
Axes of the slice: x: 2, y: 2, z: 4, core: 2. Of those that a mesh axis runs over, the one named last changes fastest.
Arguments:
- magnetic_potential_input: bfloat16 [32, 32768], P('row', 'col'), may hold values from -6 to 6
- node_reordering: int32 [32768], P('col'), may hold values from 0 to 32767, as said below
- adjacent_dense_blocks: bfloat16 [512, 256, 256], P(('row', 'col')), may hold values from -0.375 to 0.375
- adjacent_cluster_pairs: int32 [512, 2], P(('row', 'col')), may hold values from 0 to 127, as said below
- distant_row_factors: bfloat16 [960, 256, 32], P(('row', 'col')), may hold values from -1 to 1
- distant_row_factor_index: int32 [960, 2], P(('row', 'col')), may hold values from 0 to 127, as said below
- distant_column_factors: bfloat16 [960, 256, 32], P(('row', 'col')), may hold values from -0.125 to 0.125
- distant_column_factor_index: int32 [960, 2], P(('row', 'col')), may hold values from 0 to 127, as said below
Outputs:
- field: float32 [32, 32768], P('col', 'row')
Inputs may be any that keep to these rules, and one draw needn't show every extreme that they name: `node_reordering`: each column block of positions k * 32 * 256 to (k + 1) * 32 * 256 - 1 is mapped one to one onto the initial nodes of the same range. `adjacent_cluster_pairs`: slot of device d with row index i: the row cluster lies in i * 16 to (i + 1) * 16 - 1; the column cluster lies within 3 of the row cluster and in column block h = i * (col devices) // (row devices), clusters h * 32 to (h + 1) * 32 - 1. `distant_row_factor_index`: piece of device d with row index i: column 0 is a leaf cluster in i * 16 to (i + 1) * 16 - 1; column 1 is a block slot 0 to 7. A block of level l has 2**l row pieces on 2**l aligned consecutive clusters; each level 0 to 3 has 2 blocks a device. `distant_column_factor_index`: piece of device d with col index j: column 0 is a leaf cluster in j * 32 to (j + 1) * 32 - 1; column 1 is a block slot as in distant_row_factor_index; a block has as many column pieces as row pieces, on aligned consecutive clusters.
All inputs are finite; a program needn't handle non-finite values.
Results may differ from a plain program's by a relative error of at most 0.0023.
Values may be sent and summed in bfloat16 or wider, within the bound.
No kernel may reach another device: no remote copies, remote signals or barrier semaphores. Data moves between devices by JAX's collectives and lax.ppermute only.
A program may use at most 64 MiB of HBM per device.

v0:
```python
import jax
import jax.numpy as jnp
from jax import lax
from jax.sharding import PartitionSpec as P

BL = 2


def from_root(shard, axis, root):
    mine = lax.axis_index(axis) == root
    return lax.psum(jnp.where(mine, shard, jnp.zeros_like(shard)), axis)


def per_device(
    magnetic_potential_input,
    node_reordering,
    adjacent_dense_blocks,
    adjacent_cluster_pairs,
    distant_row_factors,
    distant_row_factor_index,
    distant_column_factors,
    distant_column_factor_index,
):
    row_count = lax.axis_size("row")
    col_count = lax.axis_size("col")
    row_index = lax.axis_index("row")
    column_index_list = lax.axis_index("col")
    gathered = lax.all_gather(magnetic_potential_input, "row", axis=0, tiled=True)
    states = gathered.shape[0]
    width = gathered.shape[1]
    leaf = adjacent_dense_blocks.shape[1]
    rank = distant_row_factors.shape[2]
    cluster_extent = width // leaf
    row_span = cluster_extent * col_count // row_count
    local_order = node_reordering - column_index_list * width
    leaf_clusters = (
        jnp.take(gathered, local_order, axis=1)
        .reshape(states, cluster_extent, leaf)
        .transpose(1, 0, 2)
    )
    home = row_index * col_count // row_count
    near_cols = adjacent_cluster_pairs[:, 1] - home * cluster_extent
    near_rows = adjacent_cluster_pairs[:, 0] - row_index * row_span
    home_leaves = from_root(leaf_clusters, "col", home)
    near_src = jnp.take(home_leaves, near_cols, axis=0)
    factor_fragments = distant_column_factors.shape[0]
    block_entries = 4 * BL
    distant_source_values = jnp.take(
        leaf_clusters,
        distant_column_factor_index[:, 0] - column_index_list * cluster_extent,
        axis=0,
    )
    column_indicator = (
        distant_column_factor_index[:, 1][None, :]
        == jnp.arange(block_entries, dtype=jnp.int32)[:, None]
    ).astype(jnp.float32)
    u_onehot = (
        distant_row_factor_index[:, 1][:, None]
        == jnp.arange(block_entries, dtype=jnp.int32)[None, :]
    ).astype(jnp.bfloat16)
    u_rows = distant_row_factor_index[:, 0] - row_index * row_span
    near_out = jnp.einsum(
        "nsk,nlk->snl", near_src, adjacent_dense_blocks, preferred_element_type=jnp.float32
    )
    coeffs = jnp.einsum(
        "psk,pkr->prs",
        distant_source_values,
        distant_column_factors,
        preferred_element_type=jnp.float32,
    )
    summed = jnp.dot(
        column_indicator,
        coeffs.reshape(factor_fragments, rank * states),
        precision=lax.Precision.HIGHEST,
    ).astype(jnp.bfloat16)
    picked = (
        jnp.dot(u_onehot, summed, preferred_element_type=jnp.float32)
        .astype(jnp.bfloat16)
        .reshape(factor_fragments, rank, states)
    )
    far_out = jnp.einsum(
        "prs,plr->spl", picked, distant_row_factors, preferred_element_type=jnp.float32
    )
    partial_sum = jnp.zeros((states, row_span, leaf), jnp.float32)
    partial_sum = partial_sum.at[:, near_rows].add(near_out)
    partial_sum = partial_sum.at[:, u_rows].add(far_out)
    partial_sum = partial_sum.reshape(states, row_span * leaf)
    return lax.psum_scatter(partial_sum, "col", scatter_dimension=0, tiled=True)


def solution(mesh):
    placed = (
        P("row", "col"),
        P("col"),
        P(("row", "col"), None, None),
        P(("row", "col"), None),
        P(("row", "col"), None, None),
        P(("row", "col"), None),
        P(("row", "col"), None, None),
        P(("row", "col"), None),
    )
    return jax.shard_map(
        per_device, mesh=mesh, in_specs=placed, out_specs=P("col", "row"), check_vma=False
    )
```

profile of v0, /device:TPU:0, one launch (start us, length us, event | category | flops | bytes accessed | tf_op | source)
XLA Modules:
  0.0 130.4 jit_solution(13971784443278825169)
XLA Ops:
  6.5 0.0 copy-start
  6.5 0.0 all-reduce.2.cloned.1.call-start
  6.5 0.9 fusion.7
  7.5 0.8 compare_and_fusion
  8.3 11.6 %all-gather = bf16[8,4,8192]{2,1,0:T(4,128)(2,1)S(1)} all-gather(bf16[1,4,8192]{2,1,0:T(4,128)(2,1)} %bitcast.34), channel_id=1, replica_groups=mesh['row'=8,'col'=4] {'row'}, dimensions={0}, use_global_device_ids=true | all-gather | bytes 589824 | tf_op jit(solution)/shard_map/all_gather | solution.py:28
  19.9 0.1 reshape.75
  20.0 1.8 %copy.16 = bf16[32,8192]{0,1:T(8,128)(2,1)} copy(bf16[32,8192]{1,0:T(8,128)(2,1)S(1)} %reshape.75) | data formatting | bytes 1048576
  21.8 30.1 %gather_fusion = bf16[8192,32]{1,0:T(8,128)(2,1)} fusion(bf16[32,8192]{0,1:T(8,128)(2,1)} %copy.16, s32[8192]{0:T(1024)S(1)} %fusion.7), kind=kCustom, calls=%fused_computation | custom fusion | bytes 1081344 | tf_op jit(solution)/shard_map/jit(_take)/gather | solution.py:37
  51.8 0.0 copy-start.2
  51.9 1.9 %copy.17 = bf16[32,32,256]{2,0,1:T(8,128)(2,1)S(1)} copy(bf16[32,32,256]{0,2,1:T(8,128)(2,1)} %bitcast.32) | data formatting | bytes 1048576 | tf_op jit(solution)/shard_map/jit(_take)/gather | solution.py:37
  53.8 0.9 broadcast_select_fusion
  54.7 0.0 all-reduce.2.cloned.1.call-update
  54.7 0.0 reduce-scatter.2.cloned.1.call-start
  54.7 0.0 copy-done.2
  54.8 0.0 copy-start.1
  54.8 0.0 copy-start.3
  54.8 0.6 gather_fusion.2
  55.4 1.4 %convolution_bitcast_fusion = f32[30,32,32]{1,2,0:T(8,128)S(1)} fusion(bf16[30,256,32]{1,2,0:T(8,128)(2,1)} %param.14, bf16[30,32,256]{2,1,0:T(8,128)(2,1)S(1)} %gather_fusion.2, pred[30]{0:T(512)(128)(4,1)S(1)} %get-tuple-element.5), kind=kOutput, calls=%fused_computation.5 | convolution fusion | flops 15974400 | bytes 1105950 | tf_op jit(solution)/shard_map/psk,pkr->prs/dot_general | solution.py:65
  56.8 0.2 copy.18
  57.0 0.2 reshape.30
  57.2 0.2 convolution_convert_fusion.1
  57.4 0.0 copy-done.1
  57.4 0.2 convolution_convert_fusion
  57.6 0.0 copy-done.3
  57.7 0.2 reshape.31
  57.9 2.3 %fusion.14 = f32[30,32,256]{2,1,0:T(8,128)} fusion(bf16[30,32,32]{2,1,0:T(8,128)(2,1)S(1)} %reshape.31, bf16[30,256,32]{1,2,0:T(8,128)(2,1)} %param.12), kind=kOutput, calls=%fused_computation.38 | convolution fusion | flops 15728640 | bytes 1536000 | tf_op jit(solution)/shard_map/prs,plr->spl/dot_general | solution.py:81
  60.2 33.2 %all-reduce.2.cloned.1.call-done = bf16[32,32,256]{2,1,0:T(8,128)(2,1)} async-done(((bf16[32,32,256]{2,1,0:T(8,128)(2,1)}), bf16[32,32,256]{2,1,0:T(8,128)(2,1)}) %all-reduce.2.cloned.1.call-update) | async-done | bytes 524304 | tf_op jit(solution)/shard_map/psum | solution.py:11
  93.4 1.6 %gather_fusion.1 = bf16[16,32,256]{2,1,0:T(8,128)(2,1)S(1)} fusion(bf16[32,32,256]{2,1,0:T(8,128)(2,1)} %all-reduce.2.cloned.1.call-done, s32[1024]{0:T(1024)S(1)} %pad_clamp_fusion.1), kind=kCustom, calls=%fused_computation.1 | custom fusion | bytes 524352 | tf_op jit(solution)/shard_map/jit(_take)/gather | solution.py:45
  95.1 0.0 copy-done
  95.1 0.7 fusion.2
  95.8 0.1 broadcast_in_dim.44
  95.8 1.3 %scatter_fusion = f32[32,16,256]{2,0,1:T(8,128)S(1)} fusion(f32[32,16,256]{2,0,1:T(8,128)S(1)} %broadcast_in_dim.44, s32[16]{0:T(128)S(1)} %fusion.10, f32[16,32,256]{2,1,0:T(8,128)S(1)} %fusion.2), kind=kCustom, calls=%fused_computation.3 | custom fusion | flops 131072 | bytes 1572928 | tf_op jit(solution)/shard_map/scatter-add | solution.py:85
  97.2 3.8 %scatter_fusion.1 = f32[32,16,256]{2,0,1:T(8,128)S(1)} fusion(f32[32,16,256]{2,0,1:T(8,128)S(1)} %scatter_fusion, s32[30]{0:T(128)S(1)} %get-tuple-element.12, f32[30,32,256]{2,1,0:T(8,128)} %fusion.14), kind=kCustom, calls=%fused_computation.4 | custom fusion | flops 245760 | bytes 2949240 | tf_op jit(solution)/shard_map/scatter-add | solution.py:86
  101.0 0.8 copy.22
  101.8 0.0 reduce-scatter.2.cloned.1.call-update
  101.8 21.8 %reduce-scatter.2.cloned.1.call-done = f32[8,4096]{1,0:T(8,128)} async-done(((f32[32,4096]{1,0:T(8,128)}), f32[8,4096]{1,0:T(8,128)}) %reduce-scatter.2.cloned.1.call-update) | async-done | bytes 131088 | tf_op jit(solution)/shard_map/reduce_scatter | solution.py:88
  (8 shorter events, 0.1 us)
Async XLA Ops:
  6.5 88.5 %copy-start = (bf16[16,256,256]{2,1,0:T(8,128)(2,1)S(1)}, bf16[16,256,256]{2,1,0:T(8,128)(2,1)}, u32[]{:S(2)}) copy-start(bf16[16,256,256]{2,1,0:T(8,128)(2,1)} %param.10) | copy-start | bytes 6291460
  6.5 86.9 %all-reduce.2.cloned.1.call-start = ((), (), s32[]{:S(2)}) async-start(), calls=%async_computation.1 | async-start | bytes 1048576 | tf_op jit(solution)/shard_map/psum | solution.py:11
  51.8 2.9 %copy-start.2 = (s32[30,2]{0,1:T(2,128)S(1)}, s32[30,2]{0,1:T(2,128)}, u32[]{:S(2)}) copy-start(s32[30,2]{0,1:T(2,128)} %param.15) | copy-start | bytes 724
  54.7 68.9 %reduce-scatter.2.cloned.1.call-start = ((), (), s32[]{:S(2)}) async-start(), calls=%async_computation.2 | async-start | bytes 655360 | tf_op jit(solution)/shard_map/reduce_scatter | solution.py:88
  54.8 2.6 %copy-start.1 = (s32[30,2]{0,1:T(2,128)S(1)}, s32[30,2]{0,1:T(2,128)}, u32[]{:S(2)}) copy-start(s32[30,2]{0,1:T(2,128)} %param.13) | copy-start | bytes 724
  54.8 2.8 %copy-start.3 = (s32[16,2]{0,1:T(2,128)S(1)}, s32[16,2]{0,1:T(2,128)}, u32[]{:S(2)}) copy-start(s32[16,2]{0,1:T(2,128)} %param.11) | copy-start | bytes 388
Sparse Core Ops, SparseCore 0:
  54.8 38.5 all-reduce.1
  101.9 21.6 reduce-scatter.1
where the time goes:
time: 131 us; the launch traced here: 130 us
  waiting for transfers between devices  55.1 us (42%)
  local copies, waits for them, and re-layouts  37.6 us (29%)
  between operations  13.6 us (10%)
  blocking collectives  11.6 us (9%)
  other arithmetic  7.75 us (6%)
  matrix products  4.8 us (4%)
    psum x1, waiting for transfers between devices, from_root(): return lax.psum(jnp.where(mine, shard, jnp.zeros_like(shard)), axis)  33.2 us
    gather x2, local copies, waits for them, and re-layouts, per_device(): jnp.take(gathered, local_order, axis=1)  31.9 us
    reduce_scatter x1, waiting for transfers between devices, per_device(): return lax.psum_scatter(partial_sum, 'col', scatter_dimension=0, tiled=True)  21.8 us
    all_gather x1, blocking collectives, per_device(): lax.all_gather(magnetic_potential_input, 'row', axis=0, tiled=True)  11.6 us
    scatter-add x1, other arithmetic, per_device(): partial_sum = partial_sum.at[:, u_rows].add(far_out)  3.76 us
  transfers between devices with their start and end apart: 2, of which 2 were waited for; matrix products, arithmetic and copies ran while one was open for 4% of the time, Pallas kernels for 0%

commit v1 on v0

v1 whole, which is shorter than its diff:
```python
import jax
import jax.numpy as jnp
from jax import lax
from jax.sharding import PartitionSpec as P

BL = 2
REACH = 3


def per_device(
    magnetic_potential_input,
    node_reordering,
    adjacent_dense_blocks,
    adjacent_cluster_pairs,
    distant_row_factors,
    distant_row_factor_index,
    distant_column_factors,
    distant_column_factor_index,
):
    row_count = lax.axis_size("row")
    col_count = lax.axis_size("col")
    row_index = lax.axis_index("row")
    col_index = lax.axis_index("col")
    local_states, width = magnetic_potential_input.shape
    states = local_states * row_count
    leaf = adjacent_dense_blocks.shape[1]
    rank = distant_row_factors.shape[2]
    cluster_extent = width // leaf
    row_span = cluster_extent * col_count // row_count
    window = 0
    for target in range(row_count):
        base_t = target * row_span - target * col_count // row_count * cluster_extent
        low_t = max(base_t - REACH, 0)
        high_t = min(base_t + row_span + REACH, cluster_extent)
        window = max(window, high_t - low_t)
    block_entries = 4 * BL

    local_order = node_reordering - col_index * width
    mine = jnp.take(magnetic_potential_input, local_order, axis=1)

    ordered = lax.all_gather(mine, "row", axis=0, tiled=True)
    leaf_clusters = ordered.reshape(states, cluster_extent, leaf)

    every_block = lax.all_gather(mine, "col", axis=0, tiled=False)
    pieces = []
    for target in range(row_count):
        home_t = target * col_count // row_count
        start_t = min(max(target * row_span - home_t * cluster_extent - REACH, 0), cluster_extent - window)
        pieces.append(every_block[home_t, :, start_t * leaf:(start_t + window) * leaf])
    send = jnp.concatenate(pieces, axis=0)
    near_window = lax.all_to_all(send, "row", 0, 0, tiled=True).reshape(states, window, leaf)

    home = row_index * col_count // row_count
    start = jnp.clip(row_index * row_span - home * cluster_extent - REACH, 0, cluster_extent - window)
    near_cols = adjacent_cluster_pairs[:, 1] - home * cluster_extent - start
    near_rows = adjacent_cluster_pairs[:, 0] - row_index * row_span
    near_src = jnp.take(near_window, near_cols, axis=1)
    near_out = jnp.einsum(
        "snk,nlk->nsl", near_src, adjacent_dense_blocks, preferred_element_type=jnp.float32
    )

    v_src = jnp.take(leaf_clusters, distant_column_factor_index[:, 0] - col_index * cluster_extent, axis=1)
    coeffs = jnp.einsum(
        "spk,pkr->psr", v_src, distant_column_factors, preferred_element_type=jnp.float32
    )
    fragments = coeffs.shape[0]
    column_indicator = (
        distant_column_factor_index[:, 1][None, :]
        == jnp.arange(block_entries, dtype=jnp.int32)[:, None]
    ).astype(jnp.float32)
    summed = jnp.dot(
        column_indicator,
        coeffs.reshape(fragments, states * rank),
        precision=lax.Precision.HIGHEST,
    ).astype(jnp.bfloat16).reshape(block_entries, states, rank)
    picked = jnp.take(summed, distant_row_factor_index[:, 1], axis=0)
    far_out = jnp.einsum(
        "psr,plr->psl", picked, distant_row_factors, preferred_element_type=jnp.float32
    )

    all_out = jnp.concatenate([near_out, far_out], axis=0)
    all_rows = jnp.concatenate([near_rows, distant_row_factor_index[:, 0] - row_index * row_span])
    scatter = (
        all_rows[None, :] == jnp.arange(row_span, dtype=jnp.int32)[:, None]
    ).astype(jnp.float32)
    partial_sum = jnp.dot(
        scatter,
        all_out.reshape(all_out.shape[0], states * leaf),
        precision=lax.Precision.HIGHEST,
    ).reshape(row_span, states, leaf)
    partial_sum = partial_sum.transpose(1, 0, 2).reshape(states, row_span * leaf)
    return lax.psum_scatter(partial_sum, "col", scatter_dimension=0, tiled=True)


def solution(mesh):
    placed = (
        P("row", "col"),
        P("col"),
        P(("row", "col"), None, None),
        P(("row", "col"), None),
        P(("row", "col"), None, None),
        P(("row", "col"), None),
        P(("row", "col"), None, None),
        P(("row", "col"), None),
    )
    return jax.shard_map(
        per_device, mesh=mesh, in_specs=placed, out_specs=P("col", "row"), check_vma=False
    )
```

time: 131 us -> 133 us (1.015)
  waiting for transfers between devices: 55.1 us -> 22.4 us
  blocking collectives: 11.6 us -> 25.8 us
  local copies, waits for them, and re-layouts: 37.6 us -> 46.4 us
  other arithmetic: 7.75 us -> 15.1 us
  starting transfers between devices: 0.04 us -> 4.12 us
    psum x1 -> x0, waiting for transfers between devices: 33.2 us -> none  [from_root(): return lax.psum(jnp.where(mine, shard, jnp.zeros_like(shard)), axis)]
    all_gather x1 -> x2, blocking collectives: 11.6 us -> 25.8 us  [the longest x1 15.6 us: per_device(): every_block = lax.all_gather(mine, 'col', axis=0, tiled=False)]
    unnamed x0 -> x1, other arithmetic: none -> 6.58 us
    select_n x2 -> x1, other arithmetic: 0.91 us -> 6.55 us  [per_device(): mine = jnp.take(magnetic_potential_input, local_order, axis=1)]
    scatter-add x2 -> x0, other arithmetic: 5.09 us -> none  [the longest x1 3.76 us: per_device(): partial_sum = partial_sum.at[:, u_rows].add(far_out)]
    all_to_all x0 -> x1, starting transfers between devices: none -> 4.08 us  [per_device(): lax.all_to_all(send, 'row', 0, 0, tiled=True).reshape(states, window, leaf)]
    unnamed x10 -> x11, local copies, waits for them, and re-layouts: 1.92 us -> 5.71 us
    reshape x3 -> x6, local copies, waits for them, and re-layouts: 1.24 us -> 4.75 us  [the longest x2 2.49 us: per_device(): leaf_clusters = ordered.reshape(states, cluster_extent, leaf)]
  transfers between devices with their start and end apart: 2 -> 2, of which waited for: 2 -> 1; matrix products, arithmetic and copies ran while one was open for 4% -> 12% of each run, Pallas kernels for 0% -> 0%
where the time goes in v1:
time: 133 us
  local copies, waits for them, and re-layouts  46.4 us (35%)
  blocking collectives  25.8 us (19%)
  waiting for transfers between devices  22.4 us (17%)
  other arithmetic  15.1 us (11%)
  between operations  13.7 us (10%)
  matrix products  5.1 us (4%)
  starting transfers between devices  4.12 us (3%)
    gather x1, local copies, waits for them, and re-layouts, per_device(): mine = jnp.take(magnetic_potential_input, local_order, axis=1)  30 us
    reduce_scatter x1, waiting for transfers between devices, per_device(): return lax.psum_scatter(partial_sum, 'col', scatter_dimension=0, tiled=True)  22.4 us
    all_gather x1, blocking collectives, per_device(): every_block = lax.all_gather(mine, 'col', axis=0, tiled=False)  15.6 us
    all_gather x1, blocking collectives, per_device(): ordered = lax.all_gather(mine, 'row', axis=0, tiled=True)  10.2 us
    unnamed x1, other arithmetic  6.58 us
    select_n x1, other arithmetic, per_device(): mine = jnp.take(magnetic_potential_input, local_order, axis=1)  6.55 us
    unnamed x11, local copies, waits for them, and re-layouts  5.71 us
    all_to_all x1, starting transfers between devices, per_device(): lax.all_to_all(send, 'row', 0, 0, tiled=True).reshape(states, window, leaf)  4.08 us
  transfers between devices with their start and end apart: 2, of which 1 were waited for; matrix products, arithmetic and copies ran while one was open for 12% of the time, Pallas kernels for 0%

profile of v1, /device:TPU:0, one launch (start us, length us, event | category | flops | bytes accessed | tf_op | source)
XLA Modules:
  0.0 132.6 jit_solution(3973920628634587530)
XLA Ops:
  6.5 0.0 copy-start
  6.5 0.9 fusion.17
  7.5 0.8 compare_and_fusion
  8.2 2.6 %copy.16 = bf16[4,8192]{0,1:T(8,128)(2,1)} copy(bf16[4,8192]{1,0:T(4,128)(2,1)} %param.8) | data formatting | bytes 131072 | tf_op args[0]
  10.8 30.0 %gather_fusion = bf16[8192,4]{1,0:T(8,128)(2,1)} fusion(bf16[4,8192]{0,1:T(8,128)(2,1)} %copy.16, s32[8192]{0:T(1024)S(1)} %fusion.17), kind=kCustom, calls=%fused_computation | custom fusion | bytes 163840 | tf_op jit(solution)/shard_map/jit(_take)/gather | solution.py:39
  40.9 6.6 %bitcast_select_fusion = bf16[1,4,8192]{1,2,0:T(8,128)(2,1)} fusion(bf16[8192,4]{1,0:T(8,128)(2,1)} %gather_fusion, pred[8192]{0:T(1024)(128)(4,1)S(1)} %compare_and_fusion), kind=kLoop, calls=%fused_computation.4 | loop fusion | flops 32768 | bytes 139264 | tf_op jit(solution)/shard_map/jit(_take)/select_n | solution.py:39
  47.4 2.0 %copy.17 = bf16[1,4,8192]{2,1,0:T(4,128)(2,1)S(1)} copy(bf16[1,4,8192]{1,2,0:T(8,128)(2,1)} %bitcast_select_fusion) | data formatting | bytes 131072 | tf_op jit(solution)/shard_map/jit(_take)/select_n | solution.py:39
  49.4 15.6 %all_gather.7 = bf16[4,4,8192]{2,1,0:T(4,128)(2,1)S(1)} all-gather(bf16[1,4,8192]{2,1,0:T(4,128)(2,1)S(1)} %copy.17), channel_id=1, replica_groups=mesh['row'=8,'col'=4] {'col'}, dimensions={0}, use_global_device_ids=true | all-gather | bytes 327680 | tf_op jit(solution)/shard_map/all_gather | solution.py:44
  65.1 0.1 slice_bitcast_fusion.1
  65.2 0.2 concatenate.10
  65.4 0.8 all_to_all.6
  66.2 4.1 %all-to-all-start = ((bf16[8,4,4864]{2,1,0:T(4,128)(2,1)}), bf16[8,4,4864]{2,1,0:T(4,128)(2,1)}, u32[]{:S(2)}, u32[]{:S(2)}) async-start(bf16[8,4,4864]{2,1,0:T(4,128)(2,1)} %all_to_all.6), calls=%async_computation | async-start | bytes 622592 | tf_op jit(solution)/shard_map/all_to_all | solution.py:51
  70.3 0.0 reduce-scatter.2.cloned.1.call-start
  70.3 0.0 copy-start.1
  70.3 0.0 copy-start.2
  70.4 6.6 %fusion = bf16[1,4,8192]{1,2,0:T(8,128)(2,1)} fusion(bf16[8192,4]{1,0:T(8,128)(2,1)} %gather_fusion, pred[8192]{0:T(1024)(128)(4,1)S(1)} %compare_and_fusion), kind=kLoop, calls=%fused_computation.6 | loop fusion | flops 32768 | bytes 139264
  76.9 0.0 copy-done.1
  77.0 0.0 copy-done.2
  77.0 0.0 copy-start.3
  77.1 2.0 %copy.19 = bf16[1,4,8192]{2,1,0:T(4,128)(2,1)S(1)} copy(bf16[1,4,8192]{1,2,0:T(8,128)(2,1)} %fusion) | data formatting | bytes 131072
  79.0 10.2 %all-gather = bf16[8,4,8192]{2,1,0:T(4,128)(2,1)S(1)} all-gather(bf16[1,4,8192]{2,1,0:T(4,128)(2,1)S(1)} %copy.19), channel_id=1, replica_groups=mesh['row'=8,'col'=4] {'row'}, dimensions={0}, use_global_device_ids=true | all-gather | bytes 589824 | tf_op jit(solution)/shard_map/all_gather | solution.py:41
  89.2 1.2 reshape.75
  90.4 1.3 %copy.20 = bf16[32,32,256]{2,0,1:T(8,128)(2,1)S(1)} copy(bf16[32,32,256]{2,1,0:T(8,128)(2,1)} %reshape.75) | data formatting | bytes 1048576 | tf_op jit(solution)/shard_map/reshape | solution.py:42
  91.7 0.0 copy-done.3
  91.8 0.6 gather_fusion.2
  92.4 1.4 %fusion.3 = f32[30,32,32]{2,1,0:T(8,128)S(1)} fusion(bf16[30,256,32]{1,2,0:T(8,128)(2,1)} %param.14, bf16[30,32,256]{2,1,0:T(8,128)(2,1)S(1)} %gather_fusion.2, pred[30]{0:T(512)(128)(4,1)S(1)} %get-tuple-element.7), kind=kOutput, calls=%fused_computation.12 | convolution fusion | flops 15974400 | bytes 1105950 | tf_op jit(solution)/shard_map/spk,pkr->psr/dot_general | solution.py:63
  93.8 0.2 reshape.76
  94.0 0.2 convolution_convert_fusion
  94.2 0.1 pad_add_fusion
  94.3 0.1 reshape.77
  94.4 0.6 gather_fusion.3
  95.0 1.4 %fusion.12 = f32[30,32,256]{2,1,0:T(8,128)S(1)} fusion(bf16[30,256,32]{1,2,0:T(8,128)(2,1)} %param.12, bf16[30,32,32]{2,1,0:T(8,128)(2,1)S(1)} %gather_fusion.3, pred[30]{0:T(512)(128)(4,1)S(1)} %and_bitcast_fusion.1), kind=kOutput, calls=%fused_computation.21 | convolution fusion | flops 15759360 | bytes 1536030 | tf_op jit(solution)/shard_map/psr,plr->psl/dot_general | solution.py:77
  96.3 0.0 all-to-all-done
  96.4 1.2 reshape.74
  97.5 0.8 copy.18
  98.3 1.5 %gather_fusion.1 = bf16[16,32,256]{2,1,0:T(8,128)(2,1)S(1)} fusion(bf16[32,19,256]{2,0,1:T(8,128)(2,1)} %copy.18, s32[1024]{0:T(1024)S(1)} %pad_clamp_fusion.2), kind=kCustom, calls=%fused_computation.1 | custom fusion | bytes 524352 | tf_op jit(solution)/shard_map/jit(_take)/gather | solution.py:57
  99.8 0.0 copy-done
  99.8 0.7 fusion.7
  100.6 0.1 pad_maximum_fusion
  100.7 0.1 slice_bitcast_fusion
  100.8 1.5 %fusion.1 = f32[16,32,256]{2,0,1:T(8,128)S(1)} fusion(f32[32,256,46]{1,0,2:T(8,128)S(1)} %slice_bitcast_fusion, s32[46]{0:T(128)S(1)} %pad_add_fusion), kind=kOutput, calls=%fused_computation.7 | convolution fusion | flops 72352480 | bytes 2031800 | tf_op jit(solution)/shard_map/dot_general | solution.py:86
  102.3 1.1 copy.24
  103.4 0.0 reduce-scatter.2.cloned.1.call-update
  103.4 22.4 %reduce-scatter.2.cloned.1.call-done = f32[8,4096]{1,0:T(8,128)} async-done(((f32[32,4096]{1,0:T(8,128)}), f32[8,4096]{1,0:T(8,128)}) %reduce-scatter.2.cloned.1.call-update) | async-done | bytes 131088 | tf_op jit(solution)/shard_map/reduce_scatter | solution.py:92
  (9 shorter events, 0.1 us)
Async XLA Ops:
  6.5 93.3 %copy-start = (bf16[16,256,256]{2,1,0:T(8,128)(2,1)S(1)}, bf16[16,256,256]{2,1,0:T(8,128)(2,1)}, u32[]{:S(2)}) copy-start(bf16[16,256,256]{2,1,0:T(8,128)(2,1)} %param.10) | copy-start | bytes 6291460
  66.2 30.2 %all-to-all-start = ((bf16[8,4,4864]{2,1,0:T(4,128)(2,1)}), bf16[8,4,4864]{2,1,0:T(4,128)(2,1)}, u32[]{:S(2)}, u32[]{:S(2)}) async-start(bf16[8,4,4864]{2,1,0:T(4,128)(2,1)} %all_to_all.6), calls=%async_computation | async-start | bytes 622592 | tf_op jit(solution)/shard_map/all_to_all | solution.py:51
  70.3 55.5 %reduce-scatter.2.cloned.1.call-start = ((), (), s32[]{:S(2)}) async-start(), calls=%async_computation.2 | async-start | bytes 655360 | tf_op jit(solution)/shard_map/reduce_scatter | solution.py:92
  70.3 6.6 %copy-start.1 = (s32[30,2]{0,1:T(2,128)S(1)}, s32[30,2]{0,1:T(2,128)}, u32[]{:S(2)}) copy-start(s32[30,2]{0,1:T(2,128)} %param.13) | copy-start | bytes 724
  70.3 6.6 %copy-start.2 = (s32[16,2]{0,1:T(2,128)S(1)}, s32[16,2]{0,1:T(2,128)}, u32[]{:S(2)}) copy-start(s32[16,2]{0,1:T(2,128)} %param.11) | copy-start | bytes 388
  77.0 14.7 %copy-start.3 = (s32[30,2]{0,1:T(2,128)S(1)}, s32[30,2]{0,1:T(2,128)}, u32[]{:S(2)}) copy-start(s32[30,2]{0,1:T(2,128)} %param.15) | copy-start | bytes 724
Sparse Core Ops, SparseCore 0:
  103.5 22.2 reduce-scatter.1

commit v2 on v1

--- a/solution.py
+++ b/solution.py
@@ -1,10 +1,32 @@
 import jax
 import jax.numpy as jnp
 from jax import lax
+from jax.experimental import pallas as pl
+from jax.experimental.pallas import tpu as pltpu
 from jax.sharding import PartitionSpec as P
 
 BL = 2
 REACH = 3
+UNROLL = 16
+
+
+def _row_gather_kernel(order_ref, rows_ref, out_ref):
+    def body(p, carry):
+        out_ref[pl.ds(p, 1), :] = rows_ref[pl.ds(order_ref[p], 1), :]
+        return carry
+
+    lax.fori_loop(0, out_ref.shape[0], body, 0, unroll=UNROLL)
+
+
+def reorder(values, order):
+    rows = values.astype(jnp.float32).T
+    out = pl.pallas_call(
+        _row_gather_kernel,
+        out_shape=jax.ShapeDtypeStruct(rows.shape, jnp.float32),
+        in_specs=[pl.BlockSpec(memory_space=pltpu.SMEM), pl.BlockSpec(memory_space=pltpu.VMEM)],
+        out_specs=pl.BlockSpec(memory_space=pltpu.VMEM),
+    )(order, rows)
+    return out.T.astype(values.dtype)
 
 
 def per_device(
@@ -27,6 +49,7 @@
     rank = distant_row_factors.shape[2]
     cluster_extent = width // leaf
     row_span = cluster_extent * col_count // row_count
+    rows_per_home = row_count // col_count
     window = 0
     for target in range(row_count):
         base_t = target * row_span - target * col_count // row_count * cluster_extent
@@ -35,24 +58,40 @@
         window = max(window, high_t - low_t)
     block_entries = 4 * BL
 
-    local_order = node_reordering - col_index * width
-    mine = jnp.take(magnetic_potential_input, local_order, axis=1)
+    def window_start(target):
+        home_t = target // rows_per_home
+        return jnp.clip(target * row_span - home_t * cluster_extent - REACH, 0, cluster_extent - window)
 
-    ordered = lax.all_gather(mine, "row", axis=0, tiled=True)
+    mine = reorder(magnetic_potential_input, node_reordering - col_index * width)
+
+    chunks = []
+    for step in range(row_count):
+        slot = (row_index + step) % row_count
+        target_row = col_index * rows_per_home + slot // col_count
+        piece = lax.dynamic_slice_in_dim(mine, window_start(target_row) * leaf, window * leaf, axis=1)
+        pairs = []
+        for i in range(row_count):
+            for h in range(col_count):
+                m = (i + step) % row_count
+                pairs.append((i * col_count + h, (h * rows_per_home + m // col_count) * col_count + m % col_count))
+        chunks.append(lax.ppermute(piece, ("row", "col"), pairs))
+
+    shards = [mine]
+    for step in range(1, row_count):
+        shards.append(lax.ppermute(mine, "row", [(i, (i + step) % row_count) for i in range(row_count)]))
+    stacked = jnp.stack(shards)
+    source_rows = (row_index - jnp.arange(row_count, dtype=jnp.int32)) % row_count
+    ordered = jnp.take(stacked, (row_index - jnp.arange(row_count, dtype=jnp.int32)) % row_count, axis=0)
     leaf_clusters = ordered.reshape(states, cluster_extent, leaf)
 
-    every_block = lax.all_gather(mine, "col", axis=0, tiled=False)
-    pieces = []
-    for target in range(row_count):
-        home_t = target * col_count // row_count
-        start_t = min(max(target * row_span - home_t * cluster_extent - REACH, 0), cluster_extent - window)
-        pieces.append(every_block[home_t, :, start_t * leaf:(start_t + window) * leaf])
-    send = jnp.concatenate(pieces, axis=0)
-    near_window = lax.all_to_all(send, "row", 0, 0, tiled=True).reshape(states, window, leaf)
+    home = row_index // rows_per_home
+    my_slot = (row_index % rows_per_home) * col_count + col_index
+    near_stack = jnp.stack(chunks)
+    near_window = jnp.take(
+        near_stack, (my_slot - jnp.arange(row_count, dtype=jnp.int32)) % row_count, axis=0
+    ).reshape(states, window, leaf)
 
-    home = row_index * col_count // row_count
-    start = jnp.clip(row_index * row_span - home * cluster_extent - REACH, 0, cluster_extent - window)
-    near_cols = adjacent_cluster_pairs[:, 1] - home * cluster_extent - start
+    near_cols = adjacent_cluster_pairs[:, 1] - home * cluster_extent - window_start(row_index)
     near_rows = adjacent_cluster_pairs[:, 0] - row_index * row_span
     near_src = jnp.take(near_window, near_cols, axis=1)
     near_out = jnp.einsum(
@@ -89,7 +128,15 @@
         precision=lax.Precision.HIGHEST,
     ).reshape(row_span, states, leaf)
     partial_sum = partial_sum.transpose(1, 0, 2).reshape(states, row_span * leaf)
-    return lax.psum_scatter(partial_sum, "col", scatter_dimension=0, tiled=True)
+
+    out_states = states // col_count
+    parts = partial_sum.reshape(col_count, out_states, row_span * leaf)
+    total = lax.dynamic_index_in_dim(parts, col_index, axis=0, keepdims=False)
+    for step in range(1, col_count):
+        dest = (col_index + step) % col_count
+        piece = lax.dynamic_index_in_dim(parts, dest, axis=0, keepdims=False)
+        total = total + lax.ppermute(piece, "col", [(j, (j + step) % col_count) for j in range(col_count)])
+    return total
 
 
 def solution(mesh):

time: 133 us -> 182 us (1.37)
  starting transfers between devices: 4.12 us -> 44.7 us
  blocking collectives: 25.8 us -> 0 us
  local copies, waits for them, and re-layouts: 46.4 us -> 71.4 us
  between operations: 13.7 us -> 0.43 us
  Pallas kernels: 0 us -> 13.1 us
  waiting for transfers between devices: 22.4 us -> 35.4 us
  other arithmetic: 15.1 us -> 12.5 us
  matrix products: 5.1 us -> 3.03 us
    ppermute x0 -> x18, starting transfers between devices: none -> 44.7 us  [the longest x8 28.7 us: per_device(): chunks.append(lax.ppermute(piece, ('row', 'col'), pairs))]
    ppermute x0 -> x18, waiting for transfers between devices: none -> 35.4 us  [the longest x8 26.3 us: per_device(): chunks.append(lax.ppermute(piece, ('row', 'col'), pairs))]
    gather x1 -> x4, local copies, waits for them, and re-layouts: 30 us -> 2.48 us  [the longest x2 1.36 us: per_device(): jnp.take(stacked, (row_index - jnp.arange(row_count, dtype=jnp.int32)) %...]
    dynamic_slice x0 -> x9, local copies, waits for them, and re-layouts: none -> 26 us  [per_device(): lax.dynamic_slice_in_dim(mine, window_start(target_row) * leaf, window *...]
    all_gather x2 -> x0, blocking collectives: 25.8 us -> none  [the longest x1 15.6 us: per_device(): every_block = lax.all_gather(mine, 'col', axis=0, tiled=False)]
    reduce_scatter x1 -> x0, waiting for transfers between devices: 22.4 us -> none  [per_device(): return lax.psum_scatter(partial_sum, 'col', scatter_dimension=0, tiled=True)]
    another operation x0 -> x4, local copies, waits for them, and re-layouts: none -> 13.9 us  [the longest x2 13.8 us: per_device(): stacked = jnp.stack(shards)]
    pallas_call x0 -> x1, Pallas kernels: none -> 13.1 us  [reorder(): pl.pallas_call(_row_gather_kernel, out_shape=jax.ShapeDtypeStruct(rows.sh...]
  transfers between devices with their start and end apart: 2 -> 18, of which waited for: 1 -> 9; matrix products, arithmetic and copies ran while one was open for 12% -> 30% of each run, Pallas kernels for 0% -> 0%
where the time goes in v2:
time: 182 us; the launch traced here: 181 us
  local copies, waits for them, and re-layouts  71.4 us (39%)
  starting transfers between devices  44.7 us (25%)
  waiting for transfers between devices  35.4 us (19%)
  Pallas kernels  13.1 us (7%)
  other arithmetic  12.5 us (7%)
  matrix products  3.03 us (2%)
    ppermute x8, starting transfers between devices, per_device(): chunks.append(lax.ppermute(piece, ('row', 'col'), pairs))  28.7 us
    ppermute x8, waiting for transfers between devices, per_device(): chunks.append(lax.ppermute(piece, ('row', 'col'), pairs))  26.3 us
    dynamic_slice x9, local copies, waits for them, and re-layouts, per_device(): lax.dynamic_slice_in_dim(mine, window_start(target_row) * leaf, window *...  26 us
    another operation x2, local copies, waits for them, and re-layouts, per_device(): stacked = jnp.stack(shards)  13.8 us
    pallas_call x1, Pallas kernels, reorder(): pl.pallas_call(_row_gather_kernel, out_shape=jax.ShapeDtypeStruct(rows.sh...  13.1 us
    ppermute x7, starting transfers between devices, per_device(): lax.ppermute(mine, 'row', [(i, (i + step) % row_count) for i in range(row...  12.1 us
    unnamed x39, local copies, waits for them, and re-layouts  10.5 us
    ppermute x3, waiting for transfers between devices, per_device(): lax.ppermute(piece, 'col', [(j, (j + step) % col_count) for j in range(co...  9.11 us
  transfers between devices with their start and end apart: 18, of which 9 were waited for; matrix products, arithmetic and copies ran while one was open for 30% of the time, Pallas kernels for 0%

profile of v2, /device:TPU:0, one launch (start us, length us, event | category | flops | bytes accessed | tf_op | source)
XLA Modules:
  0.0 180.5 jit_solution(16795502709752055287)
XLA Ops:
  0.0 3.3 %copy.90 = f32[4,8192]{0,1:T(8,128)} copy(bf16[4,8192]{1,0:T(4,128)(2,1)} %param.8) | data formatting | bytes 196608 | tf_op jit(solution)/shard_map/transpose | solution.py:22
  3.9 13.1 %shard_map.82 = f32[8192,4]{1,0:T(8,128)} custom-call(s32[8192]{0:T(1024)} %broadcast_subtract_fusion.order_ref, f32[8192,4]{1,0:T(8,128)} %bitcast.111), custom_call_target="tpu_custom_call" | custom-call | tf_op jit(solution)/shard_map/pallas_call | solution.py:23
  17.0 4.7 %bitcast_dynamic-update-slice_fusion = (bf16[8,4,8192]{1,2,0:T(8,128)(2,1)}, bf16[8192,4]{1,0:T(8,128)(2,1)}) fusion(f32[8192,4]{1,0:T(8,128)} %shard_map.82), kind=kLoop, calls=%fused_computation.5 | loop fusion | flops 32767 | bytes 4325376
  21.7 2.0 %copy.100 = bf16[4,8192]{1,0:T(4,128)(2,1)S(1)} copy(bf16[4,8192]{0,1:T(8,128)(2,1)} %bitcast.110) | data formatting | bytes 131072 | tf_op jit(solution)/shard_map/convert_element_type | solution.py:29
  24.2 2.6 %collective-permute-start.9 = (bf16[4,8192]{1,0:T(4,128)(2,1)S(1)}, bf16[4,8192]{1,0:T(4,128)(2,1)}, u32[]{:S(2)}, u32[]{:S(2)}) collective-permute-start(bf16[4,8192]{1,0:T(4,128)(2,1)S(1)} %copy.100), channel_id=1, source_target_pairs={{0,8},{4,12},{8,16},{12,20},{16,24},{20,28},{24,0},{28,4},{1,9},{5... | collective-permute-start | bytes 196616 | tf_op jit(solution)/shard_map/ppermute | solution.py:81
  26.8 2.4 %collective-permute-start.10 = (bf16[4,8192]{1,0:T(4,128)(2,1)S(1)}, bf16[4,8192]{1,0:T(4,128)(2,1)S(1)}, u32[]{:S(2)}, u32[]{:S(2)}) collective-permute-start(bf16[4,8192]{1,0:T(4,128)(2,1)S(1)} %copy.100), channel_id=1, source_target_pairs={{0,12},{4,16},{8,20},{12,24},{16,28},{20,0},{24,4},{28,8},{1,13},{... | collective-permute-start | bytes 196616 | tf_op jit(solution)/shard_map/ppermute | solution.py:81
  29.6 8.4 %dynamic-slice_bitcast_fusion = (bf16[4,4864]{0,1:T(8,128)(2,1)S(1)}, bf16[4,4864]{0,1:T(8,128)(2,1)}, bf16[4,4864]{0,1:T(8,128)(2,1)}, bf16[4,4864]{0,1:T(8,128...) fusion(bf16[8192,4]{1,0:T(8,128)(2,1)} %get-tuple-element.10, ...), kind=kLoop, calls=%fused_computation.17 | loop fusion | bytes 622624 | tf_op jit(solution)/shard_map/dynamic_slice | solution.py:71
  38.0 2.4 %copy.91 = bf16[4,4864]{1,0:T(4,128)(2,1)} copy(bf16[4,4864]{0,1:T(8,128)(2,1)} %get-tuple-element.18) | data formatting | bytes 77824 | tf_op jit(solution)/shard_map/dynamic_slice | solution.py:71
  40.4 2.0 %collective-permute-start = (bf16[4,4864]{1,0:T(4,128)(2,1)}, bf16[4,4864]{1,0:T(4,128)(2,1)}, u32[]{:S(2)}, u32[]{:S(2)}) collective-permute-start(bf16[4,4864]{1,0:T(4,128)(2,1)} %copy.91), channel_id=1, source_target_pairs={{0,0},{1,8},{2,16},{3,24},{4,1},{5,9},{6,17},{7,25},{8,2},{9,10},{... | collective-permute-start | bytes 116744 | tf_op jit(solution)/shard_map/ppermute | solution.py:77
  47.7 1.2 pad_add_fusion
  48.9 2.4 %copy.92 = bf16[4,4864]{1,0:T(4,128)(2,1)} copy(bf16[4,4864]{0,1:T(8,128)(2,1)} %get-tuple-element.17) | data formatting | bytes 77824 | tf_op jit(solution)/shard_map/dynamic_slice | solution.py:71
  51.3 2.4 %copy.93 = bf16[4,4864]{1,0:T(4,128)(2,1)} copy(bf16[4,4864]{0,1:T(8,128)(2,1)} %get-tuple-element.16) | data formatting | bytes 77824 | tf_op jit(solution)/shard_map/dynamic_slice | solution.py:71
  53.7 2.4 %copy.94 = bf16[4,4864]{1,0:T(4,128)(2,1)} copy(bf16[4,4864]{0,1:T(8,128)(2,1)} %get-tuple-element.15) | data formatting | bytes 77824 | tf_op jit(solution)/shard_map/dynamic_slice | solution.py:71
  56.0 2.4 %copy.95 = bf16[4,4864]{1,0:T(4,128)(2,1)} copy(bf16[4,4864]{0,1:T(8,128)(2,1)} %get-tuple-element.14) | data formatting | bytes 77824 | tf_op jit(solution)/shard_map/dynamic_slice | solution.py:71
  58.4 2.4 %copy.96 = bf16[4,4864]{1,0:T(4,128)(2,1)} copy(bf16[4,4864]{0,1:T(8,128)(2,1)} %get-tuple-element.13) | data formatting | bytes 77824 | tf_op jit(solution)/shard_map/dynamic_slice | solution.py:71
  60.7 2.4 %copy.97 = bf16[4,4864]{1,0:T(4,128)(2,1)} copy(bf16[4,4864]{0,1:T(8,128)(2,1)} %get-tuple-element.12) | data formatting | bytes 77824 | tf_op jit(solution)/shard_map/dynamic_slice | solution.py:71
  63.1 1.1 copy.98
  65.8 4.7 %collective-permute-start.1 = (bf16[4,4864]{1,0:T(4,128)(2,1)}, bf16[4,4864]{1,0:T(4,128)(2,1)S(1)}, u32[]{:S(2)}, u32[]{:S(2)}) collective-permute-start(bf16[4,4864]{1,0:T(4,128)(2,1)} %copy.92), channel_id=1, source_target_pairs={{0,1},{1,9},{2,17},{3,25},{4,2},{5,10},{6,18},{7,26},{8,3},{9,11},... | collective-permute-start | bytes 116744 | tf_op jit(solution)/shard_map/ppermute | solution.py:77
  71.3 2.9 %collective-permute-done.1 = bf16[4,4864]{1,0:T(4,128)(2,1)S(1)} collective-permute-done((bf16[4,4864]{1,0:T(4,128)(2,1)}, bf16[4,4864]{1,0:T(4,128)(2,1)S(1)}, u32[]{:S(2)}, u32[]{:S(2)}) %collective-permute-start.1) | collective-permute-done | bytes 38944 | tf_op jit(solution)/shard_map/ppermute | solution.py:77
  74.1 3.7 %collective-permute-start.2 = (bf16[4,4864]{1,0:T(4,128)(2,1)}, bf16[4,4864]{1,0:T(4,128)(2,1)S(1)}, u32[]{:S(2)}, u32[]{:S(2)}) collective-permute-start(bf16[4,4864]{1,0:T(4,128)(2,1)} %copy.93), channel_id=1, source_target_pairs={{0,2},{1,10},{2,18},{3,26},{4,3},{5,11},{6,19},{7,27},{8,4},{9,12}... | collective-permute-start | bytes 116744 | tf_op jit(solution)/shard_map/ppermute | solution.py:77
  77.9 3.2 %collective-permute-done.2 = bf16[4,4864]{1,0:T(4,128)(2,1)S(1)} collective-permute-done((bf16[4,4864]{1,0:T(4,128)(2,1)}, bf16[4,4864]{1,0:T(4,128)(2,1)S(1)}, u32[]{:S(2)}, u32[]{:S(2)}) %collective-permute-start.2) | collective-permute-done | bytes 38944 | tf_op jit(solution)/shard_map/ppermute | solution.py:77
  81.1 7.0 %collective-permute-start.3 = (bf16[4,4864]{1,0:T(4,128)(2,1)}, bf16[4,4864]{1,0:T(4,128)(2,1)S(1)}, u32[]{:S(2)}, u32[]{:S(2)}) collective-permute-start(bf16[4,4864]{1,0:T(4,128)(2,1)} %copy.94), channel_id=1, source_target_pairs={{0,3},{1,11},{2,19},{3,27},{4,4},{5,12},{6,20},{7,28},{8,5},{9,13}... | collective-permute-start | bytes 116744 | tf_op jit(solution)/shard_map/ppermute | solution.py:77
  88.1 1.9 %collective-permute-done.3 = bf16[4,4864]{1,0:T(4,128)(2,1)S(1)} collective-permute-done((bf16[4,4864]{1,0:T(4,128)(2,1)}, bf16[4,4864]{1,0:T(4,128)(2,1)S(1)}, u32[]{:S(2)}, u32[]{:S(2)}) %collective-permute-start.3) | collective-permute-done | bytes 38944 | tf_op jit(solution)/shard_map/ppermute | solution.py:77
  90.1 4.3 %collective-permute-done.4 = bf16[4,4864]{1,0:T(4,128)(2,1)S(1)} collective-permute-done((bf16[4,4864]{1,0:T(4,128)(2,1)}, bf16[4,4864]{1,0:T(4,128)(2,1)S(1)}, u32[]{:S(2)}, u32[]{:S(2)}) %collective-permute-start.4) | collective-permute-done | bytes 38944 | tf_op jit(solution)/shard_map/ppermute | solution.py:77
  94.3 1.9 %collective-permute-start.5 = (bf16[4,4864]{1,0:T(4,128)(2,1)}, bf16[4,4864]{1,0:T(4,128)(2,1)S(1)}, u32[]{:S(2)}, u32[]{:S(2)}) collective-permute-start(bf16[4,4864]{1,0:T(4,128)(2,1)} %copy.96), channel_id=1, source_target_pairs={{0,5},{1,13},{2,21},{3,29},{4,6},{5,14},{6,22},{7,30},{8,7},{9,15}... | collective-permute-start | bytes 116744 | tf_op jit(solution)/shard_map/ppermute | solution.py:77
  96.3 5.1 %collective-permute-done.5 = bf16[4,4864]{1,0:T(4,128)(2,1)S(1)} collective-permute-done((bf16[4,4864]{1,0:T(4,128)(2,1)}, bf16[4,4864]{1,0:T(4,128)(2,1)S(1)}, u32[]{:S(2)}, u32[]{:S(2)}) %collective-permute-start.5) | collective-permute-done | bytes 38944 | tf_op jit(solution)/shard_map/ppermute | solution.py:77
  101.4 1.9 %collective-permute-start.6 = (bf16[4,4864]{1,0:T(4,128)(2,1)}, bf16[4,4864]{1,0:T(4,128)(2,1)S(1)}, u32[]{:S(2)}, u32[]{:S(2)}) collective-permute-start(bf16[4,4864]{1,0:T(4,128)(2,1)} %copy.97), channel_id=1, source_target_pairs={{0,6},{1,14},{2,22},{3,30},{4,7},{5,15},{6,23},{7,31},{8,0},{9,8},... | collective-permute-start | bytes 116744 | tf_op jit(solution)/shard_map/ppermute | solution.py:77
  103.4 7.0 %collective-permute-done.6 = bf16[4,4864]{1,0:T(4,128)(2,1)S(1)} collective-permute-done((bf16[4,4864]{1,0:T(4,128)(2,1)}, bf16[4,4864]{1,0:T(4,128)(2,1)S(1)}, u32[]{:S(2)}, u32[]{:S(2)}) %collective-permute-start.6) | collective-permute-done | bytes 38944 | tf_op jit(solution)/shard_map/ppermute | solution.py:77
  110.4 7.4 %collective-permute-start.7 = (bf16[4,4864]{1,0:T(4,128)(2,1)}, bf16[4,4864]{1,0:T(4,128)(2,1)S(1)}, u32[]{:S(2)}, u32[]{:S(2)}) collective-permute-start(bf16[4,4864]{1,0:T(4,128)(2,1)} %copy.98), channel_id=1, source_target_pairs={{0,7},{1,15},{2,23},{3,31},{4,0},{5,8},{6,16},{7,24},{8,1},{9,9},{... | collective-permute-start | bytes 116744 | tf_op jit(solution)/shard_map/ppermute | solution.py:77
  117.8 1.9 %collective-permute-done.7 = bf16[4,4864]{1,0:T(4,128)(2,1)S(1)} collective-permute-done((bf16[4,4864]{1,0:T(4,128)(2,1)}, bf16[4,4864]{1,0:T(4,128)(2,1)S(1)}, u32[]{:S(2)}, u32[]{:S(2)}) %collective-permute-start.7) | collective-permute-done | bytes 38944 | tf_op jit(solution)/shard_map/ppermute | solution.py:77
  119.8 1.5 collective-permute-start.12
  123.8 4.7 %collective-permute-start.13 = (bf16[4,8192]{1,0:T(4,128)(2,1)S(1)}, bf16[4,8192]{1,0:T(4,128)(2,1)S(1)}, u32[]{:S(2)}, u32[]{:S(2)}) collective-permute-start(bf16[4,8192]{1,0:T(4,128)(2,1)S(1)} %copy.100), channel_id=1, source_target_pairs={{0,24},{4,28},{8,0},{12,4},{16,8},{20,12},{24,16},{28,20},{1,25},{... | collective-permute-start | bytes 196616 | tf_op jit(solution)/shard_map/ppermute | solution.py:81
  128.6 1.8 copy.101
  130.4 1.5 bitcast_dynamic-update-slice_fusion.7
  131.8 1.8 copy.103
  133.6 1.5 bitcast_dynamic-update-slice_fusion.6
  135.2 1.0 copy.105
  136.2 1.5 bitcast_dynamic-update-slice_fusion.5
  138.8 1.5 bitcast_dynamic-update-slice_fusion.4
  141.4 1.5 bitcast_dynamic-update-slice_fusion.3
  144.0 1.4 bitcast_dynamic-update-slice_fusion.2
  146.5 1.4 bitcast_dynamic-update-slice_fusion.1
  147.9 12.4 %copy.114 = bf16[8,4,8192]{2,1,0:T(4,128)(2,1)S(1)} copy(bf16[8,4,8192]{1,2,0:T(8,128)(2,1)} %bitcast_dynamic-update-slice_fusion.1) | data formatting | bytes 1048576 | tf_op jit(solution)/shard_map/stack | solution.py:82
  165.2 1.5 fusion.2
  166.9 2.6 %collective-permute-start.16 = (f32[8,4096]{1,0:T(8,128)S(1)}, f32[8,4096]{1,0:T(8,128)S(1)}, u32[]{:S(2)}, u32[]{:S(2)}) collective-permute-start(f32[8,4096]{1,0:T(8,128)S(1)} %get-tuple-element.21), channel_id=1, source_target_pairs={{0,2},{1,3},{2,0},{3,1},{4,6},{5,7},{6,4},{7,5},{8,10},{9,11},{10,... | collective-permute-start | bytes 393224 | tf_op jit(solution)/shard_map/ppermute | solution.py:138
  169.5 1.3 collective-permute-start.17
  170.7 4.4 %collective-permute-done.15 = f32[8,4096]{1,0:T(8,128)S(1)} collective-permute-done((f32[8,4096]{1,0:T(8,128)S(1)}, f32[8,4096]{1,0:T(8,128)S(1)}, u32[]{:S(2)}, u32[]{:S(2)}) %collective-permute-start.15) | collective-permute-done | bytes 131104 | tf_op jit(solution)/shard_map/ppermute | solution.py:138
  175.1 4.7 %collective-permute-done.16 = f32[8,4096]{1,0:T(8,128)S(1)} collective-permute-done((f32[8,4096]{1,0:T(8,128)S(1)}, f32[8,4096]{1,0:T(8,128)S(1)}, u32[]{:S(2)}, u32[]{:S(2)}) %collective-permute-start.16) | collective-permute-done | bytes 131104 | tf_op jit(solution)/shard_map/ppermute | solution.py:138
  (89 shorter events, 21.9 us)
Async XLA Ops:
  0.0 123.1 %copy-start = (bf16[16,256,256]{2,1,0:T(8,128)(2,1)S(1)}, bf16[16,256,256]{2,1,0:T(8,128)(2,1)}, u32[]{:S(2)}) copy-start(bf16[16,256,256]{2,1,0:T(8,128)(2,1)} %param.10) | copy-start | bytes 6291460
  0.0 3.3 %copy-start.4 = (s32[8192]{0:T(1024)S(1)}, s32[8192]{0:T(1024)}, u32[]{:S(2)}) copy-start(s32[8192]{0:T(1024)} %param.9) | copy-start | bytes 98308
  23.7 100.1 %collective-permute-start.8 = (bf16[4,8192]{1,0:T(4,128)(2,1)S(1)}, bf16[4,8192]{1,0:T(4,128)(2,1)}, u32[]{:S(2)}, u32[]{:S(2)}) collective-permute-start(bf16[4,8192]{1,0:T(4,128)(2,1)S(1)} %copy.100), channel_id=1, source_target_pairs={{0,4},{4,8},{8,12},{12,16},{16,20},{20,24},{24,28},{28,0},{1,5},{5... | collective-permute-start | bytes 196616 | tf_op jit(solution)/shard_map/ppermute | solution.py:81
  24.2 107.6 %collective-permute-start.9 = (bf16[4,8192]{1,0:T(4,128)(2,1)S(1)}, bf16[4,8192]{1,0:T(4,128)(2,1)}, u32[]{:S(2)}, u32[]{:S(2)}) collective-permute-start(bf16[4,8192]{1,0:T(4,128)(2,1)S(1)} %copy.100), channel_id=1, source_target_pairs={{0,8},{4,12},{8,16},{12,20},{16,24},{20,28},{24,0},{28,4},{1,9},{5... | collective-permute-start | bytes 196616 | tf_op jit(solution)/shard_map/ppermute | solution.py:81
  26.8 108.4 %collective-permute-start.10 = (bf16[4,8192]{1,0:T(4,128)(2,1)S(1)}, bf16[4,8192]{1,0:T(4,128)(2,1)S(1)}, u32[]{:S(2)}, u32[]{:S(2)}) collective-permute-start(bf16[4,8192]{1,0:T(4,128)(2,1)S(1)} %copy.100), channel_id=1, source_target_pairs={{0,12},{4,16},{8,20},{12,24},{16,28},{20,0},{24,4},{28,8},{1,13},{... | collective-permute-start | bytes 196616 | tf_op jit(solution)/shard_map/ppermute | solution.py:81
  29.1 108.6 %collective-permute-start.11 = (bf16[4,8192]{1,0:T(4,128)(2,1)S(1)}, bf16[4,8192]{1,0:T(4,128)(2,1)S(1)}, u32[]{:S(2)}, u32[]{:S(2)}) collective-permute-start(bf16[4,8192]{1,0:T(4,128)(2,1)S(1)} %copy.100), channel_id=1, source_target_pairs={{0,16},{4,20},{8,24},{12,28},{16,0},{20,4},{24,8},{28,12},{1,17},{... | collective-permute-start | bytes 196616 | tf_op jit(solution)/shard_map/ppermute | solution.py:81
  29.6 14.5 %copy-start.7 = (s32[30,2]{0,1:T(2,128)S(1)}, s32[30,2]{0,1:T(2,128)}, u32[]{:S(2)}) copy-start(s32[30,2]{0,1:T(2,128)} %param.13) | copy-start | bytes 724
  29.6 15.7 %copy-start.11 = (s32[16,2]{0,1:T(2,128)S(1)}, s32[16,2]{0,1:T(2,128)}, u32[]{:S(2)}) copy-start(s32[16,2]{0,1:T(2,128)} %param.11) | copy-start | bytes 388
  29.6 16.2 %copy-start.12 = (s32[30,2]{0,1:T(2,128)S(1)}, s32[30,2]{0,1:T(2,128)}, u32[]{:S(2)}) copy-start(s32[30,2]{0,1:T(2,128)} %param.15) | copy-start | bytes 724
  40.4 25.4 %collective-permute-start = (bf16[4,4864]{1,0:T(4,128)(2,1)}, bf16[4,4864]{1,0:T(4,128)(2,1)}, u32[]{:S(2)}, u32[]{:S(2)}) collective-permute-start(bf16[4,4864]{1,0:T(4,128)(2,1)} %copy.91), channel_id=1, source_target_pairs={{0,0},{1,8},{2,16},{3,24},{4,1},{5,9},{6,17},{7,25},{8,2},{9,10},{... | collective-permute-start | bytes 116744 | tf_op jit(solution)/shard_map/ppermute | solution.py:77
  64.2 58.9 %copy-start.5 = (pred[16]{0:T(512)(128)(4,1)S(1)}, pred[16]{0:T(512)(128)(4,1)}, u32[]{:S(2)}) copy-start(pred[16]{0:T(512)(128)(4,1)} %get-tuple-element.5) | copy-start | bytes 52
  65.8 8.4 %collective-permute-start.1 = (bf16[4,4864]{1,0:T(4,128)(2,1)}, bf16[4,4864]{1,0:T(4,128)(2,1)S(1)}, u32[]{:S(2)}, u32[]{:S(2)}) collective-permute-start(bf16[4,4864]{1,0:T(4,128)(2,1)} %copy.92), channel_id=1, source_target_pairs={{0,1},{1,9},{2,17},{3,25},{4,2},{5,10},{6,18},{7,26},{8,3},{9,11},... | collective-permute-start | bytes 116744 | tf_op jit(solution)/shard_map/ppermute | solution.py:77
  74.1 7.0 %collective-permute-start.2 = (bf16[4,4864]{1,0:T(4,128)(2,1)}, bf16[4,4864]{1,0:T(4,128)(2,1)S(1)}, u32[]{:S(2)}, u32[]{:S(2)}) collective-permute-start(bf16[4,4864]{1,0:T(4,128)(2,1)} %copy.93), channel_id=1, source_target_pairs={{0,2},{1,10},{2,18},{3,26},{4,3},{5,11},{6,19},{7,27},{8,4},{9,12}... | collective-permute-start | bytes 116744 | tf_op jit(solution)/shard_map/ppermute | solution.py:77
  81.1 8.9 %collective-permute-start.3 = (bf16[4,4864]{1,0:T(4,128)(2,1)}, bf16[4,4864]{1,0:T(4,128)(2,1)S(1)}, u32[]{:S(2)}, u32[]{:S(2)}) collective-permute-start(bf16[4,4864]{1,0:T(4,128)(2,1)} %copy.94), channel_id=1, source_target_pairs={{0,3},{1,11},{2,19},{3,27},{4,4},{5,12},{6,20},{7,28},{8,5},{9,13}... | collective-permute-start | bytes 116744 | tf_op jit(solution)/shard_map/ppermute | solution.py:77
  90.0 4.3 %collective-permute-start.4 = (bf16[4,4864]{1,0:T(4,128)(2,1)}, bf16[4,4864]{1,0:T(4,128)(2,1)S(1)}, u32[]{:S(2)}, u32[]{:S(2)}) collective-permute-start(bf16[4,4864]{1,0:T(4,128)(2,1)} %copy.95), channel_id=1, source_target_pairs={{0,4},{1,12},{2,20},{3,28},{4,5},{5,13},{6,21},{7,29},{8,6},{9,14}... | collective-permute-start | bytes 116744 | tf_op jit(solution)/shard_map/ppermute | solution.py:77
  94.3 7.1 %collective-permute-start.5 = (bf16[4,4864]{1,0:T(4,128)(2,1)}, bf16[4,4864]{1,0:T(4,128)(2,1)S(1)}, u32[]{:S(2)}, u32[]{:S(2)}) collective-permute-start(bf16[4,4864]{1,0:T(4,128)(2,1)} %copy.96), channel_id=1, source_target_pairs={{0,5},{1,13},{2,21},{3,29},{4,6},{5,14},{6,22},{7,30},{8,7},{9,15}... | collective-permute-start | bytes 116744 | tf_op jit(solution)/shard_map/ppermute | solution.py:77
  101.4 9.0 %collective-permute-start.6 = (bf16[4,4864]{1,0:T(4,128)(2,1)}, bf16[4,4864]{1,0:T(4,128)(2,1)S(1)}, u32[]{:S(2)}, u32[]{:S(2)}) collective-permute-start(bf16[4,4864]{1,0:T(4,128)(2,1)} %copy.97), channel_id=1, source_target_pairs={{0,6},{1,14},{2,22},{3,30},{4,7},{5,15},{6,23},{7,31},{8,0},{9,8},... | collective-permute-start | bytes 116744 | tf_op jit(solution)/shard_map/ppermute | solution.py:77
  110.4 9.4 %collective-permute-start.7 = (bf16[4,4864]{1,0:T(4,128)(2,1)}, bf16[4,4864]{1,0:T(4,128)(2,1)S(1)}, u32[]{:S(2)}, u32[]{:S(2)}) collective-permute-start(bf16[4,4864]{1,0:T(4,128)(2,1)} %copy.98), channel_id=1, source_target_pairs={{0,7},{1,15},{2,23},{3,31},{4,0},{5,8},{6,16},{7,24},{8,1},{9,9},{... | collective-permute-start | bytes 116744 | tf_op jit(solution)/shard_map/ppermute | solution.py:77
  119.8 20.6 %collective-permute-start.12 = (bf16[4,8192]{1,0:T(4,128)(2,1)S(1)}, bf16[4,8192]{1,0:T(4,128)(2,1)S(1)}, u32[]{:S(2)}, u32[]{:S(2)}) collective-permute-start(bf16[4,8192]{1,0:T(4,128)(2,1)S(1)} %copy.100), channel_id=1, source_target_pairs={{0,20},{4,24},{8,28},{12,0},{16,4},{20,8},{24,12},{28,16},{1,21},{... | collective-permute-start | bytes 196616 | tf_op jit(solution)/shard_map/ppermute | solution.py:81
  123.8 19.1 %collective-permute-start.13 = (bf16[4,8192]{1,0:T(4,128)(2,1)S(1)}, bf16[4,8192]{1,0:T(4,128)(2,1)S(1)}, u32[]{:S(2)}, u32[]{:S(2)}) collective-permute-start(bf16[4,8192]{1,0:T(4,128)(2,1)S(1)} %copy.100), channel_id=1, source_target_pairs={{0,24},{4,28},{8,0},{12,4},{16,8},{20,12},{24,16},{28,20},{1,25},{... | collective-permute-start | bytes 196616 | tf_op jit(solution)/shard_map/ppermute | solution.py:81
  131.8 13.6 %collective-permute-start.14 = (bf16[4,8192]{1,0:T(4,128)(2,1)S(1)}, bf16[4,8192]{1,0:T(4,128)(2,1)S(1)}, u32[]{:S(2)}, u32[]{:S(2)}) collective-permute-start(bf16[4,8192]{1,0:T(4,128)(2,1)S(1)} %copy.100), channel_id=1, source_target_pairs={{0,28},{4,0},{8,4},{12,8},{16,12},{20,16},{24,20},{28,24},{1,29},{... | collective-permute-start | bytes 196616 | tf_op jit(solution)/shard_map/ppermute | solution.py:81
  160.3 2.3 %copy-start.3 = (bf16[30,256,32]{1,2,0:T(8,128)(2,1)S(1)}, bf16[30,256,32]{1,2,0:T(8,128)(2,1)}, u32[]{:S(2)}) copy-start(bf16[30,256,32]{1,2,0:T(8,128)(2,1)} %param.14) | copy-start | bytes 1474564
  160.3 2.3 %copy-start.6 = (pred[30]{0:T(512)(128)(4,1)S(1)}, pred[30]{0:T(512)(128)(4,1)}, u32[]{:S(2)}) copy-start(pred[30]{0:T(512)(128)(4,1)} %get-tuple-element.7) | copy-start | bytes 94
  161.7 1.6 copy-start.10
  162.0 2.1 %copy-start.2 = (bf16[30,256,32]{1,2,0:T(8,128)(2,1)S(1)}, bf16[30,256,32]{1,2,0:T(8,128)(2,1)}, u32[]{:S(2)}) copy-start(bf16[30,256,32]{1,2,0:T(8,128)(2,1)} %param.12) | copy-start | bytes 1474564
  162.0 2.1 %copy-start.8 = (pred[30]{0:T(512)(128)(4,1)S(1)}, pred[30]{0:T(512)(128)(4,1)}, u32[]{:S(2)}) copy-start(pred[30]{0:T(512)(128)(4,1)} %and_bitcast_fusion.1) | copy-start | bytes 94
  164.6 0.6 copy-start.9
  164.6 15.9 %copy-start.1 = (bf16[16,256,256]{2,1,0:T(8,128)(2,1)S(1)}, bf16[16,256,256]{2,1,0:T(8,128)(2,1)}, u32[]{:S(2)}) copy-start(bf16[16,256,256]{2,1,0:T(8,128)(2,1)} %param.10) | copy-start | bytes 6291460
  166.8 8.3 %collective-permute-start.15 = (f32[8,4096]{1,0:T(8,128)S(1)}, f32[8,4096]{1,0:T(8,128)S(1)}, u32[]{:S(2)}, u32[]{:S(2)}) collective-permute-start(f32[8,4096]{1,0:T(8,128)S(1)} %get-tuple-element.19), channel_id=1, source_target_pairs={{0,1},{1,2},{2,3},{3,0},{4,5},{5,6},{6,7},{7,4},{8,9},{9,10},{10,1... | collective-permute-start | bytes 393224 | tf_op jit(solution)/shard_map/ppermute | solution.py:138
  166.9 12.9 %collective-permute-start.16 = (f32[8,4096]{1,0:T(8,128)S(1)}, f32[8,4096]{1,0:T(8,128)S(1)}, u32[]{:S(2)}, u32[]{:S(2)}) collective-permute-start(f32[8,4096]{1,0:T(8,128)S(1)} %get-tuple-element.21), channel_id=1, source_target_pairs={{0,2},{1,3},{2,0},{3,1},{4,6},{5,7},{6,4},{7,5},{8,10},{9,11},{10,... | collective-permute-start | bytes 393224 | tf_op jit(solution)/shard_map/ppermute | solution.py:138
  169.5 10.4 %collective-permute-start.17 = (f32[8,4096]{1,0:T(8,128)S(1)}, f32[8,4096]{1,0:T(8,128)S(1)}, u32[]{:S(2)}, u32[]{:S(2)}) collective-permute-start(f32[8,4096]{1,0:T(8,128)S(1)} %get-tuple-element.20), channel_id=1, source_target_pairs={{0,3},{1,0},{2,1},{3,2},{4,7},{5,4},{6,5},{7,6},{8,11},{9,8},{10,9... | collective-permute-start | bytes 393224 | tf_op jit(solution)/shard_map/ppermute | solution.py:138

commit v3 on v1

--- a/solution.py
+++ b/solution.py
@@ -1,10 +1,58 @@
 import jax
 import jax.numpy as jnp
 from jax import lax
+from jax.experimental import pallas as pl
 from jax.sharding import PartitionSpec as P
 
 BL = 2
 REACH = 3
+LANES = 128
+SUBLANES = 8
+BATCH = 16
+
+
+def _lane_gather_kernel(values_ref, low_ref, high_ref, out_ref):
+    tiles = values_ref.shape[1] // LANES
+    batch = min(BATCH, out_ref.shape[0])
+
+    def group_body(k, carry):
+        base = k * batch
+        lows = [low_ref[base + b] for b in range(batch)]
+        highs = [high_ref[base + b] for b in range(batch)]
+
+        def tile_body(v, accs):
+            src = values_ref[:, pl.ds(pl.multiple_of(v * LANES, LANES), LANES)]
+            return tuple(
+                jnp.where(
+                    highs[b] == v,
+                    jnp.take_along_axis(src, lows[b], axis=1, mode="promise_in_bounds"),
+                    accs[b],
+                )
+                for b in range(batch)
+            )
+
+        zeros = tuple(jnp.zeros((SUBLANES, LANES), jnp.float32) for _ in range(batch))
+        accs = lax.fori_loop(0, tiles, tile_body, zeros)
+        for b in range(batch):
+            out_ref[base + b] = accs[b]
+        return carry
+
+    lax.fori_loop(0, out_ref.shape[0] // batch, group_body, 0)
+
+
+def reorder(values, order):
+    rows, width = values.shape
+    group = SUBLANES // rows
+    groups = width // (LANES * group)
+    doubled = jnp.tile(values.astype(jnp.float32), (group, 1))
+    index = order.reshape(groups, group, 1, LANES)
+    index = jnp.broadcast_to(index, (groups, group, rows, LANES)).reshape(groups, SUBLANES, LANES)
+    out = pl.pallas_call(
+        _lane_gather_kernel,
+        out_shape=jax.ShapeDtypeStruct((groups, SUBLANES, LANES), jnp.float32),
+    )(doubled, index % LANES, index // LANES)
+    out = out.reshape(groups, group, rows, LANES).transpose(2, 0, 1, 3).reshape(rows, width)
+    return out.astype(values.dtype)
 
 
 def per_device(
@@ -35,8 +83,7 @@
         window = max(window, high_t - low_t)
     block_entries = 4 * BL
 
-    local_order = node_reordering - col_index * width
-    mine = jnp.take(magnetic_potential_input, local_order, axis=1)
+    mine = reorder(magnetic_potential_input, node_reordering - col_index * width)
 
     ordered = lax.all_gather(mine, "row", axis=0, tiled=True)
     leaf_clusters = ordered.reshape(states, cluster_extent, leaf)
@@ -89,7 +136,9 @@
         precision=lax.Precision.HIGHEST,
     ).reshape(row_span, states, leaf)
     partial_sum = partial_sum.transpose(1, 0, 2).reshape(states, row_span * leaf)
-    return lax.psum_scatter(partial_sum, "col", scatter_dimension=0, tiled=True)
+
+    exchanged = lax.all_to_all(partial_sum, "col", 0, 0, tiled=True)
+    return exchanged.reshape(col_count, states // col_count, row_span * leaf).sum(axis=0)
 
 
 def solution(mesh):

time: 133 us -> 87.2 us (0.66)
  local copies, waits for them, and re-layouts: 46.4 us -> 10.5 us
  waiting for transfers between devices: 22.4 us -> 0.01 us
  blocking collectives: 25.8 us -> 47.3 us
  Pallas kernels: 0 us -> 15.8 us
  between operations: 13.7 us -> 0.25 us
  other arithmetic: 15.1 us -> 3.56 us
    gather x1 -> x0, local copies, waits for them, and re-layouts: 30 us -> none  [per_device(): mine = jnp.take(magnetic_potential_input, local_order, axis=1)]
    reduce_scatter x1 -> x0, waiting for transfers between devices: 22.4 us -> none  [per_device(): return lax.psum_scatter(partial_sum, 'col', scatter_dimension=0, tiled=True)]
    all_to_all x0 -> x1, blocking collectives: none -> 20 us  [per_device(): exchanged = lax.all_to_all(partial_sum, 'col', 0, 0, tiled=True)]
    pallas_call x0 -> x1, Pallas kernels: none -> 15.8 us  [reorder(): pl.pallas_call(_lane_gather_kernel, out_shape=jax.ShapeDtypeStruct((group...]
    unnamed x1 -> x0, other arithmetic: 6.58 us -> none
    select_n x1, other arithmetic: 6.55 us -> 0.8 us  [reorder(): index // LANES]
    unnamed x11 -> x8, local copies, waits for them, and re-layouts: 5.71 us -> 0.02 us
    select_n x1 -> x0, local copies, waits for them, and re-layouts: 1.98 us -> none  [per_device(): mine = jnp.take(magnetic_potential_input, local_order, axis=1)]
  transfers between devices with their start and end apart: 2 -> 1, of which waited for: 1 -> 0; matrix products, arithmetic and copies ran while one was open for 12% -> 8% of each run, Pallas kernels for 0% -> 0%
where the time goes in v3:
time: 87.2 us; the launch traced here: 86.6 us
  blocking collectives  47.3 us (54%)
  Pallas kernels  15.8 us (18%)
  local copies, waits for them, and re-layouts  10.5 us (12%)
  matrix products  5.1 us (6%)
  starting transfers between devices  4.07 us (5%)
  other arithmetic  3.56 us (4%)
    all_to_all x1, blocking collectives, per_device(): exchanged = lax.all_to_all(partial_sum, 'col', 0, 0, tiled=True)  20 us
    pallas_call x1, Pallas kernels, reorder(): pl.pallas_call(_lane_gather_kernel, out_shape=jax.ShapeDtypeStruct((group...  15.8 us
    all_gather x1, blocking collectives, per_device(): every_block = lax.all_gather(mine, 'col', axis=0, tiled=False)  15.6 us
    all_gather x1, blocking collectives, per_device(): ordered = lax.all_gather(mine, 'row', axis=0, tiled=True)  11.7 us
    all_to_all x1, starting transfers between devices, per_device(): lax.all_to_all(send, 'row', 0, 0, tiled=True).reshape(states, window, leaf)  4.07 us
    reshape x2, local copies, waits for them, and re-layouts, per_device(): leaf_clusters = ordered.reshape(states, cluster_extent, leaf)  2.5 us
    reshape x2, local copies, waits for them, and re-layouts, per_device(): lax.all_to_all(send, 'row', 0, 0, tiled=True).reshape(states, window, leaf)  1.94 us
  transfers between devices with their start and end apart: 1, of which 0 were waited for; matrix products, arithmetic and copies ran while one was open for 8% of the time, Pallas kernels for 0%

profile of v3, /device:TPU:0, one launch (start us, length us, event | category | flops | bytes accessed | tf_op | source)
XLA Modules:
  0.0 86.6 jit_solution(4052842633906450485)
XLA Ops:
  0.0 0.0 copy-start
  0.0 0.9 %broadcast_subtract_fusion = s32[8192]{0:T(1024)S(1)} fusion(s32[8192]{0:T(1024)} %param.9, s32[]{:T(128)S(6)} %mul.21), kind=kLoop, calls=%fused_computation.39 | loop fusion | flops 8192 | bytes 65540 | tf_op jit(solution)/shard_map/sub | solution.py:86
  0.9 0.8 add_select_fusion
  1.7 0.9 tile.4
  2.6 0.8 tile.10.values_ref
  3.4 15.8 %shard_map.82 = f32[32,8,128]{2,1,0:T(8,128)} custom-call(f32[8,8192]{1,0:T(8,128)} %tile.10.values_ref, s32[32,8,128]{2,1,0:T(8,128)} %get-tuple-element.18.low_ref, s32[32,8,128]{2,1,0:T(8,128)} %get-tuple-element.17.high_ref), custom_call_target="tpu_custom_call" | custom-call | tf_op jit(solution)/shard_map/pallas_call | solution.py:50
  19.2 0.9 %convert_element_type.33 = bf16[32,8,128]{2,1,0:T(8,128)(2,1)S(1)} convert(f32[32,8,128]{2,1,0:T(8,128)} %shard_map.82) | non-fusion elementwise | flops 32768 | bytes 196608 | tf_op jit(solution)/shard_map/convert_element_type | solution.py:55
  20.1 15.6 %all_gather.7 = bf16[4,4,8192]{2,1,0:T(4,128)(2,1)S(1)} all-gather(bf16[1,4,8192]{2,1,0:T(4,128)(2,1)S(1)} %bitcast.66), channel_id=1, replica_groups=mesh['row'=8,'col'=4] {'col'}, dimensions={0}, use_global_device_ids=true | all-gather | bytes 327680 | tf_op jit(solution)/shard_map/all_gather | solution.py:91
  35.7 0.0 copy-start.1
  35.7 0.0 copy-start.2
  35.7 0.0 copy-start.3
  35.7 0.1 slice_bitcast_fusion.1
  35.8 0.2 concatenate.10
  36.1 0.8 all_to_all.12
  36.9 4.1 %all-to-all-start = ((bf16[8,4,4864]{2,1,0:T(4,128)(2,1)}), bf16[8,4,4864]{2,1,0:T(4,128)(2,1)}, u32[]{:S(2)}, u32[]{:S(2)}) async-start(bf16[8,4,4864]{2,1,0:T(4,128)(2,1)} %all_to_all.12), calls=%async_computation | async-start | bytes 622592 | tf_op jit(solution)/shard_map/all_to_all | solution.py:98
  41.0 11.7 %all-gather = bf16[8,4,8192]{2,1,0:T(4,128)(2,1)S(1)} all-gather(bf16[1,4,8192]{2,1,0:T(4,128)(2,1)S(1)} %bitcast.67), channel_id=1, replica_groups=mesh['row'=8,'col'=4] {'row'}, dimensions={0}, use_global_device_ids=true | all-gather | bytes 589824 | tf_op jit(solution)/shard_map/all_gather | solution.py:88
  52.7 0.0 copy-done.1
  52.7 0.0 copy-done.2
  52.8 0.0 copy-done.3
  52.9 1.2 %reshape.71 = bf16[32,32,256]{2,1,0:T(8,128)(2,1)} reshape(bf16[8,4,8192]{2,1,0:T(4,128)(2,1)S(1)} %all-gather) | data formatting | bytes 1048576 | tf_op jit(solution)/shard_map/reshape | solution.py:89
  54.0 1.3 %copy.15 = bf16[32,32,256]{2,0,1:T(8,128)(2,1)S(1)} copy(bf16[32,32,256]{2,1,0:T(8,128)(2,1)} %reshape.71) | data formatting | bytes 1048576 | tf_op jit(solution)/shard_map/reshape | solution.py:89
  55.4 0.6 gather_fusion.1
  55.9 1.4 %fusion.5 = f32[30,32,32]{2,1,0:T(8,128)S(1)} fusion(bf16[30,256,32]{1,2,0:T(8,128)(2,1)} %param.14, bf16[30,32,256]{2,1,0:T(8,128)(2,1)S(1)} %gather_fusion.1, pred[30]{0:T(512)(128)(4,1)S(1)} %get-tuple-element.7), kind=kOutput, calls=%fused_computation.9 | convolution fusion | flops 15974400 | bytes 1105950 | tf_op jit(solution)/shard_map/spk,pkr->psr/dot_general | solution.py:110
  57.3 0.2 reshape.72
  57.6 0.2 convolution_convert_fusion
  57.7 0.1 pad_add_fusion
  57.8 0.1 reshape.73
  57.9 0.6 gather_fusion.2
  58.5 1.4 %fusion.14 = f32[30,32,256]{2,1,0:T(8,128)S(1)} fusion(bf16[30,256,32]{1,2,0:T(8,128)(2,1)} %param.12, bf16[30,32,32]{2,1,0:T(8,128)(2,1)S(1)} %gather_fusion.2, pred[30]{0:T(512)(128)(4,1)S(1)} %and_bitcast_fusion.1), kind=kOutput, calls=%fused_computation.18 | convolution fusion | flops 15759360 | bytes 1536030 | tf_op jit(solution)/shard_map/psr,plr->psl/dot_general | solution.py:124
  59.9 0.0 all-to-all-done
  59.9 1.2 %reshape.70 = bf16[32,19,256]{2,1,0:T(8,128)(2,1)S(1)} reshape(bf16[8,4,4864]{2,1,0:T(4,128)(2,1)} %all-to-all-done) | data formatting | bytes 622592 | tf_op jit(solution)/shard_map/reshape | solution.py:98
  61.1 0.8 copy.14
  61.9 1.5 %gather_fusion = bf16[16,32,256]{2,1,0:T(8,128)(2,1)S(1)} fusion(bf16[32,19,256]{2,0,1:T(8,128)(2,1)} %copy.14, s32[1024]{0:T(1024)S(1)} %pad_clamp_fusion.2), kind=kCustom, calls=%fused_computation | custom fusion | bytes 524352 | tf_op jit(solution)/shard_map/jit(_take)/gather | solution.py:104
  63.4 0.0 copy-done
  63.4 0.7 fusion.9
  64.1 0.1 pad_maximum_fusion
  64.2 0.1 slice_bitcast_fusion
  64.4 1.5 %fusion.2 = f32[32,16,256]{2,1,0:T(8,128)S(1)} fusion(f32[32,256,46]{1,0,2:T(8,128)S(1)} %slice_bitcast_fusion, s32[46]{0:T(128)S(1)} %pad_add_fusion), kind=kOutput, calls=%fused_computation.7 | convolution fusion | flops 72352480 | bytes 2031800 | tf_op jit(solution)/shard_map/dot_general | solution.py:133
  65.8 0.1 all_to_all.14
  65.9 20.0 %all_to_all.18 = f32[4,8,4096]{2,1,0:T(8,128)S(1)} all-to-all(f32[4,8,4096]{2,1,0:T(8,128)S(1)} %all_to_all.14), channel_id=1, replica_groups=mesh['row'=8,'col'=4] {'col'}, dimensions={0} | all-to-all | bytes 1048576 | tf_op jit(solution)/shard_map/all_to_all | solution.py:140
  85.9 0.7 reduce_sum.9
  (10 shorter events, 0.1 us)
Async XLA Ops:
  0.0 63.4 %copy-start = (bf16[16,256,256]{2,1,0:T(8,128)(2,1)S(1)}, bf16[16,256,256]{2,1,0:T(8,128)(2,1)}, u32[]{:S(2)}) copy-start(bf16[16,256,256]{2,1,0:T(8,128)(2,1)} %param.10) | copy-start | bytes 6291460
  35.7 17.0 %copy-start.1 = (s32[30,2]{0,1:T(2,128)S(1)}, s32[30,2]{0,1:T(2,128)}, u32[]{:S(2)}) copy-start(s32[30,2]{0,1:T(2,128)} %param.13) | copy-start | bytes 724
  35.7 17.0 %copy-start.2 = (s32[16,2]{0,1:T(2,128)S(1)}, s32[16,2]{0,1:T(2,128)}, u32[]{:S(2)}) copy-start(s32[16,2]{0,1:T(2,128)} %param.11) | copy-start | bytes 388
  35.7 17.1 %copy-start.3 = (s32[30,2]{0,1:T(2,128)S(1)}, s32[30,2]{0,1:T(2,128)}, u32[]{:S(2)}) copy-start(s32[30,2]{0,1:T(2,128)} %param.15) | copy-start | bytes 724
  36.9 23.0 %all-to-all-start = ((bf16[8,4,4864]{2,1,0:T(4,128)(2,1)}), bf16[8,4,4864]{2,1,0:T(4,128)(2,1)}, u32[]{:S(2)}, u32[]{:S(2)}) async-start(bf16[8,4,4864]{2,1,0:T(4,128)(2,1)} %all_to_all.12), calls=%async_computation | async-start | bytes 622592 | tf_op jit(solution)/shard_map/all_to_all | solution.py:98

commit v4 on v3

--- a/solution.py
+++ b/solution.py
@@ -88,7 +88,9 @@
     ordered = lax.all_gather(mine, "row", axis=0, tiled=True)
     leaf_clusters = ordered.reshape(states, cluster_extent, leaf)
 
-    every_block = lax.all_gather(mine, "col", axis=0, tiled=False)
+    every_block = lax.all_to_all(jnp.tile(mine, (col_count, 1)), "col", 0, 0, tiled=True).reshape(
+        col_count, local_states, width
+    )
     pieces = []
     for target in range(row_count):
         home_t = target * col_count // row_count

time: 87.2 us -> 80.7 us (0.925)
  blocking collectives: 47.3 us -> 28.3 us
  starting transfers between devices: 4.07 us -> 10.4 us
  waiting for transfers between devices: 0.01 us -> 5.3 us
    all_gather x1 -> x0, blocking collectives: 15.6 us -> none  [per_device(): every_block = lax.all_gather(mine, 'col', axis=0, tiled=False)]
    all_to_all x0 -> x1, starting transfers between devices: none -> 6.32 us  [per_device(): lax.all_to_all(jnp.tile(mine, (col_count, 1)), 'col', 0, 0, tiled=True)]
    all_to_all x1, waiting for transfers between devices: 0.01 us -> 5.3 us  [per_device(): lax.all_to_all(send, 'row', 0, 0, tiled=True).reshape(states, window, leaf)]
    all_gather x1, blocking collectives: 11.7 us -> 9.87 us  [per_device(): ordered = lax.all_gather(mine, 'row', axis=0, tiled=True)]
    all_to_all x1, blocking collectives: 20 us -> 18.5 us  [per_device(): exchanged = lax.all_to_all(partial_sum, 'col', 0, 0, tiled=True)]
  transfers between devices with their start and end apart: 1 -> 2, of which waited for: 0 -> 1; matrix products, arithmetic and copies ran while one was open for 8% -> 9% of each run, Pallas kernels for 0% -> 0%
where the time goes in v4:
time: 80.7 us; the launch traced here: 80 us
  blocking collectives  28.3 us (35%)
  Pallas kernels  15.8 us (20%)
  local copies, waits for them, and re-layouts  11.3 us (14%)
  starting transfers between devices  10.4 us (13%)
  waiting for transfers between devices  5.3 us (7%)
  matrix products  5.1 us (6%)
  other arithmetic  3.57 us (4%)
    all_to_all x1, blocking collectives, per_device(): exchanged = lax.all_to_all(partial_sum, 'col', 0, 0, tiled=True)  18.5 us
    pallas_call x1, Pallas kernels, reorder(): pl.pallas_call(_lane_gather_kernel, out_shape=jax.ShapeDtypeStruct((group...  15.8 us
    all_gather x1, blocking collectives, per_device(): ordered = lax.all_gather(mine, 'row', axis=0, tiled=True)  9.87 us
    all_to_all x1, starting transfers between devices, per_device(): lax.all_to_all(jnp.tile(mine, (col_count, 1)), 'col', 0, 0, tiled=True)  6.32 us
    all_to_all x1, waiting for transfers between devices, per_device(): lax.all_to_all(send, 'row', 0, 0, tiled=True).reshape(states, window, leaf)  5.3 us
    all_to_all x1, starting transfers between devices, per_device(): lax.all_to_all(send, 'row', 0, 0, tiled=True).reshape(states, window, leaf)  4.07 us
    reshape x2, local copies, waits for them, and re-layouts, per_device(): leaf_clusters = ordered.reshape(states, cluster_extent, leaf)  2.49 us
    reshape x2, local copies, waits for them, and re-layouts, per_device(): lax.all_to_all(send, 'row', 0, 0, tiled=True).reshape(states, window, leaf)  1.93 us
  transfers between devices with their start and end apart: 2, of which 1 were waited for; matrix products, arithmetic and copies ran while one was open for 9% of the time, Pallas kernels for 0%

profile of v4, /device:TPU:0, one launch (start us, length us, event | category | flops | bytes accessed | tf_op | source)
XLA Modules:
  0.0 80.0 jit_solution(4249720440662165214)
XLA Ops:
  0.0 0.0 copy-start
  0.0 0.9 %broadcast_subtract_fusion = s32[8192]{0:T(1024)S(1)} fusion(s32[8192]{0:T(1024)} %param.9, s32[]{:T(128)S(6)} %mul.21), kind=kLoop, calls=%fused_computation.39 | loop fusion | flops 8192 | bytes 65540 | tf_op jit(solution)/shard_map/sub | solution.py:86
  0.9 0.0 copy-start.1
  1.0 0.0 copy-start.2
  1.0 0.0 copy-start.3
  1.0 0.8 %add_select_fusion = (s32[32,8,128]{2,1,0:T(8,128)}, s32[32,8,128]{2,1,0:T(8,128)}) fusion(s32[32,8,128]{2,1,0:T(8,128)S(1)} %bitcast.70), kind=kLoop, calls=%fused_computation.21 | loop fusion | flops 622592 | bytes 393216 | tf_op jit(solution)/shard_map/jit(floor_divide)/jit(_where)/select_n | solution.py:53
  1.8 0.9 %tile.6 = f32[2,4,8192]{2,1,0:T(4,128)S(1)} broadcast(bf16[4,8192]{1,0:T(4,128)(2,1)} %param.8), dimensions={1,2} | broadcast | bytes 327680 | tf_op jit(solution)/shard_map/tile | solution.py:47
  2.7 0.8 %tile.7.values_ref = f32[8,8192]{1,0:T(8,128)} reshape(f32[2,4,8192]{2,1,0:T(4,128)S(1)} %tile.6) | data formatting | bytes 524288 | tf_op jit(solution)/shard_map/tile | solution.py:47
  3.5 15.8 %shard_map.82 = f32[32,8,128]{2,1,0:T(8,128)} custom-call(f32[8,8192]{1,0:T(8,128)} %tile.7.values_ref, s32[32,8,128]{2,1,0:T(8,128)} %get-tuple-element.18.low_ref, s32[32,8,128]{2,1,0:T(8,128)} %get-tuple-element.17.high_ref), custom_call_target="tpu_custom_call" | custom-call | tf_op jit(solution)/shard_map/pallas_call | solution.py:50
  19.2 0.9 %convert_element_type.25 = bf16[32,8,128]{2,1,0:T(8,128)(2,1)S(1)} convert(f32[32,8,128]{2,1,0:T(8,128)} %shard_map.82) | non-fusion elementwise | flops 32768 | bytes 196608 | tf_op jit(solution)/shard_map/convert_element_type | solution.py:55
  20.2 0.8 tile.8
  20.9 6.3 %all-to-all-start = ((bf16[4,4,8192]{2,1,0:T(4,128)(2,1)}), bf16[4,4,8192]{2,1,0:T(4,128)(2,1)S(1)}, u32[]{:S(2)}, u32[]{:S(2)}) async-start(bf16[4,4,8192]{2,1,0:T(4,128)(2,1)} %tile.8), calls=%async_computation | async-start | bytes 524288 | tf_op jit(solution)/shard_map/all_to_all | solution.py:91
  27.2 0.0 copy-done.1
  27.3 0.0 copy-done.2
  27.3 0.0 copy-done.3
  27.4 9.9 %all-gather = bf16[8,4,8192]{2,1,0:T(4,128)(2,1)S(1)} all-gather(bf16[1,4,8192]{2,1,0:T(4,128)(2,1)S(1)} %bitcast.69), channel_id=1, replica_groups=mesh['row'=8,'col'=4] {'row'}, dimensions={0}, use_global_device_ids=true | all-gather | bytes 589824 | tf_op jit(solution)/shard_map/all_gather | solution.py:88
  37.2 1.2 %reshape.72 = bf16[32,32,256]{2,1,0:T(8,128)(2,1)} reshape(bf16[8,4,8192]{2,1,0:T(4,128)(2,1)S(1)} %all-gather) | data formatting | bytes 1048576 | tf_op jit(solution)/shard_map/reshape | solution.py:89
  38.4 1.3 %copy.15 = bf16[32,32,256]{2,0,1:T(8,128)(2,1)S(1)} copy(bf16[32,32,256]{2,1,0:T(8,128)(2,1)} %reshape.72) | data formatting | bytes 1048576 | tf_op jit(solution)/shard_map/reshape | solution.py:89
  39.7 0.6 gather_fusion.1
  40.3 1.4 %fusion.5 = f32[30,32,32]{2,1,0:T(8,128)S(1)} fusion(bf16[30,256,32]{1,2,0:T(8,128)(2,1)} %param.14, bf16[30,32,256]{2,1,0:T(8,128)(2,1)S(1)} %gather_fusion.1, pred[30]{0:T(512)(128)(4,1)S(1)} %get-tuple-element.7), kind=kOutput, calls=%fused_computation.9 | convolution fusion | flops 15974400 | bytes 1105950 | tf_op jit(solution)/shard_map/spk,pkr->psr/dot_general | solution.py:112
  41.7 0.2 reshape.73
  42.0 0.2 convolution_convert_fusion
  42.1 0.0 all-to-all-done
  42.1 0.1 slice_bitcast_fusion.1
  42.3 0.2 concatenate.10
  42.5 0.8 all_to_all.17
  43.3 4.1 %all-to-all-start.1 = ((bf16[8,4,4864]{2,1,0:T(4,128)(2,1)}), bf16[8,4,4864]{2,1,0:T(4,128)(2,1)}, u32[]{:S(2)}, u32[]{:S(2)}) async-start(bf16[8,4,4864]{2,1,0:T(4,128)(2,1)} %all_to_all.17), calls=%async_computation.1 | async-start | bytes 622592 | tf_op jit(solution)/shard_map/all_to_all | solution.py:100
  47.4 0.1 pad_add_fusion
  47.4 0.1 reshape.74
  47.5 0.6 gather_fusion.2
  48.1 1.4 %fusion.14 = f32[30,32,256]{2,1,0:T(8,128)S(1)} fusion(bf16[30,256,32]{1,2,0:T(8,128)(2,1)} %param.12, bf16[30,32,32]{2,1,0:T(8,128)(2,1)S(1)} %gather_fusion.2, pred[30]{0:T(512)(128)(4,1)S(1)} %and_bitcast_fusion.1), kind=kOutput, calls=%fused_computation.18 | convolution fusion | flops 15759360 | bytes 1536030 | tf_op jit(solution)/shard_map/psr,plr->psl/dot_general | solution.py:126
  49.5 5.3 %all-to-all-done.1 = bf16[8,4,4864]{2,1,0:T(4,128)(2,1)} async-done(((bf16[8,4,4864]{2,1,0:T(4,128)(2,1)}), bf16[8,4,4864]{2,1,0:T(4,128)(2,1)}, u32[]{:S(2)}, u32[]{:S(2)}) %all-to-all-start.1) | async-done | bytes 311328 | tf_op jit(solution)/shard_map/all_to_all | solution.py:100
  54.8 1.1 %reshape.71 = bf16[32,19,256]{2,1,0:T(8,128)(2,1)S(1)} reshape(bf16[8,4,4864]{2,1,0:T(4,128)(2,1)} %all-to-all-done.1) | data formatting | bytes 622592 | tf_op jit(solution)/shard_map/reshape | solution.py:100
  56.0 0.8 copy.14
  56.8 1.5 %gather_fusion = bf16[16,32,256]{2,1,0:T(8,128)(2,1)S(1)} fusion(bf16[32,19,256]{2,0,1:T(8,128)(2,1)} %copy.14, s32[1024]{0:T(1024)S(1)} %pad_clamp_fusion.2), kind=kCustom, calls=%fused_computation | custom fusion | bytes 524352 | tf_op jit(solution)/shard_map/jit(_take)/gather | solution.py:106
  58.3 0.0 copy-done
  58.3 0.7 fusion.9
  59.0 0.1 pad_maximum_fusion
  59.2 0.1 slice_bitcast_fusion
  59.3 1.5 %fusion.2 = f32[32,16,256]{2,1,0:T(8,128)S(1)} fusion(f32[32,256,46]{1,0,2:T(8,128)S(1)} %slice_bitcast_fusion, s32[46]{0:T(128)S(1)} %pad_add_fusion), kind=kOutput, calls=%fused_computation.7 | convolution fusion | flops 72352480 | bytes 2031800 | tf_op jit(solution)/shard_map/dot_general | solution.py:135
  60.7 0.1 all_to_all.19
  60.8 18.5 %all_to_all.24 = f32[4,8,4096]{2,1,0:T(8,128)S(1)} all-to-all(f32[4,8,4096]{2,1,0:T(8,128)S(1)} %all_to_all.19), channel_id=1, replica_groups=mesh['row'=8,'col'=4] {'col'}, dimensions={0} | all-to-all | bytes 1048576 | tf_op jit(solution)/shard_map/all_to_all | solution.py:142
  79.3 0.7 reduce_sum.9
  (10 shorter events, 0.1 us)
Async XLA Ops:
  0.0 58.3 %copy-start = (bf16[16,256,256]{2,1,0:T(8,128)(2,1)S(1)}, bf16[16,256,256]{2,1,0:T(8,128)(2,1)}, u32[]{:S(2)}) copy-start(bf16[16,256,256]{2,1,0:T(8,128)(2,1)} %param.10) | copy-start | bytes 6291460
  0.9 26.3 %copy-start.1 = (s32[30,2]{0,1:T(2,128)S(1)}, s32[30,2]{0,1:T(2,128)}, u32[]{:S(2)}) copy-start(s32[30,2]{0,1:T(2,128)} %param.13) | copy-start | bytes 724
  1.0 26.3 %copy-start.2 = (s32[16,2]{0,1:T(2,128)S(1)}, s32[16,2]{0,1:T(2,128)}, u32[]{:S(2)}) copy-start(s32[16,2]{0,1:T(2,128)} %param.11) | copy-start | bytes 388
  1.0 26.4 %copy-start.3 = (s32[30,2]{0,1:T(2,128)S(1)}, s32[30,2]{0,1:T(2,128)}, u32[]{:S(2)}) copy-start(s32[30,2]{0,1:T(2,128)} %param.15) | copy-start | bytes 724
  20.9 21.2 %all-to-all-start = ((bf16[4,4,8192]{2,1,0:T(4,128)(2,1)}), bf16[4,4,8192]{2,1,0:T(4,128)(2,1)S(1)}, u32[]{:S(2)}, u32[]{:S(2)}) async-start(bf16[4,4,8192]{2,1,0:T(4,128)(2,1)} %tile.8), calls=%async_computation | async-start | bytes 524288 | tf_op jit(solution)/shard_map/all_to_all | solution.py:91
  43.3 11.6 %all-to-all-start.1 = ((bf16[8,4,4864]{2,1,0:T(4,128)(2,1)}), bf16[8,4,4864]{2,1,0:T(4,128)(2,1)}, u32[]{:S(2)}, u32[]{:S(2)}) async-start(bf16[8,4,4864]{2,1,0:T(4,128)(2,1)} %all_to_all.17), calls=%async_computation.1 | async-start | bytes 622592 | tf_op jit(solution)/shard_map/all_to_all | solution.py:100

commit v5 on v3

--- a/solution.py
+++ b/solution.py
@@ -81,20 +81,27 @@
         low_t = max(base_t - REACH, 0)
         high_t = min(base_t + row_span + REACH, cluster_extent)
         window = max(window, high_t - low_t)
+    while (local_states * window * leaf) % (SUBLANES * 2 * LANES) and window < cluster_extent:
+        window += 1
     block_entries = 4 * BL
 
     mine = reorder(magnetic_potential_input, node_reordering - col_index * width)
 
-    ordered = lax.all_gather(mine, "row", axis=0, tiled=True)
+    dense = (SUBLANES * 2, local_states * width // (SUBLANES * 2))
+    ordered = lax.all_gather(mine.reshape(dense), "row", axis=0, tiled=True)
     leaf_clusters = ordered.reshape(states, cluster_extent, leaf)
 
-    every_block = lax.all_gather(mine, "col", axis=0, tiled=False)
+    every_block = lax.all_to_all(
+        jnp.tile(mine.reshape(dense), (col_count, 1)), "col", 0, 0, tiled=True
+    ).reshape(col_count, local_states, width)
     pieces = []
     for target in range(row_count):
         home_t = target * col_count // row_count
         start_t = min(max(target * row_span - home_t * cluster_extent - REACH, 0), cluster_extent - window)
         pieces.append(every_block[home_t, :, start_t * leaf:(start_t + window) * leaf])
-    send = jnp.concatenate(pieces, axis=0)
+    send = jnp.stack(pieces)
+    if (local_states * window * leaf) % (SUBLANES * 2 * LANES) == 0:
+        send = send.reshape(row_count * SUBLANES * 2, -1)
     near_window = lax.all_to_all(send, "row", 0, 0, tiled=True).reshape(states, window, leaf)
 
     home = row_index * col_count // row_count

time: 87.2 us -> 81.1 us (0.930)
  blocking collectives: 47.3 us -> 28.2 us
  starting transfers between devices: 4.07 us -> 10.4 us
  waiting for transfers between devices: 0.01 us -> 5.48 us
  local copies, waits for them, and re-layouts: 10.5 us -> 11.6 us
    all_gather x2 -> x1, blocking collectives: 27.3 us -> 9.85 us  [per_device(): ordered = lax.all_gather(mine.reshape(dense), 'row', axis=0, tiled=True)]
    all_to_all x0 -> x1, starting transfers between devices: none -> 6.32 us  [per_device(): lax.all_to_all(jnp.tile(mine.reshape(dense), (col_count, 1)), 'col', 0, 0...]
    all_to_all x1, waiting for transfers between devices: 0.01 us -> 5.48 us  [per_device(): lax.all_to_all(send, 'row', 0, 0, tiled=True).reshape(states, window, leaf)]
    all_to_all x1, blocking collectives: 20 us -> 18.4 us  [per_device(): exchanged = lax.all_to_all(partial_sum, 'col', 0, 0, tiled=True)]
  transfers between devices with their start and end apart: 1 -> 2, of which waited for: 0 -> 1; matrix products, arithmetic and copies ran while one was open for 8% -> 9% of each run, Pallas kernels for 0% -> 0%
where the time goes in v5:
time: 81.1 us; the launch traced here: 80.4 us
  blocking collectives  28.2 us (35%)
  Pallas kernels  15.8 us (19%)
  local copies, waits for them, and re-layouts  11.6 us (14%)
  starting transfers between devices  10.4 us (13%)
  waiting for transfers between devices  5.48 us (7%)
  matrix products  5.1 us (6%)
  other arithmetic  3.56 us (4%)
    all_to_all x1, blocking collectives, per_device(): exchanged = lax.all_to_all(partial_sum, 'col', 0, 0, tiled=True)  18.4 us
    pallas_call x1, Pallas kernels, reorder(): pl.pallas_call(_lane_gather_kernel, out_shape=jax.ShapeDtypeStruct((group...  15.8 us
    all_gather x1, blocking collectives, per_device(): ordered = lax.all_gather(mine.reshape(dense), 'row', axis=0, tiled=True)  9.85 us
    all_to_all x1, starting transfers between devices, per_device(): lax.all_to_all(jnp.tile(mine.reshape(dense), (col_count, 1)), 'col', 0, 0...  6.32 us
    all_to_all x1, waiting for transfers between devices, per_device(): lax.all_to_all(send, 'row', 0, 0, tiled=True).reshape(states, window, leaf)  5.48 us
    all_to_all x1, starting transfers between devices, per_device(): lax.all_to_all(send, 'row', 0, 0, tiled=True).reshape(states, window, leaf)  4.07 us
    reshape x2, local copies, waits for them, and re-layouts, per_device(): leaf_clusters = ordered.reshape(states, cluster_extent, leaf)  2.37 us
    reshape x2, local copies, waits for them, and re-layouts, per_device(): lax.all_to_all(send, 'row', 0, 0, tiled=True).reshape(states, window, leaf)  2.03 us
  transfers between devices with their start and end apart: 2, of which 1 were waited for; matrix products, arithmetic and copies ran while one was open for 9% of the time, Pallas kernels for 0%

profile of v5, /device:TPU:0, one launch (start us, length us, event | category | flops | bytes accessed | tf_op | source)
XLA Modules:
  0.0 80.4 jit_solution(6496538690006164350)
XLA Ops:
  0.0 0.0 copy-start
  0.0 0.9 %broadcast_subtract_fusion = s32[8192]{0:T(1024)S(1)} fusion(s32[8192]{0:T(1024)} %param.9, s32[]{:T(128)S(6)} %mul.21), kind=kLoop, calls=%fused_computation.40 | loop fusion | flops 8192 | bytes 65540 | tf_op jit(solution)/shard_map/sub | solution.py:88
  0.9 0.8 add_select_fusion
  1.7 0.9 %tile.6 = f32[2,4,8192]{2,1,0:T(4,128)S(1)} broadcast(bf16[4,8192]{1,0:T(4,128)(2,1)} %param.8), dimensions={1,2} | broadcast | bytes 327680 | tf_op jit(solution)/shard_map/tile | solution.py:47
  2.6 0.0 copy-start.1
  2.6 0.0 copy-start.2
  2.6 0.0 copy-start.3
  2.6 0.8 tile.7.values_ref
  3.4 15.8 %shard_map.82 = f32[32,8,128]{2,1,0:T(8,128)} custom-call(f32[8,8192]{1,0:T(8,128)} %tile.7.values_ref, s32[32,8,128]{2,1,0:T(8,128)} %get-tuple-element.10.low_ref, s32[32,8,128]{2,1,0:T(8,128)} %get-tuple-element.9.high_ref), custom_call_target="tpu_custom_call" | custom-call | tf_op jit(solution)/shard_map/pallas_call | solution.py:50
  19.2 0.9 %convert_element_type.26 = bf16[32,8,128]{2,1,0:T(8,128)(2,1)S(1)} convert(f32[32,8,128]{2,1,0:T(8,128)} %shard_map.82) | non-fusion elementwise | flops 32768 | bytes 196608 | tf_op jit(solution)/shard_map/convert_element_type | solution.py:55
  20.1 0.1 copy.23
  20.2 0.7 tile.8
  21.0 6.3 %all-to-all-start = ((bf16[4,16,2048]{2,1,0:T(8,128)(2,1)}), bf16[4,16,2048]{2,1,0:T(8,128)(2,1)S(1)}, u32[]{:S(2)}, u32[]{:S(2)}) async-start(bf16[4,16,2048]{2,1,0:T(8,128)(2,1)} %tile.8), calls=%async_computation | async-start | bytes 524288 | tf_op jit(solution)/shard_map/all_to_all | solution.py:94
  27.3 9.9 %all_gather.3 = bf16[128,2048]{1,0:T(8,128)(2,1)S(1)} all-gather(bf16[16,2048]{1,0:T(8,128)(2,1)S(1)} %convert_element_type.29), channel_id=1, replica_groups=mesh['row'=8,'col'=4] {'row'}, dimensions={0}, use_global_device_ids=true | all-gather | bytes 589824 | tf_op jit(solution)/shard_map/all_gather | solution.py:91
  37.1 0.0 copy-done.1
  37.2 0.0 copy-done.2
  37.2 0.0 copy-done.3
  37.3 1.0 %reshape.79 = bf16[32,32,256]{2,1,0:T(8,128)(2,1)} reshape(bf16[128,2048]{1,0:T(8,128)(2,1)S(1)} %all_gather.3) | data formatting | bytes 1048576 | tf_op jit(solution)/shard_map/reshape | solution.py:92
  38.3 1.3 %copy.14 = bf16[32,32,256]{2,0,1:T(8,128)(2,1)S(1)} copy(bf16[32,32,256]{2,1,0:T(8,128)(2,1)} %reshape.79) | data formatting | bytes 1048576 | tf_op jit(solution)/shard_map/reshape | solution.py:92
  39.6 0.6 gather_fusion.1
  40.2 1.4 %fusion.5 = f32[30,32,32]{2,1,0:T(8,128)S(1)} fusion(bf16[30,256,32]{1,2,0:T(8,128)(2,1)} %param.14, bf16[30,32,256]{2,1,0:T(8,128)(2,1)S(1)} %gather_fusion.1, pred[30]{0:T(512)(128)(4,1)S(1)} %get-tuple-element.7), kind=kOutput, calls=%fused_computation.9 | convolution fusion | flops 15974400 | bytes 1105950 | tf_op jit(solution)/shard_map/spk,pkr->psr/dot_general | solution.py:117
  41.6 0.2 reshape.80
  41.9 0.2 convolution_convert_fusion
  42.0 0.0 all-to-all-done
  42.0 0.3 reshape.77
  42.6 0.9 %all_to_all.17 = bf16[8,16,1280]{2,1,0:T(8,128)(2,1)} reshape(bf16[8,4,5120]{2,1,0:T(4,128)(2,1)S(1)} %slice_dynamic-update-slice_fusion) | data formatting | bytes 655360 | tf_op jit(solution)/shard_map/all_to_all | solution.py:105
  43.5 4.1 %all-to-all-start.1 = ((bf16[8,16,1280]{2,1,0:T(8,128)(2,1)}), bf16[8,16,1280]{2,1,0:T(8,128)(2,1)}, u32[]{:S(2)}, u32[]{:S(2)}) async-start(bf16[8,16,1280]{2,1,0:T(8,128)(2,1)} %all_to_all.17), calls=%async_computation.1 | async-start | bytes 655360 | tf_op jit(solution)/shard_map/all_to_all | solution.py:105
  47.6 0.1 pad_add_fusion
  47.6 0.1 reshape.81
  47.8 0.6 gather_fusion.2
  48.4 1.4 %fusion.14 = f32[30,32,256]{2,1,0:T(8,128)S(1)} fusion(bf16[30,256,32]{1,2,0:T(8,128)(2,1)} %param.12, bf16[30,32,32]{2,1,0:T(8,128)(2,1)S(1)} %gather_fusion.2, pred[30]{0:T(512)(128)(4,1)S(1)} %and_bitcast_fusion.1), kind=kOutput, calls=%fused_computation.18 | convolution fusion | flops 15759360 | bytes 1536030 | tf_op jit(solution)/shard_map/psr,plr->psl/dot_general | solution.py:131
  49.7 5.5 %all-to-all-done.1 = bf16[8,16,1280]{2,1,0:T(8,128)(2,1)} async-done(((bf16[8,16,1280]{2,1,0:T(8,128)(2,1)}), bf16[8,16,1280]{2,1,0:T(8,128)(2,1)}, u32[]{:S(2)}, u32[]{:S(2)}) %all-to-all-start.1) | async-done | bytes 327712 | tf_op jit(solution)/shard_map/all_to_all | solution.py:105
  55.2 1.2 %reshape.78 = bf16[32,20,256]{2,1,0:T(8,128)(2,1)S(1)} reshape(bf16[8,16,1280]{2,1,0:T(8,128)(2,1)} %all-to-all-done.1) | data formatting | bytes 655360 | tf_op jit(solution)/shard_map/reshape | solution.py:105
  56.5 0.8 copy.13
  57.2 1.5 %gather_fusion = bf16[16,32,256]{2,1,0:T(8,128)(2,1)S(1)} fusion(bf16[32,20,256]{2,0,1:T(8,128)(2,1)} %copy.13, s32[1024]{0:T(1024)S(1)} %pad_clamp_fusion.2), kind=kCustom, calls=%fused_computation | custom fusion | bytes 524352 | tf_op jit(solution)/shard_map/jit(_take)/gather | solution.py:111
  58.8 0.0 copy-done
  58.8 0.7 fusion.9
  59.5 0.1 pad_maximum_fusion
  59.6 0.1 slice_bitcast_fusion
  59.7 1.5 %fusion.2 = f32[32,16,256]{2,1,0:T(8,128)S(1)} fusion(f32[32,256,46]{1,0,2:T(8,128)S(1)} %slice_bitcast_fusion, s32[46]{0:T(128)S(1)} %pad_add_fusion), kind=kOutput, calls=%fused_computation.7 | convolution fusion | flops 72352480 | bytes 2031800 | tf_op jit(solution)/shard_map/dot_general | solution.py:140
  61.2 0.1 all_to_all.19
  61.3 18.4 %all_to_all.24 = f32[4,8,4096]{2,1,0:T(8,128)S(1)} all-to-all(f32[4,8,4096]{2,1,0:T(8,128)S(1)} %all_to_all.19), channel_id=1, replica_groups=mesh['row'=8,'col'=4] {'col'}, dimensions={0} | all-to-all | bytes 1048576 | tf_op jit(solution)/shard_map/all_to_all | solution.py:147
  79.7 0.7 reduce_sum.9
  (19 shorter events, 0.3 us)
Async XLA Ops:
  0.0 58.8 %copy-start = (bf16[16,256,256]{2,1,0:T(8,128)(2,1)S(1)}, bf16[16,256,256]{2,1,0:T(8,128)(2,1)}, u32[]{:S(2)}) copy-start(bf16[16,256,256]{2,1,0:T(8,128)(2,1)} %param.10) | copy-start | bytes 6291460
  2.6 34.5 %copy-start.1 = (s32[30,2]{0,1:T(2,128)S(1)}, s32[30,2]{0,1:T(2,128)}, u32[]{:S(2)}) copy-start(s32[30,2]{0,1:T(2,128)} %param.13) | copy-start | bytes 724
  2.6 34.5 %copy-start.2 = (s32[16,2]{0,1:T(2,128)S(1)}, s32[16,2]{0,1:T(2,128)}, u32[]{:S(2)}) copy-start(s32[16,2]{0,1:T(2,128)} %param.11) | copy-start | bytes 388
  2.6 34.6 %copy-start.3 = (s32[30,2]{0,1:T(2,128)S(1)}, s32[30,2]{0,1:T(2,128)}, u32[]{:S(2)}) copy-start(s32[30,2]{0,1:T(2,128)} %param.15) | copy-start | bytes 724
  21.0 21.1 %all-to-all-start = ((bf16[4,16,2048]{2,1,0:T(8,128)(2,1)}), bf16[4,16,2048]{2,1,0:T(8,128)(2,1)S(1)}, u32[]{:S(2)}, u32[]{:S(2)}) async-start(bf16[4,16,2048]{2,1,0:T(8,128)(2,1)} %tile.8), calls=%async_computation | async-start | bytes 524288 | tf_op jit(solution)/shard_map/all_to_all | solution.py:94
  43.5 11.7 %all-to-all-start.1 = ((bf16[8,16,1280]{2,1,0:T(8,128)(2,1)}), bf16[8,16,1280]{2,1,0:T(8,128)(2,1)}, u32[]{:S(2)}, u32[]{:S(2)}) async-start(bf16[8,16,1280]{2,1,0:T(8,128)(2,1)} %all_to_all.17), calls=%async_computation.1 | async-start | bytes 655360 | tf_op jit(solution)/shard_map/all_to_all | solution.py:105

commit v6 on v4

--- a/solution.py
+++ b/solution.py
@@ -2,6 +2,7 @@
 import jax.numpy as jnp
 from jax import lax
 from jax.experimental import pallas as pl
+from jax.experimental.pallas import tpu as pltpu
 from jax.sharding import PartitionSpec as P
 
 BL = 2
@@ -11,17 +12,33 @@
 BATCH = 16
 
 
-def _lane_gather_kernel(values_ref, low_ref, high_ref, out_ref):
-    tiles = values_ref.shape[1] // LANES
-    batch = min(BATCH, out_ref.shape[0])
+def _lane_gather_kernel(values_ref, order_ref, out_ref, doubled_ref):
+    rows, width = values_ref.shape
+    group = SUBLANES // rows
+    tiles = width // LANES
+    groups = tiles // group
+    batch = min(BATCH, groups)
+    for v in range(tiles):
+        piece = values_ref[:, v * LANES:(v + 1) * LANES].astype(jnp.float32)
+        doubled_ref[:, v * LANES:(v + 1) * LANES] = jnp.concatenate([piece] * group, axis=0)
+    sub = lax.broadcasted_iota(jnp.int32, (SUBLANES, LANES), 0) // rows
 
     def group_body(k, carry):
         base = k * batch
-        lows = [low_ref[base + b] for b in range(batch)]
-        highs = [high_ref[base + b] for b in range(batch)]
+        lows, highs = [], []
+        for b in range(batch):
+            first = (base + b) * group
+            index = jnp.broadcast_to(order_ref[pl.ds(first, 1), :], (SUBLANES, LANES))
+            for g in range(1, group):
+                index = jnp.where(
+                    sub == g, jnp.broadcast_to(order_ref[pl.ds(first + g, 1), :], (SUBLANES, LANES)), index
+                )
+            index = index % width
+            lows.append(index % LANES)
+            highs.append(index // LANES)
 
         def tile_body(v, accs):
-            src = values_ref[:, pl.ds(pl.multiple_of(v * LANES, LANES), LANES)]
+            src = doubled_ref[:, pl.ds(pl.multiple_of(v * LANES, LANES), LANES)]
             return tuple(
                 jnp.where(
                     highs[b] == v,
@@ -34,24 +51,21 @@
         zeros = tuple(jnp.zeros((SUBLANES, LANES), jnp.float32) for _ in range(batch))
         accs = lax.fori_loop(0, tiles, tile_body, zeros)
         for b in range(batch):
-            out_ref[base + b] = accs[b]
+            for g in range(group):
+                column = pl.multiple_of(((base + b) * group + g) * LANES, LANES)
+                out_ref[:, pl.ds(column, LANES)] = accs[b][g * rows:(g + 1) * rows, :]
         return carry
 
-    lax.fori_loop(0, out_ref.shape[0] // batch, group_body, 0)
+    lax.fori_loop(0, groups // batch, group_body, 0)
 
 
 def reorder(values, order):
     rows, width = values.shape
-    group = SUBLANES // rows
-    groups = width // (LANES * group)
-    doubled = jnp.tile(values.astype(jnp.float32), (group, 1))
-    index = order.reshape(groups, group, 1, LANES)
-    index = jnp.broadcast_to(index, (groups, group, rows, LANES)).reshape(groups, SUBLANES, LANES)
     out = pl.pallas_call(
         _lane_gather_kernel,
-        out_shape=jax.ShapeDtypeStruct((groups, SUBLANES, LANES), jnp.float32),
-    )(doubled, index % LANES, index // LANES)
-    out = out.reshape(groups, group, rows, LANES).transpose(2, 0, 1, 3).reshape(rows, width)
+        out_shape=jax.ShapeDtypeStruct((rows, width), jnp.float32),
+        scratch_shapes=[pltpu.VMEM((SUBLANES, width), jnp.float32)],
+    )(values, order.reshape(width // LANES, LANES))
     return out.astype(values.dtype)
 
 
@@ -83,10 +97,7 @@
         window = max(window, high_t - low_t)
     block_entries = 4 * BL
 
-    mine = reorder(magnetic_potential_input, node_reordering - col_index * width)
-
-    ordered = lax.all_gather(mine, "row", axis=0, tiled=True)
-    leaf_clusters = ordered.reshape(states, cluster_extent, leaf)
+    mine = reorder(magnetic_potential_input, node_reordering)
 
     every_block = lax.all_to_all(jnp.tile(mine, (col_count, 1)), "col", 0, 0, tiled=True).reshape(
         col_count, local_states, width
@@ -97,6 +108,10 @@
         start_t = min(max(target * row_span - home_t * cluster_extent - REACH, 0), cluster_extent - window)
         pieces.append(every_block[home_t, :, start_t * leaf:(start_t + window) * leaf])
     send = jnp.concatenate(pieces, axis=0)
+    mine_late, send = lax.optimization_barrier((mine, send))
+
+    ordered = lax.all_gather(mine_late, "row", axis=0, tiled=True)
+    leaf_clusters = ordered.reshape(states, cluster_extent, leaf)
     near_window = lax.all_to_all(send, "row", 0, 0, tiled=True).reshape(states, window, leaf)
 
     home = row_index * col_count // row_count

time: 80.7 us -> 82.1 us (1.017)
  other arithmetic: 3.57 us -> 5.33 us
  blocking collectives: 28.3 us -> 29.4 us
  local copies, waits for them, and re-layouts: 11.3 us -> 10.3 us
    all_to_all x1, waiting for transfers between devices: 5.3 us -> 0.01 us  [per_device(): lax.all_to_all(send, 'row', 0, 0, tiled=True).reshape(states, window, leaf)]
    all_to_all x1, waiting for transfers between devices: 0.01 us -> 4.62 us  [per_device(): lax.all_to_all(jnp.tile(mine, (col_count, 1)), 'col', 0, 0, tiled=True)]
    all_gather x1, blocking collectives: 9.87 us -> 11.7 us  [per_device(): ordered = lax.all_gather(mine_late, 'row', axis=0, tiled=True)]
    another operation x2 -> x0, local copies, waits for them, and re-layouts: 1.66 us -> none  [reorder(): doubled = jnp.tile(values.astype(jnp.float32), (group, 1))]
    sub x1 -> x0, other arithmetic: 0.91 us -> none  [per_device(): node_reordering - col_index * width]
  transfers between devices with their start and end apart: 2 -> 2, of which waited for: 1 -> 1; matrix products, arithmetic and copies ran while one was open for 9% -> 14% of each run, Pallas kernels for 0% -> 0%
where the time goes in v6:
time: 82.1 us; the launch traced here: 81.4 us
  blocking collectives  29.4 us (36%)
  Pallas kernels  16.1 us (20%)
  starting transfers between devices  10.4 us (13%)
  local copies, waits for them, and re-layouts  10.3 us (13%)
  other arithmetic  5.33 us (6%)
  matrix products  5.09 us (6%)
  waiting for transfers between devices  4.62 us (6%)
    all_to_all x1, blocking collectives, per_device(): exchanged = lax.all_to_all(partial_sum, 'col', 0, 0, tiled=True)  17.7 us
    pallas_call x1, Pallas kernels, reorder(): pl.pallas_call(_lane_gather_kernel, out_shape=jax.ShapeDtypeStruct((rows,...  16.1 us
    all_gather x1, blocking collectives, per_device(): ordered = lax.all_gather(mine_late, 'row', axis=0, tiled=True)  11.7 us
    all_to_all x1, starting transfers between devices, per_device(): lax.all_to_all(jnp.tile(mine, (col_count, 1)), 'col', 0, 0, tiled=True)  6.32 us
    all_to_all x1, waiting for transfers between devices, per_device(): lax.all_to_all(jnp.tile(mine, (col_count, 1)), 'col', 0, 0, tiled=True)  4.62 us
    all_to_all x1, starting transfers between devices, per_device(): lax.all_to_all(send, 'row', 0, 0, tiled=True).reshape(states, window, leaf)  4.07 us
    reshape x2, local copies, waits for them, and re-layouts, per_device(): leaf_clusters = ordered.reshape(states, cluster_extent, leaf)  2.49 us
    reshape x2, local copies, waits for them, and re-layouts, per_device(): lax.all_to_all(send, 'row', 0, 0, tiled=True).reshape(states, window, leaf)  1.94 us
  transfers between devices with their start and end apart: 2, of which 1 were waited for; matrix products, arithmetic and copies ran while one was open for 14% of the time, Pallas kernels for 0%

profile of v6, /device:TPU:0, one launch (start us, length us, event | category | flops | bytes accessed | tf_op | source)
XLA Modules:
  0.0 81.4 jit_solution(1988677617784206648)
XLA Ops:
  0.0 0.0 copy-start
  0.0 16.1 %shard_map.82 = f32[4,8192]{1,0:T(4,128)} custom-call(bf16[4,8192]{1,0:T(4,128)(2,1)} %values_ref.1, s32[64,128]{1,0:T(8,128)} %bitcast.62), custom_call_target="tpu_custom_call" | custom-call | tf_op jit(solution)/shard_map/pallas_call | solution.py:64
  16.1 0.9 %convert_element_type.8 = bf16[4,8192]{1,0:T(4,128)(2,1)S(1)} convert(f32[4,8192]{1,0:T(4,128)} %shard_map.82) | non-fusion elementwise | flops 32768 | bytes 196608 | tf_op jit(solution)/shard_map/convert_element_type | solution.py:69
  17.0 0.8 tile.2
  17.8 6.3 %all-to-all-start = ((bf16[4,4,8192]{2,1,0:T(4,128)(2,1)}), bf16[4,4,8192]{2,1,0:T(4,128)(2,1)S(1)}, u32[]{:S(2)}, u32[]{:S(2)}) async-start(bf16[4,4,8192]{2,1,0:T(4,128)(2,1)} %tile.2), calls=%async_computation | async-start | bytes 524288 | tf_op jit(solution)/shard_map/all_to_all | solution.py:102
  24.1 0.7 subtract_bitcast_fusion.1
  24.8 0.7 and_bitcast_fusion.2
  25.5 0.8 subtract_bitcast_fusion
  26.2 0.7 and_bitcast_fusion
  27.0 0.1 pad_add_fusion
  27.0 0.7 and_bitcast_fusion.1
  27.7 0.7 slice_bitcast_fusion.9
  28.4 4.6 %all-to-all-done = bf16[4,4,8192]{2,1,0:T(4,128)(2,1)S(1)} async-done(((bf16[4,4,8192]{2,1,0:T(4,128)(2,1)}), bf16[4,4,8192]{2,1,0:T(4,128)(2,1)S(1)}, u32[]{:S(2)}, u32[]{:S(2)}) %all-to-all-start) | async-done | bytes 262176 | tf_op jit(solution)/shard_map/all_to_all | solution.py:102
  33.0 0.1 slice_bitcast_fusion.1
  33.1 0.2 concatenate.10
  33.4 0.8 all_to_all.17
  34.2 4.1 %all-to-all-start.1 = ((bf16[8,4,4864]{2,1,0:T(4,128)(2,1)}), bf16[8,4,4864]{2,1,0:T(4,128)(2,1)}, u32[]{:S(2)}, u32[]{:S(2)}) async-start(bf16[8,4,4864]{2,1,0:T(4,128)(2,1)} %all_to_all.17), calls=%async_computation.1 | async-start | bytes 622592 | tf_op jit(solution)/shard_map/all_to_all | solution.py:115
  38.2 11.7 %all-gather = bf16[8,4,8192]{2,1,0:T(4,128)(2,1)S(1)} all-gather(bf16[1,4,8192]{2,1,0:T(4,128)(2,1)S(1)} %bitcast.61), channel_id=1, replica_groups=mesh['row'=8,'col'=4] {'row'}, dimensions={0}, use_global_device_ids=true | all-gather | bytes 589824 | tf_op jit(solution)/shard_map/all_gather | solution.py:113
  50.0 1.2 %reshape.58 = bf16[32,32,256]{2,1,0:T(8,128)(2,1)} reshape(bf16[8,4,8192]{2,1,0:T(4,128)(2,1)S(1)} %all-gather) | data formatting | bytes 1048576 | tf_op jit(solution)/shard_map/reshape | solution.py:114
  51.1 1.3 %copy.15 = bf16[32,32,256]{2,0,1:T(8,128)(2,1)S(1)} copy(bf16[32,32,256]{2,1,0:T(8,128)(2,1)} %reshape.58) | data formatting | bytes 1048576 | tf_op jit(solution)/shard_map/reshape | solution.py:114
  52.5 0.6 gather_fusion.1
  53.1 1.4 %fusion.5 = f32[30,32,32]{2,1,0:T(8,128)S(1)} fusion(bf16[30,256,32]{1,2,0:T(8,128)(2,1)} %param.14, bf16[30,32,256]{2,1,0:T(8,128)(2,1)S(1)} %gather_fusion.1, pred[30]{0:T(512)(128)(4,1)S(1)} %get-tuple-element.11), kind=kOutput, calls=%fused_computation.9 | convolution fusion | flops 15974400 | bytes 1105950 | tf_op jit(solution)/shard_map/spk,pkr->psr/dot_general | solution.py:127
  54.5 0.2 reshape.59
  54.7 0.2 convolution_convert_fusion
  54.9 0.1 reshape.60
  55.0 0.6 gather_fusion.2
  55.6 1.4 %fusion.14 = f32[30,32,256]{2,1,0:T(8,128)S(1)} fusion(bf16[30,256,32]{1,2,0:T(8,128)(2,1)} %param.12, bf16[30,32,32]{2,1,0:T(8,128)(2,1)S(1)} %gather_fusion.2, pred[30]{0:T(512)(128)(4,1)S(1)} %and_bitcast_fusion.1), kind=kOutput, calls=%fused_computation.18 | convolution fusion | flops 15759360 | bytes 1536030 | tf_op jit(solution)/shard_map/psr,plr->psl/dot_general | solution.py:141
  56.9 0.0 all-to-all-done.1
  57.0 1.2 %reshape.57 = bf16[32,19,256]{2,1,0:T(8,128)(2,1)S(1)} reshape(bf16[8,4,4864]{2,1,0:T(4,128)(2,1)} %all-to-all-done.1) | data formatting | bytes 622592 | tf_op jit(solution)/shard_map/reshape | solution.py:115
  58.1 0.8 copy.14
  58.9 1.5 %gather_fusion = bf16[16,32,256]{2,1,0:T(8,128)(2,1)S(1)} fusion(bf16[32,19,256]{2,0,1:T(8,128)(2,1)} %copy.14, s32[1024]{0:T(1024)S(1)} %pad_clamp_fusion.2), kind=kCustom, calls=%fused_computation | custom fusion | bytes 524352 | tf_op jit(solution)/shard_map/jit(_take)/gather | solution.py:121
  60.4 0.0 copy-done
  60.4 0.7 fusion.9
  61.2 0.1 pad_maximum_fusion
  61.3 0.1 slice_bitcast_fusion
  61.4 1.5 %fusion.2 = f32[32,16,256]{2,1,0:T(8,128)S(1)} fusion(f32[32,256,46]{1,0,2:T(8,128)S(1)} %slice_bitcast_fusion, s32[46]{0:T(128)S(1)} %pad_add_fusion), kind=kOutput, calls=%fused_computation.7 | convolution fusion | flops 72352480 | bytes 2031800 | tf_op jit(solution)/shard_map/dot_general | solution.py:150
  62.9 0.1 all_to_all.19
  63.0 17.7 %all_to_all.24 = f32[4,8,4096]{2,1,0:T(8,128)S(1)} all-to-all(f32[4,8,4096]{2,1,0:T(8,128)S(1)} %all_to_all.19), channel_id=1, replica_groups=mesh['row'=8,'col'=4] {'col'}, dimensions={0} | all-to-all | bytes 1048576 | tf_op jit(solution)/shard_map/all_to_all | solution.py:157
  80.7 0.7 reduce_sum.9
  (3 shorter events, 0.0 us)
Async XLA Ops:
  0.0 60.4 %copy-start = (bf16[16,256,256]{2,1,0:T(8,128)(2,1)S(1)}, bf16[16,256,256]{2,1,0:T(8,128)(2,1)}, u32[]{:S(2)}) copy-start(bf16[16,256,256]{2,1,0:T(8,128)(2,1)} %param.10) | copy-start | bytes 6291460
  17.8 15.2 %all-to-all-start = ((bf16[4,4,8192]{2,1,0:T(4,128)(2,1)}), bf16[4,4,8192]{2,1,0:T(4,128)(2,1)S(1)}, u32[]{:S(2)}, u32[]{:S(2)}) async-start(bf16[4,4,8192]{2,1,0:T(4,128)(2,1)} %tile.2), calls=%async_computation | async-start | bytes 524288 | tf_op jit(solution)/shard_map/all_to_all | solution.py:102
  34.2 22.8 %all-to-all-start.1 = ((bf16[8,4,4864]{2,1,0:T(4,128)(2,1)}), bf16[8,4,4864]{2,1,0:T(4,128)(2,1)}, u32[]{:S(2)}, u32[]{:S(2)}) async-start(bf16[8,4,4864]{2,1,0:T(4,128)(2,1)} %all_to_all.17), calls=%async_computation.1 | async-start | bytes 622592 | tf_op jit(solution)/shard_map/all_to_all | solution.py:115

commit v7 on v6

--- a/solution.py
+++ b/solution.py
@@ -108,9 +108,8 @@
         start_t = min(max(target * row_span - home_t * cluster_extent - REACH, 0), cluster_extent - window)
         pieces.append(every_block[home_t, :, start_t * leaf:(start_t + window) * leaf])
     send = jnp.concatenate(pieces, axis=0)
-    mine_late, send = lax.optimization_barrier((mine, send))
 
-    ordered = lax.all_gather(mine_late, "row", axis=0, tiled=True)
+    ordered = lax.all_gather(mine, "row", axis=0, tiled=True)
     leaf_clusters = ordered.reshape(states, cluster_extent, leaf)
     near_window = lax.all_to_all(send, "row", 0, 0, tiled=True).reshape(states, window, leaf)
 

time: 82.1 us -> 78.5 us (0.956)
  other arithmetic: 5.33 us -> 2.8 us
  blocking collectives: 29.4 us -> 28.3 us
    all_to_all x1, waiting for transfers between devices: 0.01 us -> 5.3 us  [per_device(): lax.all_to_all(send, 'row', 0, 0, tiled=True).reshape(states, window, leaf)]
    all_to_all x1, waiting for transfers between devices: 4.62 us -> 0.01 us  [per_device(): lax.all_to_all(jnp.tile(mine, (col_count, 1)), 'col', 0, 0, tiled=True)]
    all_gather x1, blocking collectives: 11.7 us -> 9.87 us  [per_device(): ordered = lax.all_gather(mine, 'row', axis=0, tiled=True)]
    unnamed x0 -> x1, other arithmetic: none -> 0.93 us
  transfers between devices with their start and end apart: 2 -> 2, of which waited for: 1 -> 1; matrix products, arithmetic and copies ran while one was open for 14% -> 10% of each run, Pallas kernels for 0% -> 0%
where the time goes in v7:
time: 78.5 us; the launch traced here: 77.9 us
  blocking collectives  28.3 us (36%)
  Pallas kernels  16.1 us (21%)
  starting transfers between devices  10.4 us (13%)
  local copies, waits for them, and re-layouts  9.59 us (12%)
  waiting for transfers between devices  5.3 us (7%)
  matrix products  5.1 us (6%)
  other arithmetic  2.8 us (4%)
    all_to_all x1, blocking collectives, per_device(): exchanged = lax.all_to_all(partial_sum, 'col', 0, 0, tiled=True)  18.5 us
    pallas_call x1, Pallas kernels, reorder(): pl.pallas_call(_lane_gather_kernel, out_shape=jax.ShapeDtypeStruct((rows,...  16.1 us
    all_gather x1, blocking collectives, per_device(): ordered = lax.all_gather(mine, 'row', axis=0, tiled=True)  9.87 us
    all_to_all x1, starting transfers between devices, per_device(): lax.all_to_all(jnp.tile(mine, (col_count, 1)), 'col', 0, 0, tiled=True)  6.32 us
    all_to_all x1, waiting for transfers between devices, per_device(): lax.all_to_all(send, 'row', 0, 0, tiled=True).reshape(states, window, leaf)  5.3 us
    all_to_all x1, starting transfers between devices, per_device(): lax.all_to_all(send, 'row', 0, 0, tiled=True).reshape(states, window, leaf)  4.06 us
    reshape x2, local copies, waits for them, and re-layouts, per_device(): leaf_clusters = ordered.reshape(states, cluster_extent, leaf)  2.5 us
    reshape x2, local copies, waits for them, and re-layouts, per_device(): lax.all_to_all(send, 'row', 0, 0, tiled=True).reshape(states, window, leaf)  1.94 us
  transfers between devices with their start and end apart: 2, of which 1 were waited for; matrix products, arithmetic and copies ran while one was open for 10% of the time, Pallas kernels for 0%

profile of v7, /device:TPU:0, one launch (start us, length us, event | category | flops | bytes accessed | tf_op | source)
XLA Modules:
  0.0 77.9 jit_solution(10536406514061349326)
XLA Ops:
  0.0 0.0 copy-start
  0.0 0.0 copy-start.1
  0.0 0.0 copy-start.2
  0.0 0.0 copy-start.3
  0.0 16.1 %shard_map.82 = f32[4,8192]{1,0:T(4,128)} custom-call(bf16[4,8192]{1,0:T(4,128)(2,1)} %values_ref.1, s32[64,128]{1,0:T(8,128)} %bitcast.62), custom_call_target="tpu_custom_call" | custom-call | tf_op jit(solution)/shard_map/pallas_call | solution.py:64
  16.1 0.9 %convert_element_type.8 = bf16[4,8192]{1,0:T(4,128)(2,1)S(1)} convert(f32[4,8192]{1,0:T(4,128)} %shard_map.82) | non-fusion elementwise | flops 32768 | bytes 196608 | tf_op jit(solution)/shard_map/convert_element_type | solution.py:69
  17.0 0.8 tile.2
  17.8 6.3 %all-to-all-start = ((bf16[4,4,8192]{2,1,0:T(4,128)(2,1)}), bf16[4,4,8192]{2,1,0:T(4,128)(2,1)S(1)}, u32[]{:S(2)}, u32[]{:S(2)}) async-start(bf16[4,4,8192]{2,1,0:T(4,128)(2,1)} %tile.2), calls=%async_computation | async-start | bytes 524288 | tf_op jit(solution)/shard_map/all_to_all | solution.py:102
  24.1 0.9 %convert_bitcast_fusion = bf16[1,4,8192]{2,1,0:T(4,128)(2,1)S(1)} fusion(f32[4,8192]{1,0:T(4,128)} %shard_map.82), kind=kLoop, calls=%fused_computation.53 | loop fusion | flops 32768 | bytes 196608
  25.1 0.0 copy-done.1
  25.1 0.0 copy-done.2
  25.2 0.0 copy-done.3
  25.2 9.9 %all-gather = bf16[8,4,8192]{2,1,0:T(4,128)(2,1)S(1)} all-gather(bf16[1,4,8192]{2,1,0:T(4,128)(2,1)S(1)} %convert_bitcast_fusion), channel_id=1, replica_groups=mesh['row'=8,'col'=4] {'row'}, dimensions={0}, use_global_device_ids=true | all-gather | bytes 589824 | tf_op jit(solution)/shard_map/all_gather | solution.py:112
  35.1 1.2 %reshape.58 = bf16[32,32,256]{2,1,0:T(8,128)(2,1)} reshape(bf16[8,4,8192]{2,1,0:T(4,128)(2,1)S(1)} %all-gather) | data formatting | bytes 1048576 | tf_op jit(solution)/shard_map/reshape | solution.py:113
  36.3 1.3 %copy.15 = bf16[32,32,256]{2,0,1:T(8,128)(2,1)S(1)} copy(bf16[32,32,256]{2,1,0:T(8,128)(2,1)} %reshape.58) | data formatting | bytes 1048576 | tf_op jit(solution)/shard_map/reshape | solution.py:113
  37.6 0.6 gather_fusion.1
  38.2 1.4 %fusion.5 = f32[30,32,32]{2,1,0:T(8,128)S(1)} fusion(bf16[30,256,32]{1,2,0:T(8,128)(2,1)} %param.14, bf16[30,32,256]{2,1,0:T(8,128)(2,1)S(1)} %gather_fusion.1, pred[30]{0:T(512)(128)(4,1)S(1)} %get-tuple-element.7), kind=kOutput, calls=%fused_computation.9 | convolution fusion | flops 15974400 | bytes 1105950 | tf_op jit(solution)/shard_map/spk,pkr->psr/dot_general | solution.py:126
  39.6 0.2 reshape.59
  39.8 0.2 convolution_convert_fusion
  40.0 0.0 all-to-all-done
  40.0 0.1 slice_bitcast_fusion.1
  40.1 0.2 concatenate.10
  40.4 0.8 %all_to_all.17 = bf16[8,4,4864]{2,1,0:T(4,128)(2,1)} reshape(bf16[32,4864]{1,0:T(8,128)(2,1)S(1)} %concatenate.10) | data formatting | bytes 622592 | tf_op jit(solution)/shard_map/all_to_all | solution.py:114
  41.2 4.1 %all-to-all-start.1 = ((bf16[8,4,4864]{2,1,0:T(4,128)(2,1)}), bf16[8,4,4864]{2,1,0:T(4,128)(2,1)}, u32[]{:S(2)}, u32[]{:S(2)}) async-start(bf16[8,4,4864]{2,1,0:T(4,128)(2,1)} %all_to_all.17), calls=%async_computation.1 | async-start | bytes 622592 | tf_op jit(solution)/shard_map/all_to_all | solution.py:114
  45.2 0.1 pad_add_fusion
  45.3 0.1 reshape.60
  45.4 0.6 gather_fusion.2
  46.0 1.4 %fusion.14 = f32[30,32,256]{2,1,0:T(8,128)S(1)} fusion(bf16[30,256,32]{1,2,0:T(8,128)(2,1)} %param.12, bf16[30,32,32]{2,1,0:T(8,128)(2,1)S(1)} %gather_fusion.2, pred[30]{0:T(512)(128)(4,1)S(1)} %and_bitcast_fusion.1), kind=kOutput, calls=%fused_computation.18 | convolution fusion | flops 15759360 | bytes 1536030 | tf_op jit(solution)/shard_map/psr,plr->psl/dot_general | solution.py:140
  47.4 5.3 %all-to-all-done.1 = bf16[8,4,4864]{2,1,0:T(4,128)(2,1)} async-done(((bf16[8,4,4864]{2,1,0:T(4,128)(2,1)}), bf16[8,4,4864]{2,1,0:T(4,128)(2,1)}, u32[]{:S(2)}, u32[]{:S(2)}) %all-to-all-start.1) | async-done | bytes 311328 | tf_op jit(solution)/shard_map/all_to_all | solution.py:114
  52.7 1.1 %reshape.57 = bf16[32,19,256]{2,1,0:T(8,128)(2,1)S(1)} reshape(bf16[8,4,4864]{2,1,0:T(4,128)(2,1)} %all-to-all-done.1) | data formatting | bytes 622592 | tf_op jit(solution)/shard_map/reshape | solution.py:114
  53.9 0.8 %copy.14 = bf16[32,19,256]{2,0,1:T(8,128)(2,1)} copy(bf16[32,19,256]{2,1,0:T(8,128)(2,1)S(1)} %reshape.57) | data formatting | bytes 622592 | tf_op jit(solution)/shard_map/reshape | solution.py:114
  54.6 1.5 %gather_fusion = bf16[16,32,256]{2,1,0:T(8,128)(2,1)S(1)} fusion(bf16[32,19,256]{2,0,1:T(8,128)(2,1)} %copy.14, s32[1024]{0:T(1024)S(1)} %pad_clamp_fusion.2), kind=kCustom, calls=%fused_computation | custom fusion | bytes 524352 | tf_op jit(solution)/shard_map/jit(_take)/gather | solution.py:120
  56.2 0.0 copy-done
  56.2 0.7 fusion.9
  56.9 0.1 pad_maximum_fusion
  57.0 0.1 slice_bitcast_fusion
  57.1 1.5 %fusion.2 = f32[32,16,256]{2,1,0:T(8,128)S(1)} fusion(f32[32,256,46]{1,0,2:T(8,128)S(1)} %slice_bitcast_fusion, s32[46]{0:T(128)S(1)} %pad_add_fusion), kind=kOutput, calls=%fused_computation.7 | convolution fusion | flops 72352480 | bytes 2031800 | tf_op jit(solution)/shard_map/dot_general | solution.py:149
  58.6 0.1 all_to_all.19
  58.7 18.5 %all_to_all.24 = f32[4,8,4096]{2,1,0:T(8,128)S(1)} all-to-all(f32[4,8,4096]{2,1,0:T(8,128)S(1)} %all_to_all.19), channel_id=1, replica_groups=mesh['row'=8,'col'=4] {'col'}, dimensions={0} | all-to-all | bytes 1048576 | tf_op jit(solution)/shard_map/all_to_all | solution.py:156
  77.2 0.7 reduce_sum.9
  (9 shorter events, 0.1 us)
Async XLA Ops:
  0.0 56.2 %copy-start = (bf16[16,256,256]{2,1,0:T(8,128)(2,1)S(1)}, bf16[16,256,256]{2,1,0:T(8,128)(2,1)}, u32[]{:S(2)}) copy-start(bf16[16,256,256]{2,1,0:T(8,128)(2,1)} %param.10) | copy-start | bytes 6291460
  0.0 25.1 %copy-start.1 = (s32[30,2]{0,1:T(2,128)S(1)}, s32[30,2]{0,1:T(2,128)}, u32[]{:S(2)}) copy-start(s32[30,2]{0,1:T(2,128)} %param.13) | copy-start | bytes 724
  0.0 25.1 %copy-start.2 = (s32[16,2]{0,1:T(2,128)S(1)}, s32[16,2]{0,1:T(2,128)}, u32[]{:S(2)}) copy-start(s32[16,2]{0,1:T(2,128)} %param.11) | copy-start | bytes 388
  0.0 25.2 %copy-start.3 = (s32[30,2]{0,1:T(2,128)S(1)}, s32[30,2]{0,1:T(2,128)}, u32[]{:S(2)}) copy-start(s32[30,2]{0,1:T(2,128)} %param.15) | copy-start | bytes 724
  17.8 22.2 %all-to-all-start = ((bf16[4,4,8192]{2,1,0:T(4,128)(2,1)}), bf16[4,4,8192]{2,1,0:T(4,128)(2,1)S(1)}, u32[]{:S(2)}, u32[]{:S(2)}) async-start(bf16[4,4,8192]{2,1,0:T(4,128)(2,1)} %tile.2), calls=%async_computation | async-start | bytes 524288 | tf_op jit(solution)/shard_map/all_to_all | solution.py:102
  41.2 11.5 %all-to-all-start.1 = ((bf16[8,4,4864]{2,1,0:T(4,128)(2,1)}), bf16[8,4,4864]{2,1,0:T(4,128)(2,1)}, u32[]{:S(2)}, u32[]{:S(2)}) async-start(bf16[8,4,4864]{2,1,0:T(4,128)(2,1)} %all_to_all.17), calls=%async_computation.1 | async-start | bytes 622592 | tf_op jit(solution)/shard_map/all_to_all | solution.py:114

commit v8 on v7

--- a/solution.py
+++ b/solution.py
@@ -49,7 +49,7 @@
             )
 
         zeros = tuple(jnp.zeros((SUBLANES, LANES), jnp.float32) for _ in range(batch))
-        accs = lax.fori_loop(0, tiles, tile_body, zeros)
+        accs = lax.fori_loop(0, tiles, tile_body, zeros, unroll=True)
         for b in range(batch):
             for g in range(group):
                 column = pl.multiple_of(((base + b) * group + g) * LANES, LANES)

time: 78.5 us -> 70 us (0.89)
  Pallas kernels: 16.1 us -> 7.6 us
    pallas_call x1, Pallas kernels: 16.1 us -> 7.6 us  [reorder(): pl.pallas_call(_lane_gather_kernel, out_shape=jax.ShapeDtypeStruct((rows,...]
  transfers between devices with their start and end apart: 2 -> 2, of which waited for: 1 -> 1; matrix products, arithmetic and copies ran while one was open for 10% -> 12% of each run, Pallas kernels for 0% -> 0%
where the time goes in v8:
time: 70 us; the launch traced here: 69.4 us
  blocking collectives  28.3 us (40%)
  starting transfers between devices  10.4 us (15%)
  local copies, waits for them, and re-layouts  9.59 us (14%)
  Pallas kernels  7.6 us (11%)
  waiting for transfers between devices  5.3 us (8%)
  matrix products  5.1 us (7%)
  other arithmetic  2.8 us (4%)
    all_to_all x1, blocking collectives, per_device(): exchanged = lax.all_to_all(partial_sum, 'col', 0, 0, tiled=True)  18.5 us
    all_gather x1, blocking collectives, per_device(): ordered = lax.all_gather(mine, 'row', axis=0, tiled=True)  9.87 us
    pallas_call x1, Pallas kernels, reorder(): pl.pallas_call(_lane_gather_kernel, out_shape=jax.ShapeDtypeStruct((rows,...  7.6 us
    all_to_all x1, starting transfers between devices, per_device(): lax.all_to_all(jnp.tile(mine, (col_count, 1)), 'col', 0, 0, tiled=True)  6.32 us
    all_to_all x1, waiting for transfers between devices, per_device(): lax.all_to_all(send, 'row', 0, 0, tiled=True).reshape(states, window, leaf)  5.3 us
    all_to_all x1, starting transfers between devices, per_device(): lax.all_to_all(send, 'row', 0, 0, tiled=True).reshape(states, window, leaf)  4.06 us
    reshape x2, local copies, waits for them, and re-layouts, per_device(): leaf_clusters = ordered.reshape(states, cluster_extent, leaf)  2.5 us
    reshape x2, local copies, waits for them, and re-layouts, per_device(): lax.all_to_all(send, 'row', 0, 0, tiled=True).reshape(states, window, leaf)  1.94 us
  transfers between devices with their start and end apart: 2, of which 1 were waited for; matrix products, arithmetic and copies ran while one was open for 12% of the time, Pallas kernels for 0%

profile of v8, /device:TPU:0, one launch (start us, length us, event | category | flops | bytes accessed | tf_op | source)
XLA Modules:
  0.0 69.4 jit_solution(17848053382876500210)
XLA Ops:
  0.0 0.0 copy-start
  0.0 0.0 copy-start.1
  0.0 0.0 copy-start.2
  0.0 0.0 copy-start.3
  0.0 7.6 %shard_map.82 = f32[4,8192]{1,0:T(4,128)} custom-call(bf16[4,8192]{1,0:T(4,128)(2,1)} %values_ref.1, s32[64,128]{1,0:T(8,128)} %bitcast.62), custom_call_target="tpu_custom_call" | custom-call | tf_op jit(solution)/shard_map/pallas_call | solution.py:64
  7.6 0.9 %convert_element_type.8 = bf16[4,8192]{1,0:T(4,128)(2,1)S(1)} convert(f32[4,8192]{1,0:T(4,128)} %shard_map.82) | non-fusion elementwise | flops 32768 | bytes 196608 | tf_op jit(solution)/shard_map/convert_element_type | solution.py:69
  8.5 0.8 %tile.2 = bf16[4,4,8192]{2,1,0:T(4,128)(2,1)} broadcast(bf16[4,8192]{1,0:T(4,128)(2,1)S(1)} %convert_element_type.8), dimensions={1,2} | broadcast | bytes 327680 | tf_op jit(solution)/shard_map/tile | solution.py:102
  9.3 6.3 %all-to-all-start = ((bf16[4,4,8192]{2,1,0:T(4,128)(2,1)}), bf16[4,4,8192]{2,1,0:T(4,128)(2,1)S(1)}, u32[]{:S(2)}, u32[]{:S(2)}) async-start(bf16[4,4,8192]{2,1,0:T(4,128)(2,1)} %tile.2), calls=%async_computation | async-start | bytes 524288 | tf_op jit(solution)/shard_map/all_to_all | solution.py:102
  15.6 0.9 %convert_bitcast_fusion = bf16[1,4,8192]{2,1,0:T(4,128)(2,1)S(1)} fusion(f32[4,8192]{1,0:T(4,128)} %shard_map.82), kind=kLoop, calls=%fused_computation.53 | loop fusion | flops 32768 | bytes 196608
  16.6 0.0 copy-done.1
  16.7 0.0 copy-done.2
  16.7 0.0 copy-done.3
  16.7 9.9 %all-gather = bf16[8,4,8192]{2,1,0:T(4,128)(2,1)S(1)} all-gather(bf16[1,4,8192]{2,1,0:T(4,128)(2,1)S(1)} %convert_bitcast_fusion), channel_id=1, replica_groups=mesh['row'=8,'col'=4] {'row'}, dimensions={0}, use_global_device_ids=true | all-gather | bytes 589824 | tf_op jit(solution)/shard_map/all_gather | solution.py:112
  26.6 1.2 %reshape.58 = bf16[32,32,256]{2,1,0:T(8,128)(2,1)} reshape(bf16[8,4,8192]{2,1,0:T(4,128)(2,1)S(1)} %all-gather) | data formatting | bytes 1048576 | tf_op jit(solution)/shard_map/reshape | solution.py:113
  27.8 1.3 %copy.15 = bf16[32,32,256]{2,0,1:T(8,128)(2,1)S(1)} copy(bf16[32,32,256]{2,1,0:T(8,128)(2,1)} %reshape.58) | data formatting | bytes 1048576 | tf_op jit(solution)/shard_map/reshape | solution.py:113
  29.1 0.6 gather_fusion.1
  29.7 1.4 %fusion.5 = f32[30,32,32]{2,1,0:T(8,128)S(1)} fusion(bf16[30,256,32]{1,2,0:T(8,128)(2,1)} %param.14, bf16[30,32,256]{2,1,0:T(8,128)(2,1)S(1)} %gather_fusion.1, pred[30]{0:T(512)(128)(4,1)S(1)} %get-tuple-element.7), kind=kOutput, calls=%fused_computation.9 | convolution fusion | flops 15974400 | bytes 1105950 | tf_op jit(solution)/shard_map/spk,pkr->psr/dot_general | solution.py:126
  31.1 0.2 reshape.59
  31.3 0.2 convolution_convert_fusion
  31.5 0.0 all-to-all-done
  31.5 0.1 slice_bitcast_fusion.1
  31.6 0.2 concatenate.10
  31.9 0.8 %all_to_all.17 = bf16[8,4,4864]{2,1,0:T(4,128)(2,1)} reshape(bf16[32,4864]{1,0:T(8,128)(2,1)S(1)} %concatenate.10) | data formatting | bytes 622592 | tf_op jit(solution)/shard_map/all_to_all | solution.py:114
  32.7 4.1 %all-to-all-start.1 = ((bf16[8,4,4864]{2,1,0:T(4,128)(2,1)}), bf16[8,4,4864]{2,1,0:T(4,128)(2,1)}, u32[]{:S(2)}, u32[]{:S(2)}) async-start(bf16[8,4,4864]{2,1,0:T(4,128)(2,1)} %all_to_all.17), calls=%async_computation.1 | async-start | bytes 622592 | tf_op jit(solution)/shard_map/all_to_all | solution.py:114
  36.7 0.1 pad_add_fusion
  36.8 0.1 reshape.60
  36.9 0.6 gather_fusion.2
  37.5 1.4 %fusion.14 = f32[30,32,256]{2,1,0:T(8,128)S(1)} fusion(bf16[30,256,32]{1,2,0:T(8,128)(2,1)} %param.12, bf16[30,32,32]{2,1,0:T(8,128)(2,1)S(1)} %gather_fusion.2, pred[30]{0:T(512)(128)(4,1)S(1)} %and_bitcast_fusion.1), kind=kOutput, calls=%fused_computation.18 | convolution fusion | flops 15759360 | bytes 1536030 | tf_op jit(solution)/shard_map/psr,plr->psl/dot_general | solution.py:140
  38.9 5.3 %all-to-all-done.1 = bf16[8,4,4864]{2,1,0:T(4,128)(2,1)} async-done(((bf16[8,4,4864]{2,1,0:T(4,128)(2,1)}), bf16[8,4,4864]{2,1,0:T(4,128)(2,1)}, u32[]{:S(2)}, u32[]{:S(2)}) %all-to-all-start.1) | async-done | bytes 311328 | tf_op jit(solution)/shard_map/all_to_all | solution.py:114
  44.2 1.1 %reshape.57 = bf16[32,19,256]{2,1,0:T(8,128)(2,1)S(1)} reshape(bf16[8,4,4864]{2,1,0:T(4,128)(2,1)} %all-to-all-done.1) | data formatting | bytes 622592 | tf_op jit(solution)/shard_map/reshape | solution.py:114
  45.4 0.8 %copy.14 = bf16[32,19,256]{2,0,1:T(8,128)(2,1)} copy(bf16[32,19,256]{2,1,0:T(8,128)(2,1)S(1)} %reshape.57) | data formatting | bytes 622592 | tf_op jit(solution)/shard_map/reshape | solution.py:114
  46.2 1.5 %gather_fusion = bf16[16,32,256]{2,1,0:T(8,128)(2,1)S(1)} fusion(bf16[32,19,256]{2,0,1:T(8,128)(2,1)} %copy.14, s32[1024]{0:T(1024)S(1)} %pad_clamp_fusion.2), kind=kCustom, calls=%fused_computation | custom fusion | bytes 524352 | tf_op jit(solution)/shard_map/jit(_take)/gather | solution.py:120
  47.7 0.0 copy-done
  47.7 0.7 %fusion.9 = f32[16,32,256]{2,1,0:T(8,128)S(1)} fusion(bf16[16,256,256]{2,1,0:T(8,128)(2,1)S(1)} %copy-done, bf16[16,32,256]{2,1,0:T(8,128)(2,1)S(1)} %gather_fusion, pred[16]{0:T(512)(128)(4,1)S(1)} %get-tuple-element.5), kind=kOutput, calls=%fused_computation.13 | convolution fusion | flops 67239936 | bytes 2883600 | tf_op jit(solution)/shard_map/snk,nlk->nsl/dot_general | solution.py:121
  48.4 0.1 pad_maximum_fusion
  48.5 0.1 slice_bitcast_fusion
  48.6 1.5 %fusion.2 = f32[32,16,256]{2,1,0:T(8,128)S(1)} fusion(f32[32,256,46]{1,0,2:T(8,128)S(1)} %slice_bitcast_fusion, s32[46]{0:T(128)S(1)} %pad_add_fusion), kind=kOutput, calls=%fused_computation.7 | convolution fusion | flops 72352480 | bytes 2031800 | tf_op jit(solution)/shard_map/dot_general | solution.py:149
  50.1 0.1 all_to_all.19
  50.2 18.5 %all_to_all.24 = f32[4,8,4096]{2,1,0:T(8,128)S(1)} all-to-all(f32[4,8,4096]{2,1,0:T(8,128)S(1)} %all_to_all.19), channel_id=1, replica_groups=mesh['row'=8,'col'=4] {'col'}, dimensions={0} | all-to-all | bytes 1048576 | tf_op jit(solution)/shard_map/all_to_all | solution.py:156
  68.7 0.7 reduce_sum.9
  (9 shorter events, 0.1 us)
Async XLA Ops:
  0.0 47.7 %copy-start = (bf16[16,256,256]{2,1,0:T(8,128)(2,1)S(1)}, bf16[16,256,256]{2,1,0:T(8,128)(2,1)}, u32[]{:S(2)}) copy-start(bf16[16,256,256]{2,1,0:T(8,128)(2,1)} %param.10) | copy-start | bytes 6291460
  0.0 16.6 %copy-start.1 = (s32[30,2]{0,1:T(2,128)S(1)}, s32[30,2]{0,1:T(2,128)}, u32[]{:S(2)}) copy-start(s32[30,2]{0,1:T(2,128)} %param.13) | copy-start | bytes 724
  0.0 16.6 %copy-start.2 = (s32[16,2]{0,1:T(2,128)S(1)}, s32[16,2]{0,1:T(2,128)}, u32[]{:S(2)}) copy-start(s32[16,2]{0,1:T(2,128)} %param.11) | copy-start | bytes 388
  0.0 16.7 %copy-start.3 = (s32[30,2]{0,1:T(2,128)S(1)}, s32[30,2]{0,1:T(2,128)}, u32[]{:S(2)}) copy-start(s32[30,2]{0,1:T(2,128)} %param.15) | copy-start | bytes 724
  9.3 22.2 %all-to-all-start = ((bf16[4,4,8192]{2,1,0:T(4,128)(2,1)}), bf16[4,4,8192]{2,1,0:T(4,128)(2,1)S(1)}, u32[]{:S(2)}, u32[]{:S(2)}) async-start(bf16[4,4,8192]{2,1,0:T(4,128)(2,1)} %tile.2), calls=%async_computation | async-start | bytes 524288 | tf_op jit(solution)/shard_map/all_to_all | solution.py:102
  32.7 11.5 %all-to-all-start.1 = ((bf16[8,4,4864]{2,1,0:T(4,128)(2,1)}), bf16[8,4,4864]{2,1,0:T(4,128)(2,1)}, u32[]{:S(2)}, u32[]{:S(2)}) async-start(bf16[8,4,4864]{2,1,0:T(4,128)(2,1)} %all_to_all.17), calls=%async_computation.1 | async-start | bytes 622592 | tf_op jit(solution)/shard_map/all_to_all | solution.py:114

commit v9 on v8

--- a/solution.py
+++ b/solution.py
@@ -53,20 +53,21 @@
         for b in range(batch):
             for g in range(group):
                 column = pl.multiple_of(((base + b) * group + g) * LANES, LANES)
-                out_ref[:, pl.ds(column, LANES)] = accs[b][g * rows:(g + 1) * rows, :]
+                piece = accs[b][g * rows:(g + 1) * rows, :].astype(out_ref.dtype)
+                for c in range(out_ref.shape[0]):
+                    out_ref[c, :, pl.ds(column, LANES)] = piece
         return carry
 
     lax.fori_loop(0, groups // batch, group_body, 0)
 
 
-def reorder(values, order):
+def reorder(values, order, copies):
     rows, width = values.shape
-    out = pl.pallas_call(
+    return pl.pallas_call(
         _lane_gather_kernel,
-        out_shape=jax.ShapeDtypeStruct((rows, width), jnp.float32),
+        out_shape=jax.ShapeDtypeStruct((copies, rows, width), values.dtype),
         scratch_shapes=[pltpu.VMEM((SUBLANES, width), jnp.float32)],
     )(values, order.reshape(width // LANES, LANES))
-    return out.astype(values.dtype)
 
 
 def per_device(
@@ -97,11 +98,10 @@
         window = max(window, high_t - low_t)
     block_entries = 4 * BL
 
-    mine = reorder(magnetic_potential_input, node_reordering)
+    copies = reorder(magnetic_potential_input, node_reordering, col_count)
+    mine = copies[0]
 
-    every_block = lax.all_to_all(jnp.tile(mine, (col_count, 1)), "col", 0, 0, tiled=True).reshape(
-        col_count, local_states, width
-    )
+    every_block = lax.all_to_all(copies, "col", 0, 0, tiled=True)
     pieces = []
     for target in range(row_count):
         home_t = target * col_count // row_count
@@ -141,16 +141,14 @@
         "psr,plr->psl", picked, distant_row_factors, preferred_element_type=jnp.float32
     )
 
-    all_out = jnp.concatenate([near_out, far_out], axis=0)
-    all_rows = jnp.concatenate([near_rows, distant_row_factor_index[:, 0] - row_index * row_span])
-    scatter = (
-        all_rows[None, :] == jnp.arange(row_span, dtype=jnp.int32)[:, None]
-    ).astype(jnp.float32)
-    partial_sum = jnp.dot(
-        scatter,
-        all_out.reshape(all_out.shape[0], states * leaf),
-        precision=lax.Precision.HIGHEST,
-    ).reshape(row_span, states, leaf)
+    def scatter_add(pieces, targets):
+        onehot = (targets[None, :] == jnp.arange(row_span, dtype=jnp.int32)[:, None]).astype(jnp.float32)
+        return jnp.dot(
+            onehot, pieces.reshape(pieces.shape[0], states * leaf), precision=lax.Precision.HIGHEST
+        ).reshape(row_span, states, leaf)
+
+    far_sum = scatter_add(far_out, distant_row_factor_index[:, 0] - row_index * row_span)
+    partial_sum = far_sum + scatter_add(near_out, near_rows)
     partial_sum = partial_sum.transpose(1, 0, 2).reshape(states, row_span * leaf)
 
     exchanged = lax.all_to_all(partial_sum, "col", 0, 0, tiled=True)

time: 70 us -> 73.4 us (1.049)
  Pallas kernels: 7.6 us -> 4.93 us
  matrix products: 5.1 us -> 7.06 us
  other arithmetic: 2.8 us -> 4.7 us
  blocking collectives: 28.3 us -> 29.7 us
  local copies, waits for them, and re-layouts: 9.59 us -> 10.7 us
    all_gather x0 -> x1, other arithmetic: none -> 3.96 us  [per_device(): ordered = lax.all_gather(mine, 'row', axis=0, tiled=True)]
    pallas_call x1, Pallas kernels: 7.6 us -> 4.93 us  [reorder(): pl.pallas_call(_lane_gather_kernel, out_shape=jax.ShapeDtypeStruct((copie...]
    concatenate x1, local copies, waits for them, and re-layouts: 0.22 us -> 2.55 us  [per_device(): send = jnp.concatenate(pieces, axis=0)]
    reshape x2, local copies, waits for them, and re-layouts: 1.94 us -> 0.24 us  [per_device(): lax.all_to_all(send, 'row', 0, 0, tiled=True).reshape(states, window, leaf)]
    reshape x2 -> x1, local copies, waits for them, and re-layouts: 2.5 us -> 1.11 us  [per_device(): leaf_clusters = ordered.reshape(states, cluster_extent, leaf)]
    all_gather x1, blocking collectives: 9.87 us -> 11.1 us  [per_device(): ordered = lax.all_gather(mine, 'row', axis=0, tiled=True)]
    dot_general x1, local copies, waits for them, and re-layouts: 0.1 us -> 1.27 us  [scatter_add(): jnp.dot(onehot, pieces.reshape(pieces.shape[0], states * leaf), precision...]
    dot_general x1 -> x2, matrix products: 1.48 us -> 2.5 us  [scatter_add(): jnp.dot(onehot, pieces.reshape(pieces.shape[0], states * leaf), precision...]
  transfers between devices with their start and end apart: 2 -> 2, of which waited for: 1 -> 1; matrix products, arithmetic and copies ran while one was open for 12% -> 20% of each run, Pallas kernels for 0% -> 0%
where the time goes in v9:
time: 73.4 us; the launch traced here: 72.7 us
  blocking collectives  29.7 us (40%)
  local copies, waits for them, and re-layouts  10.7 us (15%)
  starting transfers between devices  9.74 us (13%)
  matrix products  7.06 us (10%)
  waiting for transfers between devices  5.56 us (8%)
  Pallas kernels  4.93 us (7%)
  other arithmetic  4.7 us (6%)
    all_to_all x1, blocking collectives, per_device(): exchanged = lax.all_to_all(partial_sum, 'col', 0, 0, tiled=True)  18.7 us
    all_gather x1, blocking collectives, per_device(): ordered = lax.all_gather(mine, 'row', axis=0, tiled=True)  11.1 us
    all_to_all x1, starting transfers between devices, per_device(): every_block = lax.all_to_all(copies, 'col', 0, 0, tiled=True)  6.32 us
    all_to_all x1, waiting for transfers between devices, per_device(): lax.all_to_all(send, 'row', 0, 0, tiled=True).reshape(states, window, leaf)  5.56 us
    pallas_call x1, Pallas kernels, reorder(): pl.pallas_call(_lane_gather_kernel, out_shape=jax.ShapeDtypeStruct((copie...  4.93 us
    all_gather x1, other arithmetic, per_device(): ordered = lax.all_gather(mine, 'row', axis=0, tiled=True)  3.96 us
    all_to_all x1, starting transfers between devices, per_device(): lax.all_to_all(send, 'row', 0, 0, tiled=True).reshape(states, window, leaf)  3.43 us
    concatenate x1, local copies, waits for them, and re-layouts, per_device(): send = jnp.concatenate(pieces, axis=0)  2.55 us
  transfers between devices with their start and end apart: 2, of which 1 were waited for; matrix products, arithmetic and copies ran while one was open for 20% of the time, Pallas kernels for 0%

profile of v9, /device:TPU:0, one launch (start us, length us, event | category | flops | bytes accessed | tf_op | source)
XLA Modules:
  0.0 72.7 jit_solution(10426908981979296136)
XLA Ops:
  0.0 0.0 copy-start
  0.0 4.9 %shard_map.82 = bf16[4,4,8192]{2,1,0:T(4,128)(2,1)} custom-call(bf16[4,8192]{1,0:T(4,128)(2,1)} %values_ref.1, s32[64,128]{1,0:T(8,128)} %bitcast.81), custom_call_target="tpu_custom_call" | custom-call | tf_op jit(solution)/shard_map/pallas_call | solution.py:66
  4.9 6.3 %all-to-all-start = ((bf16[4,4,8192]{2,1,0:T(4,128)(2,1)}), bf16[4,4,8192]{2,1,0:T(4,128)(2,1)S(1)}, u32[]{:S(2)}, u32[]{:S(2)}) async-start(bf16[4,4,8192]{2,1,0:T(4,128)(2,1)} %shard_map.82), calls=%async_computation | async-start | bytes 524288 | tf_op jit(solution)/shard_map/all_to_all | solution.py:104
  11.2 0.0 copy-start.4
  11.2 0.9 %slice.66 = bf16[1,4,8192]{2,1,0:T(4,128)(2,1)S(1)} slice(bf16[4,4,8192]{2,1,0:T(4,128)(2,1)} %shard_map.82), slice={[0:1], [0:4], [0:8192]} | slice | bytes 131072 | tf_op jit(solution)/shard_map/slice | solution.py:102
  12.1 0.1 copy.17
  12.2 11.1 %all-gather = bf16[1,32,8192]{2,0,1:T(2,128)(2,1)S(1)} all-gather(bf16[1,4,8192]{2,0,1:T(2,128)(2,1)S(1)} %copy.17), channel_id=2, replica_groups=mesh['row'=8,'col'=4] {'row'}, dimensions={1}, use_global_device_ids=true | all-gather | bytes 589824 | tf_op jit(solution)/shard_map/all_gather | solution.py:112
  23.3 4.0 %reduce.1 = bf16[32,8192]{1,0:T(8,128)(2,1)} reduce(bf16[1,32,8192]{2,0,1:T(2,128)(2,1)S(1)} %all-gather, bf16[]{:T(256)} %constant.87), dimensions={0}, to_apply=%all-gather.reduce_sub_computation | reduce | bytes 1048578 | tf_op jit(solution)/shard_map/all_gather | solution.py:112
  27.3 0.0 copy-start.2
  27.3 1.1 %copy.37 = bf16[4,32,8,256]{3,2,0,1:T(8,128)(2,1)S(1)} copy(bf16[4,32,8,256]{3,2,1,0:T(8,128)(2,1)} %bitcast.79) | data formatting | bytes 1048576 | tf_op jit(solution)/shard_map/reshape | solution.py:113
  28.4 0.0 copy-done.4
  28.4 0.6 gather_fusion
  29.0 0.0 copy-start.3
  29.0 1.4 %fusion.5 = f32[30,32,32]{2,1,0:T(8,128)S(1)} fusion(bf16[30,256,32]{1,2,0:T(8,128)(2,1)} %param.14, bf16[30,32,256]{2,1,0:T(8,128)(2,1)S(1)} %gather_fusion, pred[30]{0:T(512)(128)(4,1)S(1)} %get-tuple-element.7), kind=kOutput, calls=%fused_computation.12 | convolution fusion | flops 15974400 | bytes 1105950 | tf_op jit(solution)/shard_map/spk,pkr->psr/dot_general | solution.py:126
  30.4 0.2 reshape.63
  30.6 0.2 convolution_convert_fusion
  30.8 0.1 reshape.64
  30.9 0.0 copy-done.2
  31.0 0.6 gather_fusion.1
  31.6 2.3 %fusion.14 = f32[30,32,256]{2,1,0:T(8,128)} fusion(bf16[30,256,32]{1,2,0:T(8,128)(2,1)} %param.12, bf16[30,32,32]{2,1,0:T(8,128)(2,1)S(1)} %gather_fusion.1, pred[30]{0:T(512)(128)(4,1)S(1)} %and_bitcast_fusion.2), kind=kOutput, calls=%fused_computation.21 | convolution fusion | flops 15759360 | bytes 1536030 | tf_op jit(solution)/shard_map/psr,plr->psl/dot_general | solution.py:140
  33.9 0.0 copy-done.3
  33.9 1.3 %slice_bitcast_fusion = f32[32,256,30]{1,0,2:T(8,128)S(1)} fusion(f32[30,32,256]{2,1,0:T(8,128)} %fusion.14), kind=kLoop, calls=%fused_computation.8 | loop fusion | bytes 1966080 | tf_op jit(solution)/shard_map/dot_general | solution.py:146
  35.2 0.0 all-to-all-done
  35.2 0.7 %slice_bitcast_fusion.1 = (bf16[4,4864]{1,0:T(4,128)(2,1)S(1)}, bf16[4,4864]{1,0:T(4,128)(2,1)S(1)}, bf16[4,4864]{1,0:T(4,128)(2,1)S(1)}, bf16[4,4864]{1,0:T(4,1...) fusion(bf16[4,4,8192]{2,1,0:T(4,128)(2,1)S(1)} %all-to-all-done), kind=kLoop, calls=%fused_computation.26 | loop fusion | bytes 622592 | tf_op jit(solution)/shard_map/squeeze | solution.py:109
  36.0 2.6 %concatenate.3 = bf16[32,4864]{1,0:T(8,128)(2,1)S(1)} concatenate(bf16[4,4864]{1,0:T(4,128)(2,1)} %get-tuple-element.16, bf16[4,4864]{1,0:T(4,128)(2,1)} %get-tuple-element.15, bf16[4,4864]{1,0:T(4,128)(2,1)} %get-tuple-element.14, bf16[4,4864]{1,0:T(4,128)(2,1)} %get-tuple-element.13, bf16[4,4864]{1,0:T(4,128)(2,1)} %get-tuple-element.12, ...), dimensions={0} | concatenate | bytes 622592 | tf_op jit(solution)/shard_map/concatenate | solution.py:110
  38.5 0.8 %all_to_all.16 = bf16[8,4,4864]{2,1,0:T(4,128)(2,1)} reshape(bf16[32,4864]{1,0:T(8,128)(2,1)S(1)} %concatenate.3) | data formatting | bytes 622592 | tf_op jit(solution)/shard_map/all_to_all | solution.py:114
  39.3 3.4 %all-to-all-start.1 = ((bf16[8,4,4864]{2,1,0:T(4,128)(2,1)}), bf16[8,4,4864]{2,1,0:T(4,128)(2,1)S(1)}, u32[]{:S(2)}, u32[]{:S(2)}) async-start(bf16[8,4,4864]{2,1,0:T(4,128)(2,1)} %all_to_all.16), calls=%async_computation.1 | async-start | bytes 622592 | tf_op jit(solution)/shard_map/all_to_all | solution.py:114
  42.8 1.8 %fusion.1 = f32[16,32,256]{2,0,1:T(8,128)} fusion(f32[32,256,30]{1,0,2:T(8,128)S(1)} %slice_bitcast_fusion, s32[30]{0:T(128)S(1)} %get-tuple-element.17), kind=kOutput, calls=%fused_computation.6 | convolution fusion | flops 47186400 | bytes 1507448 | tf_op jit(solution)/shard_map/dot_general | solution.py:146
  44.6 5.6 %all-to-all-done.1 = bf16[8,4,4864]{2,1,0:T(4,128)(2,1)S(1)} async-done(((bf16[8,4,4864]{2,1,0:T(4,128)(2,1)}), bf16[8,4,4864]{2,1,0:T(4,128)(2,1)S(1)}, u32[]{:S(2)}, u32[]{:S(2)}) %all-to-all-start.1) | async-done | bytes 311328 | tf_op jit(solution)/shard_map/all_to_all | solution.py:114
  50.1 0.2 reshape.66
  50.3 0.0 copy-start.1
  50.3 0.1 copy.20
  50.4 0.6 gather_fusion.2
  51.0 0.0 copy-done
  51.0 0.7 fusion.9
  51.7 0.0 copy-done.1
  51.7 0.7 fusion
  52.4 0.9 %all_to_all.18 = f32[4,8,4096]{2,1,0:T(8,128)} reshape(f32[32,16,256]{2,1,0:T(8,128)S(1)} %fusion) | data formatting | bytes 1048576 | tf_op jit(solution)/shard_map/all_to_all | solution.py:154
  53.3 18.7 %all_to_all.23 = f32[4,8,4096]{2,1,0:T(8,128)S(1)} all-to-all(f32[4,8,4096]{2,1,0:T(8,128)} %all_to_all.18), channel_id=1, replica_groups=mesh['row'=8,'col'=4] {'col'}, dimensions={0} | all-to-all | bytes 1048576 | tf_op jit(solution)/shard_map/all_to_all | solution.py:154
  72.0 0.7 reduce_sum.9
  (9 shorter events, 0.1 us)
Async XLA Ops:
  0.0 51.0 %copy-start = (bf16[16,256,256]{2,1,0:T(8,128)(2,1)S(1)}, bf16[16,256,256]{2,1,0:T(8,128)(2,1)}, u32[]{:S(2)}) copy-start(bf16[16,256,256]{2,1,0:T(8,128)(2,1)} %param.10) | copy-start | bytes 6291460
  4.9 30.3 %all-to-all-start = ((bf16[4,4,8192]{2,1,0:T(4,128)(2,1)}), bf16[4,4,8192]{2,1,0:T(4,128)(2,1)S(1)}, u32[]{:S(2)}, u32[]{:S(2)}) async-start(bf16[4,4,8192]{2,1,0:T(4,128)(2,1)} %shard_map.82), calls=%async_computation | async-start | bytes 524288 | tf_op jit(solution)/shard_map/all_to_all | solution.py:104
  11.2 17.1 %copy-start.4 = (s32[30,2]{0,1:T(2,128)S(1)}, s32[30,2]{0,1:T(2,128)}, u32[]{:S(2)}) copy-start(s32[30,2]{0,1:T(2,128)} %param.15) | copy-start | bytes 724
  27.3 3.7 %copy-start.2 = (s32[30,2]{0,1:T(2,128)S(1)}, s32[30,2]{0,1:T(2,128)}, u32[]{:S(2)}) copy-start(s32[30,2]{0,1:T(2,128)} %param.13) | copy-start | bytes 724
  29.0 4.9 %copy-start.3 = (s32[16,2]{0,1:T(2,128)S(1)}, s32[16,2]{0,1:T(2,128)}, u32[]{:S(2)}) copy-start(s32[16,2]{0,1:T(2,128)} %param.11) | copy-start | bytes 388
  39.3 10.8 %all-to-all-start.1 = ((bf16[8,4,4864]{2,1,0:T(4,128)(2,1)}), bf16[8,4,4864]{2,1,0:T(4,128)(2,1)S(1)}, u32[]{:S(2)}, u32[]{:S(2)}) async-start(bf16[8,4,4864]{2,1,0:T(4,128)(2,1)} %all_to_all.16), calls=%async_computation.1 | async-start | bytes 622592 | tf_op jit(solution)/shard_map/all_to_all | solution.py:114
  50.3 1.4 %copy-start.1 = (f32[16,32,256]{2,0,1:T(8,128)S(1)}, f32[16,32,256]{2,0,1:T(8,128)}, u32[]{:S(2)}) copy-start(f32[16,32,256]{2,0,1:T(8,128)} %fusion.1) | copy-start | bytes 1572868

commit v10 on v8

--- a/solution.py
+++ b/solution.py
@@ -53,7 +53,7 @@
         for b in range(batch):
             for g in range(group):
                 column = pl.multiple_of(((base + b) * group + g) * LANES, LANES)
-                out_ref[:, pl.ds(column, LANES)] = accs[b][g * rows:(g + 1) * rows, :]
+                out_ref[:, pl.ds(column, LANES)] = accs[b][g * rows:(g + 1) * rows, :].astype(out_ref.dtype)
         return carry
 
     lax.fori_loop(0, groups // batch, group_body, 0)
@@ -61,12 +61,11 @@
 
 def reorder(values, order):
     rows, width = values.shape
-    out = pl.pallas_call(
+    return pl.pallas_call(
         _lane_gather_kernel,
-        out_shape=jax.ShapeDtypeStruct((rows, width), jnp.float32),
+        out_shape=jax.ShapeDtypeStruct((rows, width), values.dtype),
         scratch_shapes=[pltpu.VMEM((SUBLANES, width), jnp.float32)],
     )(values, order.reshape(width // LANES, LANES))
-    return out.astype(values.dtype)
 
 
 def per_device(

time: 70 us -> 70.7 us (1.010)
  Pallas kernels: 7.6 us -> 4.85 us
  other arithmetic: 2.8 us -> 4.4 us
  local copies, waits for them, and re-layouts: 9.59 us -> 11.1 us
    pallas_call x1, Pallas kernels: 7.6 us -> 4.85 us  [reorder(): pl.pallas_call(_lane_gather_kernel, out_shape=jax.ShapeDtypeStruct((rows,...]
    convert_element_type x1 -> x0, other arithmetic: 0.93 us -> none  [reorder(): return out.astype(values.dtype)]
    unnamed x1 -> x0, other arithmetic: 0.93 us -> none
    another operation x1, local copies, waits for them, and re-layouts: 0.78 us -> 1.61 us  [per_device(): jnp.tile(mine, (col_count, 1))]
    sub x1, other arithmetic: 0.01 us -> 0.76 us  [per_device(): distant_row_factor_index[:, 0] - row_index * row_span]
  transfers between devices with their start and end apart: 2 -> 2, of which waited for: 1 -> 1; matrix products, arithmetic and copies ran while one was open for 12% -> 16% of each run, Pallas kernels for 0% -> 0%
where the time goes in v10:
time: 70.7 us; the launch traced here: 69.9 us
  blocking collectives  28.6 us (40%)
  local copies, waits for them, and re-layouts  11.1 us (16%)
  starting transfers between devices  10.4 us (15%)
  waiting for transfers between devices  5.3 us (7%)
  matrix products  5.09 us (7%)
  Pallas kernels  4.85 us (7%)
  other arithmetic  4.4 us (6%)
    all_to_all x1, blocking collectives, per_device(): exchanged = lax.all_to_all(partial_sum, 'col', 0, 0, tiled=True)  18.5 us
    all_gather x1, blocking collectives, per_device(): ordered = lax.all_gather(mine, 'row', axis=0, tiled=True)  10.2 us
    all_to_all x1, starting transfers between devices, per_device(): lax.all_to_all(jnp.tile(mine, (col_count, 1)), 'col', 0, 0, tiled=True)  6.32 us
    all_to_all x1, waiting for transfers between devices, per_device(): lax.all_to_all(send, 'row', 0, 0, tiled=True).reshape(states, window, leaf)  5.3 us
    pallas_call x1, Pallas kernels, reorder(): pl.pallas_call(_lane_gather_kernel, out_shape=jax.ShapeDtypeStruct((rows,...  4.85 us
    all_to_all x1, starting transfers between devices, per_device(): lax.all_to_all(send, 'row', 0, 0, tiled=True).reshape(states, window, leaf)  4.06 us
    reshape x2, local copies, waits for them, and re-layouts, per_device(): leaf_clusters = ordered.reshape(states, cluster_extent, leaf)  2.49 us
    reshape x2, local copies, waits for them, and re-layouts, per_device(): lax.all_to_all(send, 'row', 0, 0, tiled=True).reshape(states, window, leaf)  1.94 us
  transfers between devices with their start and end apart: 2, of which 1 were waited for; matrix products, arithmetic and copies ran while one was open for 16% of the time, Pallas kernels for 0%

profile of v10, /device:TPU:0, one launch (start us, length us, event | category | flops | bytes accessed | tf_op | source)
XLA Modules:
  0.0 69.9 jit_solution(11584755429472558770)
XLA Ops:
  0.0 0.0 copy-start
  0.0 4.9 %shard_map.82 = bf16[4,8192]{1,0:T(4,128)(2,1)} custom-call(bf16[4,8192]{1,0:T(4,128)(2,1)} %values_ref.1, s32[64,128]{1,0:T(8,128)} %bitcast.62), custom_call_target="tpu_custom_call" | custom-call | tf_op jit(solution)/shard_map/pallas_call | solution.py:64
  4.9 1.6 %tile.2 = bf16[4,4,8192]{2,1,0:T(4,128)(2,1)} broadcast(bf16[4,8192]{1,0:T(4,128)(2,1)} %shard_map.82), dimensions={1,2} | broadcast | bytes 327680 | tf_op jit(solution)/shard_map/tile | solution.py:101
  6.5 6.3 %all-to-all-start = ((bf16[4,4,8192]{2,1,0:T(4,128)(2,1)}), bf16[4,4,8192]{2,1,0:T(4,128)(2,1)S(1)}, u32[]{:S(2)}, u32[]{:S(2)}) async-start(bf16[4,4,8192]{2,1,0:T(4,128)(2,1)} %tile.2), calls=%async_computation | async-start | bytes 524288 | tf_op jit(solution)/shard_map/all_to_all | solution.py:101
  12.8 0.7 and_bitcast_fusion.1
  13.5 0.8 %subtract_bitcast_fusion = (s32[30]{0:T(128)S(1)}, s32[30]{0:T(128)S(1)}) fusion(s32[30,2]{0,1:T(2,128)} %param.13, s32[]{:T(128)S(6)} %mul.15), kind=kLoop, calls=%fused_computation.47 | loop fusion | flops 120 | bytes 484 | tf_op jit(solution)/shard_map/sub | solution.py:144
  14.2 0.7 subtract_bitcast_fusion.1
  14.9 0.7 and_bitcast_fusion.2
  15.6 0.7 slice_bitcast_fusion.9
  16.3 0.7 and_bitcast_fusion
  17.0 10.2 %all-gather = bf16[8,4,8192]{2,1,0:T(4,128)(2,1)S(1)} all-gather(bf16[1,4,8192]{2,1,0:T(4,128)(2,1)} %bitcast.61), channel_id=1, replica_groups=mesh['row'=8,'col'=4] {'row'}, dimensions={0}, use_global_device_ids=true | all-gather | bytes 589824 | tf_op jit(solution)/shard_map/all_gather | solution.py:111
  27.1 1.2 %reshape.58 = bf16[32,32,256]{2,1,0:T(8,128)(2,1)} reshape(bf16[8,4,8192]{2,1,0:T(4,128)(2,1)S(1)} %all-gather) | data formatting | bytes 1048576 | tf_op jit(solution)/shard_map/reshape | solution.py:112
  28.3 1.3 %copy.15 = bf16[32,32,256]{2,0,1:T(8,128)(2,1)S(1)} copy(bf16[32,32,256]{2,1,0:T(8,128)(2,1)} %reshape.58) | data formatting | bytes 1048576 | tf_op jit(solution)/shard_map/reshape | solution.py:112
  29.6 0.6 gather_fusion.1
  30.2 1.4 %fusion.5 = f32[30,32,32]{2,1,0:T(8,128)S(1)} fusion(bf16[30,256,32]{1,2,0:T(8,128)(2,1)} %param.14, bf16[30,32,256]{2,1,0:T(8,128)(2,1)S(1)} %gather_fusion.1, pred[30]{0:T(512)(128)(4,1)S(1)} %get-tuple-element.7), kind=kOutput, calls=%fused_computation.9 | convolution fusion | flops 15974400 | bytes 1105950 | tf_op jit(solution)/shard_map/spk,pkr->psr/dot_general | solution.py:125
  31.6 0.2 reshape.59
  31.9 0.2 convolution_convert_fusion
  32.0 0.0 all-to-all-done
  32.0 0.1 slice_bitcast_fusion.1
  32.2 0.2 concatenate.10
  32.4 0.8 %all_to_all.17 = bf16[8,4,4864]{2,1,0:T(4,128)(2,1)} reshape(bf16[32,4864]{1,0:T(8,128)(2,1)S(1)} %concatenate.10) | data formatting | bytes 622592 | tf_op jit(solution)/shard_map/all_to_all | solution.py:113
  33.2 4.1 %all-to-all-start.1 = ((bf16[8,4,4864]{2,1,0:T(4,128)(2,1)}), bf16[8,4,4864]{2,1,0:T(4,128)(2,1)}, u32[]{:S(2)}, u32[]{:S(2)}) async-start(bf16[8,4,4864]{2,1,0:T(4,128)(2,1)} %all_to_all.17), calls=%async_computation.1 | async-start | bytes 622592 | tf_op jit(solution)/shard_map/all_to_all | solution.py:113
  37.3 0.1 pad_add_fusion
  37.3 0.1 reshape.60
  37.4 0.6 gather_fusion.2
  38.0 1.4 %fusion.14 = f32[30,32,256]{2,1,0:T(8,128)S(1)} fusion(bf16[30,256,32]{1,2,0:T(8,128)(2,1)} %param.12, bf16[30,32,32]{2,1,0:T(8,128)(2,1)S(1)} %gather_fusion.2, pred[30]{0:T(512)(128)(4,1)S(1)} %and_bitcast_fusion.1), kind=kOutput, calls=%fused_computation.18 | convolution fusion | flops 15759360 | bytes 1536030 | tf_op jit(solution)/shard_map/psr,plr->psl/dot_general | solution.py:139
  39.4 5.3 %all-to-all-done.1 = bf16[8,4,4864]{2,1,0:T(4,128)(2,1)} async-done(((bf16[8,4,4864]{2,1,0:T(4,128)(2,1)}), bf16[8,4,4864]{2,1,0:T(4,128)(2,1)}, u32[]{:S(2)}, u32[]{:S(2)}) %all-to-all-start.1) | async-done | bytes 311328 | tf_op jit(solution)/shard_map/all_to_all | solution.py:113
  44.7 1.1 %reshape.57 = bf16[32,19,256]{2,1,0:T(8,128)(2,1)S(1)} reshape(bf16[8,4,4864]{2,1,0:T(4,128)(2,1)} %all-to-all-done.1) | data formatting | bytes 622592 | tf_op jit(solution)/shard_map/reshape | solution.py:113
  45.9 0.8 %copy.14 = bf16[32,19,256]{2,0,1:T(8,128)(2,1)} copy(bf16[32,19,256]{2,1,0:T(8,128)(2,1)S(1)} %reshape.57) | data formatting | bytes 622592 | tf_op jit(solution)/shard_map/reshape | solution.py:113
  46.7 1.5 %gather_fusion = bf16[16,32,256]{2,1,0:T(8,128)(2,1)S(1)} fusion(bf16[32,19,256]{2,0,1:T(8,128)(2,1)} %copy.14, s32[1024]{0:T(1024)S(1)} %pad_clamp_fusion.2), kind=kCustom, calls=%fused_computation | custom fusion | bytes 524352 | tf_op jit(solution)/shard_map/jit(_take)/gather | solution.py:119
  48.2 0.0 copy-done
  48.2 0.7 %fusion.9 = f32[16,32,256]{2,1,0:T(8,128)S(1)} fusion(bf16[16,256,256]{2,1,0:T(8,128)(2,1)S(1)} %copy-done, bf16[16,32,256]{2,1,0:T(8,128)(2,1)S(1)} %gather_fusion, pred[16]{0:T(512)(128)(4,1)S(1)} %get-tuple-element.5), kind=kOutput, calls=%fused_computation.13 | convolution fusion | flops 67239936 | bytes 2883600 | tf_op jit(solution)/shard_map/snk,nlk->nsl/dot_general | solution.py:120
  48.9 0.1 pad_maximum_fusion
  49.1 0.1 slice_bitcast_fusion
  49.2 1.5 %fusion.2 = f32[32,16,256]{2,1,0:T(8,128)S(1)} fusion(f32[32,256,46]{1,0,2:T(8,128)S(1)} %slice_bitcast_fusion, s32[46]{0:T(128)S(1)} %pad_add_fusion), kind=kOutput, calls=%fused_computation.7 | convolution fusion | flops 72352480 | bytes 2031800 | tf_op jit(solution)/shard_map/dot_general | solution.py:148
  50.6 0.1 all_to_all.19
  50.8 18.5 %all_to_all.24 = f32[4,8,4096]{2,1,0:T(8,128)S(1)} all-to-all(f32[4,8,4096]{2,1,0:T(8,128)S(1)} %all_to_all.19), channel_id=1, replica_groups=mesh['row'=8,'col'=4] {'col'}, dimensions={0} | all-to-all | bytes 1048576 | tf_op jit(solution)/shard_map/all_to_all | solution.py:155
  69.2 0.7 reduce_sum.9
  (3 shorter events, 0.0 us)
Async XLA Ops:
  0.0 48.2 %copy-start = (bf16[16,256,256]{2,1,0:T(8,128)(2,1)S(1)}, bf16[16,256,256]{2,1,0:T(8,128)(2,1)}, u32[]{:S(2)}) copy-start(bf16[16,256,256]{2,1,0:T(8,128)(2,1)} %param.10) | copy-start | bytes 6291460
  6.5 25.6 %all-to-all-start = ((bf16[4,4,8192]{2,1,0:T(4,128)(2,1)}), bf16[4,4,8192]{2,1,0:T(4,128)(2,1)S(1)}, u32[]{:S(2)}, u32[]{:S(2)}) async-start(bf16[4,4,8192]{2,1,0:T(4,128)(2,1)} %tile.2), calls=%async_computation | async-start | bytes 524288 | tf_op jit(solution)/shard_map/all_to_all | solution.py:101
  33.2 11.5 %all-to-all-start.1 = ((bf16[8,4,4864]{2,1,0:T(4,128)(2,1)}), bf16[8,4,4864]{2,1,0:T(4,128)(2,1)}, u32[]{:S(2)}, u32[]{:S(2)}) async-start(bf16[8,4,4864]{2,1,0:T(4,128)(2,1)} %all_to_all.17), calls=%async_computation.1 | async-start | bytes 622592 | tf_op jit(solution)/shard_map/all_to_all | solution.py:113

commit v11 on v10

--- a/solution.py
+++ b/solution.py
@@ -107,8 +107,9 @@
         start_t = min(max(target * row_span - home_t * cluster_extent - REACH, 0), cluster_extent - window)
         pieces.append(every_block[home_t, :, start_t * leaf:(start_t + window) * leaf])
     send = jnp.concatenate(pieces, axis=0)
+    mine_late, send = lax.optimization_barrier((mine, send))
 
-    ordered = lax.all_gather(mine, "row", axis=0, tiled=True)
+    ordered = lax.all_gather(mine_late, "row", axis=0, tiled=True)
     leaf_clusters = ordered.reshape(states, cluster_extent, leaf)
     near_window = lax.all_to_all(send, "row", 0, 0, tiled=True).reshape(states, window, leaf)
 

time: 70.7 us -> 70.9 us (level)
  blocking collectives: 28.6 us -> 29.4 us
    all_to_all x1, waiting for transfers between devices: 5.3 us -> 0.01 us  [per_device(): lax.all_to_all(send, 'row', 0, 0, tiled=True).reshape(states, window, leaf)]
    all_to_all x1, waiting for transfers between devices: 0.01 us -> 4.62 us  [per_device(): lax.all_to_all(jnp.tile(mine, (col_count, 1)), 'col', 0, 0, tiled=True)]
    all_gather x1, blocking collectives: 10.2 us -> 11.7 us  [per_device(): ordered = lax.all_gather(mine_late, 'row', axis=0, tiled=True)]
    all_to_all x1, blocking collectives: 18.5 us -> 17.7 us  [per_device(): exchanged = lax.all_to_all(partial_sum, 'col', 0, 0, tiled=True)]
where the time goes in v11:
time: 70.9 us; the launch traced here: 70.1 us
  blocking collectives  29.4 us (41%)
  local copies, waits for them, and re-layouts  11.1 us (16%)
  starting transfers between devices  10.5 us (15%)
  matrix products  5.09 us (7%)
  Pallas kernels  4.85 us (7%)
  waiting for transfers between devices  4.62 us (7%)
  other arithmetic  4.4 us (6%)
    all_to_all x1, blocking collectives, per_device(): exchanged = lax.all_to_all(partial_sum, 'col', 0, 0, tiled=True)  17.7 us
    all_gather x1, blocking collectives, per_device(): ordered = lax.all_gather(mine_late, 'row', axis=0, tiled=True)  11.7 us
    all_to_all x1, starting transfers between devices, per_device(): lax.all_to_all(jnp.tile(mine, (col_count, 1)), 'col', 0, 0, tiled=True)  6.45 us
    pallas_call x1, Pallas kernels, reorder(): pl.pallas_call(_lane_gather_kernel, out_shape=jax.ShapeDtypeStruct((rows,...  4.85 us
    all_to_all x1, waiting for transfers between devices, per_device(): lax.all_to_all(jnp.tile(mine, (col_count, 1)), 'col', 0, 0, tiled=True)  4.62 us
    all_to_all x1, starting transfers between devices, per_device(): lax.all_to_all(send, 'row', 0, 0, tiled=True).reshape(states, window, leaf)  4.05 us
    reshape x2, local copies, waits for them, and re-layouts, per_device(): leaf_clusters = ordered.reshape(states, cluster_extent, leaf)  2.49 us
    reshape x2, local copies, waits for them, and re-layouts, per_device(): lax.all_to_all(send, 'row', 0, 0, tiled=True).reshape(states, window, leaf)  1.95 us
  transfers between devices with their start and end apart: 2, of which 1 were waited for; matrix products, arithmetic and copies ran while one was open for 16% of the time, Pallas kernels for 0%

profile of v11, /device:TPU:0, one launch (start us, length us, event | category | flops | bytes accessed | tf_op | source)
XLA Modules:
  0.0 70.1 jit_solution(3575593686480670591)
XLA Ops:
  0.0 0.0 copy-start
  0.0 4.9 %shard_map.82 = bf16[4,8192]{1,0:T(4,128)(2,1)} custom-call(bf16[4,8192]{1,0:T(4,128)(2,1)} %values_ref.1, s32[64,128]{1,0:T(8,128)} %bitcast.62), custom_call_target="tpu_custom_call" | custom-call | tf_op jit(solution)/shard_map/pallas_call | solution.py:64
  4.9 1.6 %tile.2 = bf16[4,4,8192]{2,1,0:T(4,128)(2,1)} broadcast(bf16[4,8192]{1,0:T(4,128)(2,1)} %shard_map.82), dimensions={1,2} | broadcast | bytes 327680 | tf_op jit(solution)/shard_map/tile | solution.py:101
  6.5 0.0 copy-start.1
  6.5 6.4 %all-to-all-start = ((bf16[4,4,8192]{2,1,0:T(4,128)(2,1)}), bf16[4,4,8192]{2,1,0:T(4,128)(2,1)S(1)}, u32[]{:S(2)}, u32[]{:S(2)}) async-start(bf16[4,4,8192]{2,1,0:T(4,128)(2,1)} %tile.2), calls=%async_computation | async-start | bytes 524288 | tf_op jit(solution)/shard_map/all_to_all | solution.py:101
  12.9 0.7 subtract_bitcast_fusion.1
  13.6 0.7 and_bitcast_fusion.2
  14.3 0.8 %subtract_bitcast_fusion = (s32[30]{0:T(128)S(1)}, s32[30]{0:T(128)S(1)}) fusion(s32[30,2]{0,1:T(2,128)} %param.13, s32[]{:T(128)S(6)} %mul.15), kind=kLoop, calls=%fused_computation.47 | loop fusion | flops 120 | bytes 484 | tf_op jit(solution)/shard_map/sub | solution.py:145
  15.0 0.7 and_bitcast_fusion
  15.8 0.1 pad_add_fusion
  15.8 0.7 and_bitcast_fusion.1
  16.5 0.7 slice_bitcast_fusion.9
  17.2 4.6 %all-to-all-done = bf16[4,4,8192]{2,1,0:T(4,128)(2,1)S(1)} async-done(((bf16[4,4,8192]{2,1,0:T(4,128)(2,1)}), bf16[4,4,8192]{2,1,0:T(4,128)(2,1)S(1)}, u32[]{:S(2)}, u32[]{:S(2)}) %all-to-all-start) | async-done | bytes 262176 | tf_op jit(solution)/shard_map/all_to_all | solution.py:101
  21.8 0.1 slice_bitcast_fusion.1
  21.9 0.2 concatenate.10
  22.2 0.8 %all_to_all.17 = bf16[8,4,4864]{2,1,0:T(4,128)(2,1)} reshape(bf16[32,4864]{1,0:T(8,128)(2,1)S(1)} %concatenate.10) | data formatting | bytes 622592 | tf_op jit(solution)/shard_map/all_to_all | solution.py:114
  23.0 4.1 %all-to-all-start.1 = ((bf16[8,4,4864]{2,1,0:T(4,128)(2,1)}), bf16[8,4,4864]{2,1,0:T(4,128)(2,1)}, u32[]{:S(2)}, u32[]{:S(2)}) async-start(bf16[8,4,4864]{2,1,0:T(4,128)(2,1)} %all_to_all.17), calls=%async_computation.1 | async-start | bytes 622592 | tf_op jit(solution)/shard_map/all_to_all | solution.py:114
  27.0 0.0 copy-done.1
  27.0 11.7 %all-gather = bf16[8,4,8192]{2,1,0:T(4,128)(2,1)S(1)} all-gather(bf16[1,4,8192]{2,1,0:T(4,128)(2,1)S(1)} %bitcast.61), channel_id=1, replica_groups=mesh['row'=8,'col'=4] {'row'}, dimensions={0}, use_global_device_ids=true | all-gather | bytes 589824 | tf_op jit(solution)/shard_map/all_gather | solution.py:112
  38.8 1.2 %reshape.58 = bf16[32,32,256]{2,1,0:T(8,128)(2,1)} reshape(bf16[8,4,8192]{2,1,0:T(4,128)(2,1)S(1)} %all-gather) | data formatting | bytes 1048576 | tf_op jit(solution)/shard_map/reshape | solution.py:113
  39.9 1.3 %copy.15 = bf16[32,32,256]{2,0,1:T(8,128)(2,1)S(1)} copy(bf16[32,32,256]{2,1,0:T(8,128)(2,1)} %reshape.58) | data formatting | bytes 1048576 | tf_op jit(solution)/shard_map/reshape | solution.py:113
  41.3 0.6 gather_fusion.1
  41.9 1.4 %fusion.5 = f32[30,32,32]{2,1,0:T(8,128)S(1)} fusion(bf16[30,256,32]{1,2,0:T(8,128)(2,1)} %param.14, bf16[30,32,256]{2,1,0:T(8,128)(2,1)S(1)} %gather_fusion.1, pred[30]{0:T(512)(128)(4,1)S(1)} %get-tuple-element.11), kind=kOutput, calls=%fused_computation.9 | convolution fusion | flops 15974400 | bytes 1105950 | tf_op jit(solution)/shard_map/spk,pkr->psr/dot_general | solution.py:126
  43.2 0.2 reshape.59
  43.5 0.2 convolution_convert_fusion
  43.6 0.1 reshape.60
  43.8 0.6 gather_fusion.2
  44.4 1.4 %fusion.14 = f32[30,32,256]{2,1,0:T(8,128)S(1)} fusion(bf16[30,256,32]{1,2,0:T(8,128)(2,1)} %param.12, bf16[30,32,32]{2,1,0:T(8,128)(2,1)S(1)} %gather_fusion.2, pred[30]{0:T(512)(128)(4,1)S(1)} %and_bitcast_fusion.1), kind=kOutput, calls=%fused_computation.18 | convolution fusion | flops 15759360 | bytes 1536030 | tf_op jit(solution)/shard_map/psr,plr->psl/dot_general | solution.py:140
  45.7 0.0 all-to-all-done.1
  45.7 1.2 %reshape.57 = bf16[32,19,256]{2,1,0:T(8,128)(2,1)S(1)} reshape(bf16[8,4,4864]{2,1,0:T(4,128)(2,1)} %all-to-all-done.1) | data formatting | bytes 622592 | tf_op jit(solution)/shard_map/reshape | solution.py:114
  46.9 0.8 %copy.14 = bf16[32,19,256]{2,0,1:T(8,128)(2,1)} copy(bf16[32,19,256]{2,1,0:T(8,128)(2,1)S(1)} %reshape.57) | data formatting | bytes 622592 | tf_op jit(solution)/shard_map/reshape | solution.py:114
  47.7 1.5 %gather_fusion = bf16[16,32,256]{2,1,0:T(8,128)(2,1)S(1)} fusion(bf16[32,19,256]{2,0,1:T(8,128)(2,1)} %copy.14, s32[1024]{0:T(1024)S(1)} %pad_clamp_fusion.2), kind=kCustom, calls=%fused_computation | custom fusion | bytes 524352 | tf_op jit(solution)/shard_map/jit(_take)/gather | solution.py:120
  49.2 0.0 copy-done
  49.2 0.7 %fusion.9 = f32[16,32,256]{2,1,0:T(8,128)S(1)} fusion(bf16[16,256,256]{2,1,0:T(8,128)(2,1)S(1)} %copy-done, bf16[16,32,256]{2,1,0:T(8,128)(2,1)S(1)} %gather_fusion, pred[16]{0:T(512)(128)(4,1)S(1)} %get-tuple-element.9), kind=kOutput, calls=%fused_computation.13 | convolution fusion | flops 67239936 | bytes 2883600 | tf_op jit(solution)/shard_map/snk,nlk->nsl/dot_general | solution.py:121
  49.9 0.1 pad_maximum_fusion
  50.1 0.1 slice_bitcast_fusion
  50.2 1.5 %fusion.2 = f32[32,16,256]{2,1,0:T(8,128)S(1)} fusion(f32[32,256,46]{1,0,2:T(8,128)S(1)} %slice_bitcast_fusion, s32[46]{0:T(128)S(1)} %pad_add_fusion), kind=kOutput, calls=%fused_computation.7 | convolution fusion | flops 72352480 | bytes 2031800 | tf_op jit(solution)/shard_map/dot_general | solution.py:149
  51.7 0.1 all_to_all.19
  51.8 17.7 %all_to_all.24 = f32[4,8,4096]{2,1,0:T(8,128)S(1)} all-to-all(f32[4,8,4096]{2,1,0:T(8,128)S(1)} %all_to_all.19), channel_id=1, replica_groups=mesh['row'=8,'col'=4] {'col'}, dimensions={0} | all-to-all | bytes 1048576 | tf_op jit(solution)/shard_map/all_to_all | solution.py:156
  69.5 0.7 reduce_sum.9
  (3 shorter events, 0.0 us)
Async XLA Ops:
  0.0 49.2 %copy-start = (bf16[16,256,256]{2,1,0:T(8,128)(2,1)S(1)}, bf16[16,256,256]{2,1,0:T(8,128)(2,1)}, u32[]{:S(2)}) copy-start(bf16[16,256,256]{2,1,0:T(8,128)(2,1)} %param.10) | copy-start | bytes 6291460
  6.5 20.6 %copy-start.1 = (bf16[4,8192]{1,0:T(4,128)(2,1)S(1)}, bf16[4,8192]{1,0:T(4,128)(2,1)}, u32[]{:S(2)}) copy-start(bf16[4,8192]{1,0:T(4,128)(2,1)} %shard_map.82) | copy-start | bytes 196612
  6.5 15.4 %all-to-all-start = ((bf16[4,4,8192]{2,1,0:T(4,128)(2,1)}), bf16[4,4,8192]{2,1,0:T(4,128)(2,1)S(1)}, u32[]{:S(2)}, u32[]{:S(2)}) async-start(bf16[4,4,8192]{2,1,0:T(4,128)(2,1)} %tile.2), calls=%async_computation | async-start | bytes 524288 | tf_op jit(solution)/shard_map/all_to_all | solution.py:101
  23.0 22.8 %all-to-all-start.1 = ((bf16[8,4,4864]{2,1,0:T(4,128)(2,1)}), bf16[8,4,4864]{2,1,0:T(4,128)(2,1)}, u32[]{:S(2)}, u32[]{:S(2)}) async-start(bf16[8,4,4864]{2,1,0:T(4,128)(2,1)} %all_to_all.17), calls=%async_computation.1 | async-start | bytes 622592 | tf_op jit(solution)/shard_map/all_to_all | solution.py:114

commit v12 on v8

--- a/solution.py
+++ b/solution.py
@@ -117,7 +117,10 @@
     start = jnp.clip(row_index * row_span - home * cluster_extent - REACH, 0, cluster_extent - window)
     near_cols = adjacent_cluster_pairs[:, 1] - home * cluster_extent - start
     near_rows = adjacent_cluster_pairs[:, 0] - row_index * row_span
-    near_src = jnp.take(near_window, near_cols, axis=1)
+    pick = (near_cols[:, None] == jnp.arange(window, dtype=jnp.int32)[None, :]).astype(near_window.dtype)
+    near_src = jnp.einsum("nw,swk->snk", pick, near_window, preferred_element_type=jnp.float32).astype(
+        near_window.dtype
+    )
     near_out = jnp.einsum(
         "snk,nlk->nsl", near_src, adjacent_dense_blocks, preferred_element_type=jnp.float32
     )

time: 70 us -> 66 us (0.943)
  local copies, waits for them, and re-layouts: 9.59 us -> 5.43 us
    reshape x2, local copies, waits for them, and re-layouts: 2.5 us -> 0.66 us  [per_device(): leaf_clusters = ordered.reshape(states, cluster_extent, leaf)]
    gather x1 -> x0, local copies, waits for them, and re-layouts: 1.53 us -> none  [per_device(): near_src = jnp.take(near_window, near_cols, axis=1)]
    reshape x2 -> x1, local copies, waits for them, and re-layouts: 1.94 us -> 1.15 us  [per_device(): lax.all_to_all(send, 'row', 0, 0, tiled=True).reshape(states, window, leaf)]
  transfers between devices with their start and end apart: 2 -> 2, of which waited for: 1 -> 1; matrix products, arithmetic and copies ran while one was open for 12% -> 9% of each run, Pallas kernels for 0% -> 0%
where the time goes in v12:
time: 66 us; the launch traced here: 65.5 us
  blocking collectives  28.3 us (43%)
  starting transfers between devices  10.4 us (16%)
  Pallas kernels  7.6 us (12%)
  local copies, waits for them, and re-layouts  5.43 us (8%)
  matrix products  5.37 us (8%)
  waiting for transfers between devices  5.3 us (8%)
  other arithmetic  2.79 us (4%)
    all_to_all x1, blocking collectives, per_device(): exchanged = lax.all_to_all(partial_sum, 'col', 0, 0, tiled=True)  18.5 us
    all_gather x1, blocking collectives, per_device(): ordered = lax.all_gather(mine, 'row', axis=0, tiled=True)  9.87 us
    pallas_call x1, Pallas kernels, reorder(): pl.pallas_call(_lane_gather_kernel, out_shape=jax.ShapeDtypeStruct((rows,...  7.6 us
    all_to_all x1, starting transfers between devices, per_device(): lax.all_to_all(jnp.tile(mine, (col_count, 1)), 'col', 0, 0, tiled=True)  6.32 us
    all_to_all x1, waiting for transfers between devices, per_device(): lax.all_to_all(send, 'row', 0, 0, tiled=True).reshape(states, window, leaf)  5.3 us
    all_to_all x1, starting transfers between devices, per_device(): lax.all_to_all(send, 'row', 0, 0, tiled=True).reshape(states, window, leaf)  4.06 us
    dot_general x1, matrix products, per_device(): jnp.dot(scatter, all_out.reshape(all_out.shape[0], states * leaf), precis...  1.48 us
    dot_general x1, matrix products, per_device(): jnp.einsum('spk,pkr->psr', v_src, distant_column_factors, preferred_eleme...  1.37 us
  transfers between devices with their start and end apart: 2, of which 1 were waited for; matrix products, arithmetic and copies ran while one was open for 9% of the time, Pallas kernels for 0%

profile of v12, /device:TPU:0, one launch (start us, length us, event | category | flops | bytes accessed | tf_op | source)
XLA Modules:
  0.0 65.5 jit_solution(12169195386969657526)
XLA Ops:
  0.0 0.0 copy-start
  0.0 0.0 copy-start.2
  0.0 0.0 copy-start.3
  0.0 7.6 %shard_map.82 = f32[4,8192]{1,0:T(4,128)} custom-call(bf16[4,8192]{1,0:T(4,128)(2,1)} %values_ref.1, s32[64,128]{1,0:T(8,128)} %bitcast.64), custom_call_target="tpu_custom_call" | custom-call | tf_op jit(solution)/shard_map/pallas_call | solution.py:64
  7.6 0.9 %convert_element_type.15 = bf16[4,8192]{1,0:T(4,128)(2,1)S(1)} convert(f32[4,8192]{1,0:T(4,128)} %shard_map.82) | non-fusion elementwise | flops 32768 | bytes 196608 | tf_op jit(solution)/shard_map/convert_element_type | solution.py:69
  8.5 0.8 %tile.2 = bf16[4,4,8192]{2,1,0:T(4,128)(2,1)} broadcast(bf16[4,8192]{1,0:T(4,128)(2,1)S(1)} %convert_element_type.15), dimensions={1,2} | broadcast | bytes 327680 | tf_op jit(solution)/shard_map/tile | solution.py:102
  9.3 6.3 %all-to-all-start = ((bf16[4,4,8192]{2,1,0:T(4,128)(2,1)}), bf16[4,4,8192]{2,1,0:T(4,128)(2,1)S(1)}, u32[]{:S(2)}, u32[]{:S(2)}) async-start(bf16[4,4,8192]{2,1,0:T(4,128)(2,1)} %tile.2), calls=%async_computation | async-start | bytes 524288 | tf_op jit(solution)/shard_map/all_to_all | solution.py:102
  15.6 0.0 copy-start.1
  15.6 0.9 %convert_bitcast_fusion = bf16[1,4,8192]{2,1,0:T(4,128)(2,1)S(1)} fusion(f32[4,8192]{1,0:T(4,128)} %shard_map.82), kind=kLoop, calls=%fused_computation.51 | loop fusion | flops 32768 | bytes 196608
  16.6 0.0 copy-done.2
  16.6 0.0 copy-done.3
  16.7 9.9 %all-gather = bf16[8,4,8192]{2,1,0:T(4,128)(2,1)S(1)} all-gather(bf16[1,4,8192]{2,1,0:T(4,128)(2,1)S(1)} %convert_bitcast_fusion), channel_id=1, replica_groups=mesh['row'=8,'col'=4] {'row'}, dimensions={0}, use_global_device_ids=true | all-gather | bytes 589824 | tf_op jit(solution)/shard_map/all_gather | solution.py:112
  26.6 0.4 reshape.54
  26.9 0.3 copy.14
  27.2 0.0 copy-done.1
  27.3 0.6 gather_fusion
  27.8 1.4 %fusion.6 = f32[30,32,32]{2,1,0:T(8,128)S(1)} fusion(bf16[30,256,32]{1,2,0:T(8,128)(2,1)} %param.14, bf16[30,32,256]{2,1,0:T(8,128)(2,1)S(1)} %gather_fusion, pred[30]{0:T(512)(128)(4,1)S(1)} %get-tuple-element.5), kind=kOutput, calls=%fused_computation.10 | convolution fusion | flops 15974400 | bytes 1105950 | tf_op jit(solution)/shard_map/spk,pkr->psr/dot_general | solution.py:129
  29.2 0.2 reshape.55
  29.5 0.2 convolution_convert_fusion.1
  29.7 0.0 all-to-all-done
  29.7 0.1 slice_bitcast_fusion.1
  29.8 0.2 concatenate.10
  30.0 0.8 %all_to_all.17 = bf16[8,4,4864]{2,1,0:T(4,128)(2,1)} reshape(bf16[32,4864]{1,0:T(8,128)(2,1)S(1)} %concatenate.10) | data formatting | bytes 622592 | tf_op jit(solution)/shard_map/all_to_all | solution.py:114
  30.8 4.1 %all-to-all-start.1 = ((bf16[8,4,4864]{2,1,0:T(4,128)(2,1)}), bf16[8,4,4864]{2,1,0:T(4,128)(2,1)}, u32[]{:S(2)}, u32[]{:S(2)}) async-start(bf16[8,4,4864]{2,1,0:T(4,128)(2,1)} %all_to_all.17), calls=%async_computation.1 | async-start | bytes 622592 | tf_op jit(solution)/shard_map/all_to_all | solution.py:114
  34.9 0.1 pad_add_fusion
  35.0 0.1 reshape.56
  35.1 0.6 gather_fusion.1
  35.7 1.4 %fusion.13 = f32[30,32,256]{2,1,0:T(8,128)S(1)} fusion(bf16[30,256,32]{1,2,0:T(8,128)(2,1)} %param.12, bf16[30,32,32]{2,1,0:T(8,128)(2,1)S(1)} %gather_fusion.1, pred[30]{0:T(512)(128)(4,1)S(1)} %and_bitcast_fusion.1), kind=kOutput, calls=%fused_computation.17 | convolution fusion | flops 15759360 | bytes 1536030 | tf_op jit(solution)/shard_map/psr,plr->psl/dot_general | solution.py:143
  37.0 5.3 %all-to-all-done.1 = bf16[8,4,4864]{2,1,0:T(4,128)(2,1)} async-done(((bf16[8,4,4864]{2,1,0:T(4,128)(2,1)}), bf16[8,4,4864]{2,1,0:T(4,128)(2,1)}, u32[]{:S(2)}, u32[]{:S(2)}) %all-to-all-start.1) | async-done | bytes 311328 | tf_op jit(solution)/shard_map/all_to_all | solution.py:114
  42.4 1.1 %reshape.53 = bf16[32,19,256]{2,1,0:T(8,128)(2,1)S(1)} reshape(bf16[8,4,4864]{2,1,0:T(4,128)(2,1)} %all-to-all-done.1) | data formatting | bytes 622592 | tf_op jit(solution)/shard_map/reshape | solution.py:114
  43.5 0.3 fusion.5
  43.8 0.0 copy-done
  43.8 0.7 %fusion.10 = f32[16,32,256]{2,1,0:T(8,128)S(1)} fusion(bf16[16,256,256]{2,1,0:T(8,128)(2,1)S(1)} %copy-done, bf16[32,16,256]{2,1,0:T(8,128)(2,1)S(1)} %fusion.5), kind=kOutput, calls=%fused_computation.14 | convolution fusion | flops 67108864 | bytes 2883584 | tf_op jit(solution)/shard_map/snk,nlk->nsl/dot_general | solution.py:124
  44.5 0.1 pad_maximum_fusion
  44.6 0.1 slice_bitcast_fusion
  44.7 1.5 %fusion.2 = f32[32,16,256]{2,1,0:T(8,128)S(1)} fusion(f32[32,256,46]{1,0,2:T(8,128)S(1)} %slice_bitcast_fusion, s32[46]{0:T(128)S(1)} %pad_add_fusion), kind=kOutput, calls=%fused_computation.6 | convolution fusion | flops 72352480 | bytes 2031800 | tf_op jit(solution)/shard_map/dot_general | solution.py:152
  46.2 0.1 all_to_all.19
  46.3 18.5 %all_to_all.24 = f32[4,8,4096]{2,1,0:T(8,128)S(1)} all-to-all(f32[4,8,4096]{2,1,0:T(8,128)S(1)} %all_to_all.19), channel_id=1, replica_groups=mesh['row'=8,'col'=4] {'col'}, dimensions={0} | all-to-all | bytes 1048576 | tf_op jit(solution)/shard_map/all_to_all | solution.py:159
  64.8 0.7 %reduce_sum.9 = f32[8,4096]{1,0:T(8,128)} reduce(f32[4,8,4096]{2,1,0:T(8,128)S(1)} %all_to_all.24, f32[]{:T(128)} %constant.65.clone.1), dimensions={0}, to_apply=%region_0.1 | reduce | flops 98304 | bytes 655364 | tf_op jit(solution)/shard_map/reduce_sum | solution.py:160
  (7 shorter events, 0.1 us)
Async XLA Ops:
  0.0 43.8 %copy-start = (bf16[16,256,256]{2,1,0:T(8,128)(2,1)S(1)}, bf16[16,256,256]{2,1,0:T(8,128)(2,1)}, u32[]{:S(2)}) copy-start(bf16[16,256,256]{2,1,0:T(8,128)(2,1)} %param.10) | copy-start | bytes 6291460
  0.0 16.6 %copy-start.2 = (s32[30,2]{0,1:T(2,128)S(1)}, s32[30,2]{0,1:T(2,128)}, u32[]{:S(2)}) copy-start(s32[30,2]{0,1:T(2,128)} %param.13) | copy-start | bytes 724
  0.0 16.6 %copy-start.3 = (s32[30,2]{0,1:T(2,128)S(1)}, s32[30,2]{0,1:T(2,128)}, u32[]{:S(2)}) copy-start(s32[30,2]{0,1:T(2,128)} %param.15) | copy-start | bytes 724
  9.3 20.3 %all-to-all-start = ((bf16[4,4,8192]{2,1,0:T(4,128)(2,1)}), bf16[4,4,8192]{2,1,0:T(4,128)(2,1)S(1)}, u32[]{:S(2)}, u32[]{:S(2)}) async-start(bf16[4,4,8192]{2,1,0:T(4,128)(2,1)} %tile.2), calls=%async_computation | async-start | bytes 524288 | tf_op jit(solution)/shard_map/all_to_all | solution.py:102
  15.6 11.6 %copy-start.1 = (s32[16,2]{0,1:T(2,128)S(1)}, s32[16,2]{0,1:T(2,128)}, u32[]{:S(2)}) copy-start(s32[16,2]{0,1:T(2,128)} %param.11) | copy-start | bytes 388
  30.8 11.5 %all-to-all-start.1 = ((bf16[8,4,4864]{2,1,0:T(4,128)(2,1)}), bf16[8,4,4864]{2,1,0:T(4,128)(2,1)}, u32[]{:S(2)}, u32[]{:S(2)}) async-start(bf16[8,4,4864]{2,1,0:T(4,128)(2,1)} %all_to_all.17), calls=%async_computation.1 | async-start | bytes 622592 | tf_op jit(solution)/shard_map/all_to_all | solution.py:114

commit v13 on v12

--- a/solution.py
+++ b/solution.py
@@ -125,7 +125,13 @@
         "snk,nlk->nsl", near_src, adjacent_dense_blocks, preferred_element_type=jnp.float32
     )
 
-    v_src = jnp.take(leaf_clusters, distant_column_factor_index[:, 0] - col_index * cluster_extent, axis=1)
+    v_pick = (
+        (distant_column_factor_index[:, 0] - col_index * cluster_extent)[:, None]
+        == jnp.arange(cluster_extent, dtype=jnp.int32)[None, :]
+    ).astype(leaf_clusters.dtype)
+    v_src = jnp.einsum("pc,sck->spk", v_pick, leaf_clusters, preferred_element_type=jnp.float32).astype(
+        leaf_clusters.dtype
+    )
     coeffs = jnp.einsum(
         "spk,pkr->psr", v_src, distant_column_factors, preferred_element_type=jnp.float32
     )

time: 66 us -> 65.5 us (level)
  local copies, waits for them, and re-layouts: 5.43 us -> 4.55 us
where the time goes in v13:
time: 65.5 us; the launch traced here: 65 us
  blocking collectives  28.3 us (43%)
  starting transfers between devices  10.4 us (16%)
  Pallas kernels  7.62 us (12%)
  matrix products  5.76 us (9%)
  waiting for transfers between devices  5.3 us (8%)
  local copies, waits for them, and re-layouts  4.55 us (7%)
  other arithmetic  2.8 us (4%)
    all_to_all x1, blocking collectives, per_device(): exchanged = lax.all_to_all(partial_sum, 'col', 0, 0, tiled=True)  18.5 us
    all_gather x1, blocking collectives, per_device(): ordered = lax.all_gather(mine, 'row', axis=0, tiled=True)  9.87 us
    pallas_call x1, Pallas kernels, reorder(): pl.pallas_call(_lane_gather_kernel, out_shape=jax.ShapeDtypeStruct((rows,...  7.62 us
    all_to_all x1, starting transfers between devices, per_device(): lax.all_to_all(jnp.tile(mine, (col_count, 1)), 'col', 0, 0, tiled=True)  6.32 us
    all_to_all x1, waiting for transfers between devices, per_device(): lax.all_to_all(send, 'row', 0, 0, tiled=True).reshape(states, window, leaf)  5.3 us
    all_to_all x1, starting transfers between devices, per_device(): lax.all_to_all(send, 'row', 0, 0, tiled=True).reshape(states, window, leaf)  4.06 us
    dot_general x1, matrix products, per_device(): jnp.dot(scatter, all_out.reshape(all_out.shape[0], states * leaf), precis...  1.48 us
    dot_general x1, matrix products, per_device(): jnp.einsum('spk,pkr->psr', v_src, distant_column_factors, preferred_eleme...  1.43 us
  transfers between devices with their start and end apart: 2, of which 1 were waited for; matrix products, arithmetic and copies ran while one was open for 9% of the time, Pallas kernels for 0%

profile of v13, /device:TPU:0, one launch (start us, length us, event | category | flops | bytes accessed | tf_op | source)
XLA Modules:
  0.0 65.0 jit_solution(7970224065676790525)
XLA Ops:
  0.0 0.0 copy-start
  0.0 0.0 copy-start.3
  0.0 7.6 %shard_map.82 = f32[4,8192]{1,0:T(4,128)} custom-call(bf16[4,8192]{1,0:T(4,128)(2,1)} %values_ref.1, s32[64,128]{1,0:T(8,128)} %bitcast.66), custom_call_target="tpu_custom_call" | custom-call | tf_op jit(solution)/shard_map/pallas_call | solution.py:64
  7.6 0.0 copy-start.1
  7.6 0.0 copy-start.2
  7.6 1.0 %convert_element_type.22 = bf16[4,8192]{1,0:T(4,128)(2,1)S(1)} convert(f32[4,8192]{1,0:T(4,128)} %shard_map.82) | non-fusion elementwise | flops 32768 | bytes 196608 | tf_op jit(solution)/shard_map/convert_element_type | solution.py:69
  8.6 0.8 %tile.2 = bf16[4,4,8192]{2,1,0:T(4,128)(2,1)} broadcast(bf16[4,8192]{1,0:T(4,128)(2,1)S(1)} %convert_element_type.22), dimensions={1,2} | broadcast | bytes 327680 | tf_op jit(solution)/shard_map/tile | solution.py:102
  9.4 6.3 %all-to-all-start = ((bf16[4,4,8192]{2,1,0:T(4,128)(2,1)}), bf16[4,4,8192]{2,1,0:T(4,128)(2,1)S(1)}, u32[]{:S(2)}, u32[]{:S(2)}) async-start(bf16[4,4,8192]{2,1,0:T(4,128)(2,1)} %tile.2), calls=%async_computation | async-start | bytes 524288 | tf_op jit(solution)/shard_map/all_to_all | solution.py:102
  15.7 0.9 %convert_bitcast_fusion = bf16[1,4,8192]{2,1,0:T(4,128)(2,1)S(1)} fusion(f32[4,8192]{1,0:T(4,128)} %shard_map.82), kind=kLoop, calls=%fused_computation.49 | loop fusion | flops 32768 | bytes 196608
  16.6 0.0 copy-done.3
  16.7 9.9 %all-gather = bf16[8,4,8192]{2,1,0:T(4,128)(2,1)S(1)} all-gather(bf16[1,4,8192]{2,1,0:T(4,128)(2,1)S(1)} %convert_bitcast_fusion), channel_id=1, replica_groups=mesh['row'=8,'col'=4] {'row'}, dimensions={0}, use_global_device_ids=true | all-gather | bytes 589824 | tf_op jit(solution)/shard_map/all_gather | solution.py:112
  26.5 0.4 reshape.50
  26.9 0.0 copy-done.1
  26.9 0.0 copy-done.2
  26.9 0.3 fusion.2
  27.3 1.4 %fusion.7 = f32[30,32,32]{2,1,0:T(8,128)S(1)} fusion(bf16[30,256,32]{1,2,0:T(8,128)(2,1)} %param.14, bf16[32,30,256]{2,1,0:T(8,128)(2,1)S(1)} %fusion.2), kind=kOutput, calls=%fused_computation.11 | convolution fusion | flops 15728640 | bytes 1105920 | tf_op jit(solution)/shard_map/spk,pkr->psr/dot_general | solution.py:135
  28.7 0.2 reshape.51
  29.0 0.2 convolution_convert_fusion.2
  29.2 0.0 all-to-all-done
  29.2 0.1 slice_bitcast_fusion.1
  29.3 0.2 concatenate.10
  29.5 0.8 %all_to_all.17 = bf16[8,4,4864]{2,1,0:T(4,128)(2,1)} reshape(bf16[32,4864]{1,0:T(8,128)(2,1)S(1)} %concatenate.10) | data formatting | bytes 622592 | tf_op jit(solution)/shard_map/all_to_all | solution.py:114
  30.3 4.1 %all-to-all-start.1 = ((bf16[8,4,4864]{2,1,0:T(4,128)(2,1)}), bf16[8,4,4864]{2,1,0:T(4,128)(2,1)}, u32[]{:S(2)}, u32[]{:S(2)}) async-start(bf16[8,4,4864]{2,1,0:T(4,128)(2,1)} %all_to_all.17), calls=%async_computation.1 | async-start | bytes 622592 | tf_op jit(solution)/shard_map/all_to_all | solution.py:114
  34.4 0.1 pad_add_fusion
  34.5 0.1 reshape.52
  34.6 0.6 gather_fusion
  35.2 1.4 %fusion.11 = f32[30,32,256]{2,1,0:T(8,128)S(1)} fusion(bf16[30,256,32]{1,2,0:T(8,128)(2,1)} %param.12, bf16[30,32,32]{2,1,0:T(8,128)(2,1)S(1)} %gather_fusion, pred[30]{0:T(512)(128)(4,1)S(1)} %and_bitcast_fusion), kind=kOutput, calls=%fused_computation.15 | convolution fusion | flops 15759360 | bytes 1536030 | tf_op jit(solution)/shard_map/psr,plr->psl/dot_general | solution.py:149
  36.5 5.3 %all-to-all-done.1 = bf16[8,4,4864]{2,1,0:T(4,128)(2,1)} async-done(((bf16[8,4,4864]{2,1,0:T(4,128)(2,1)}), bf16[8,4,4864]{2,1,0:T(4,128)(2,1)}, u32[]{:S(2)}, u32[]{:S(2)}) %all-to-all-start.1) | async-done | bytes 311328 | tf_op jit(solution)/shard_map/all_to_all | solution.py:114
  41.9 1.1 %reshape.49 = bf16[32,19,256]{2,1,0:T(8,128)(2,1)S(1)} reshape(bf16[8,4,4864]{2,1,0:T(4,128)(2,1)} %all-to-all-done.1) | data formatting | bytes 622592 | tf_op jit(solution)/shard_map/reshape | solution.py:114
  43.0 0.3 fusion.6
  43.3 0.0 copy-done
  43.3 0.7 %fusion.9 = f32[16,32,256]{2,1,0:T(8,128)S(1)} fusion(bf16[16,256,256]{2,1,0:T(8,128)(2,1)S(1)} %copy-done, bf16[32,16,256]{2,1,0:T(8,128)(2,1)S(1)} %fusion.6), kind=kOutput, calls=%fused_computation.13 | convolution fusion | flops 67108864 | bytes 2883584 | tf_op jit(solution)/shard_map/snk,nlk->nsl/dot_general | solution.py:124
  44.0 0.1 pad_maximum_fusion
  44.1 0.1 slice_bitcast_fusion
  44.2 1.5 %fusion.3 = f32[32,16,256]{2,1,0:T(8,128)S(1)} fusion(f32[32,256,46]{1,0,2:T(8,128)S(1)} %slice_bitcast_fusion, s32[46]{0:T(128)S(1)} %pad_add_fusion), kind=kOutput, calls=%fused_computation.7 | convolution fusion | flops 72352480 | bytes 2031800 | tf_op jit(solution)/shard_map/dot_general | solution.py:158
  45.7 0.1 all_to_all.19
  45.8 18.5 %all_to_all.24 = f32[4,8,4096]{2,1,0:T(8,128)S(1)} all-to-all(f32[4,8,4096]{2,1,0:T(8,128)S(1)} %all_to_all.19), channel_id=1, replica_groups=mesh['row'=8,'col'=4] {'col'}, dimensions={0} | all-to-all | bytes 1048576 | tf_op jit(solution)/shard_map/all_to_all | solution.py:165
  64.3 0.7 %reduce_sum.9 = f32[8,4096]{1,0:T(8,128)} reduce(f32[4,8,4096]{2,1,0:T(8,128)S(1)} %all_to_all.24, f32[]{:T(128)} %constant.52.clone.1), dimensions={0}, to_apply=%region_0.1 | reduce | flops 98304 | bytes 655364 | tf_op jit(solution)/shard_map/reduce_sum | solution.py:166
  (5 shorter events, 0.0 us)
Async XLA Ops:
  0.0 43.3 %copy-start = (bf16[16,256,256]{2,1,0:T(8,128)(2,1)S(1)}, bf16[16,256,256]{2,1,0:T(8,128)(2,1)}, u32[]{:S(2)}) copy-start(bf16[16,256,256]{2,1,0:T(8,128)(2,1)} %param.10) | copy-start | bytes 6291460
  0.0 16.6 %copy-start.3 = (s32[30,2]{0,1:T(2,128)S(1)}, s32[30,2]{0,1:T(2,128)}, u32[]{:S(2)}) copy-start(s32[30,2]{0,1:T(2,128)} %param.13) | copy-start | bytes 724
  7.6 19.3 %copy-start.1 = (s32[16,2]{0,1:T(2,128)S(1)}, s32[16,2]{0,1:T(2,128)}, u32[]{:S(2)}) copy-start(s32[16,2]{0,1:T(2,128)} %param.11) | copy-start | bytes 388
  7.6 19.3 %copy-start.2 = (s32[30,2]{0,1:T(2,128)S(1)}, s32[30,2]{0,1:T(2,128)}, u32[]{:S(2)}) copy-start(s32[30,2]{0,1:T(2,128)} %param.15) | copy-start | bytes 724
  9.4 19.8 %all-to-all-start = ((bf16[4,4,8192]{2,1,0:T(4,128)(2,1)}), bf16[4,4,8192]{2,1,0:T(4,128)(2,1)S(1)}, u32[]{:S(2)}, u32[]{:S(2)}) async-start(bf16[4,4,8192]{2,1,0:T(4,128)(2,1)} %tile.2), calls=%async_computation | async-start | bytes 524288 | tf_op jit(solution)/shard_map/all_to_all | solution.py:102
  30.3 11.5 %all-to-all-start.1 = ((bf16[8,4,4864]{2,1,0:T(4,128)(2,1)}), bf16[8,4,4864]{2,1,0:T(4,128)(2,1)}, u32[]{:S(2)}, u32[]{:S(2)}) async-start(bf16[8,4,4864]{2,1,0:T(4,128)(2,1)} %all_to_all.17), calls=%async_computation.1 | async-start | bytes 622592 | tf_op jit(solution)/shard_map/all_to_all | solution.py:114

commit v14 on v13

--- a/solution.py
+++ b/solution.py
@@ -53,7 +53,7 @@
         for b in range(batch):
             for g in range(group):
                 column = pl.multiple_of(((base + b) * group + g) * LANES, LANES)
-                out_ref[:, pl.ds(column, LANES)] = accs[b][g * rows:(g + 1) * rows, :]
+                out_ref[:, pl.ds(column, LANES)] = accs[b][g * rows:(g + 1) * rows, :].astype(out_ref.dtype)
         return carry
 
     lax.fori_loop(0, groups // batch, group_body, 0)
@@ -61,12 +61,11 @@
 
 def reorder(values, order):
     rows, width = values.shape
-    out = pl.pallas_call(
+    return pl.pallas_call(
         _lane_gather_kernel,
-        out_shape=jax.ShapeDtypeStruct((rows, width), jnp.float32),
+        out_shape=jax.ShapeDtypeStruct((rows, width), values.dtype),
         scratch_shapes=[pltpu.VMEM((SUBLANES, width), jnp.float32)],
     )(values, order.reshape(width // LANES, LANES))
-    return out.astype(values.dtype)
 
 
 def per_device(

time: 65.5 us -> 62.8 us (0.959)
  Pallas kernels: 7.62 us -> 4.85 us
  other arithmetic: 2.8 us -> 1.68 us
  local copies, waits for them, and re-layouts: 4.55 us -> 5.39 us
    pallas_call x1, Pallas kernels: 7.62 us -> 4.85 us  [reorder(): pl.pallas_call(_lane_gather_kernel, out_shape=jax.ShapeDtypeStruct((rows,...]
    convert_element_type x1 -> x0, other arithmetic: 0.95 us -> none  [reorder(): return out.astype(values.dtype)]
    unnamed x1 -> x0, other arithmetic: 0.93 us -> none
    another operation x1, local copies, waits for them, and re-layouts: 0.77 us -> 1.61 us  [per_device(): jnp.tile(mine, (col_count, 1))]
    sub x1, other arithmetic: 0.01 us -> 0.76 us  [per_device(): distant_row_factor_index[:, 0] - row_index * row_span]
where the time goes in v14:
time: 62.8 us; the launch traced here: 62.2 us
  blocking collectives  28.6 us (46%)
  starting transfers between devices  10.4 us (17%)
  matrix products  5.78 us (9%)
  local copies, waits for them, and re-layouts  5.39 us (9%)
  waiting for transfers between devices  5.3 us (8%)
  Pallas kernels  4.85 us (8%)
  other arithmetic  1.68 us (3%)
    all_to_all x1, blocking collectives, per_device(): exchanged = lax.all_to_all(partial_sum, 'col', 0, 0, tiled=True)  18.5 us
    all_gather x1, blocking collectives, per_device(): ordered = lax.all_gather(mine, 'row', axis=0, tiled=True)  10.1 us
    all_to_all x1, starting transfers between devices, per_device(): lax.all_to_all(jnp.tile(mine, (col_count, 1)), 'col', 0, 0, tiled=True)  6.32 us
    all_to_all x1, waiting for transfers between devices, per_device(): lax.all_to_all(send, 'row', 0, 0, tiled=True).reshape(states, window, leaf)  5.3 us
    pallas_call x1, Pallas kernels, reorder(): pl.pallas_call(_lane_gather_kernel, out_shape=jax.ShapeDtypeStruct((rows,...  4.85 us
    all_to_all x1, starting transfers between devices, per_device(): lax.all_to_all(send, 'row', 0, 0, tiled=True).reshape(states, window, leaf)  4.06 us
    another operation x1, local copies, waits for them, and re-layouts, per_device(): jnp.tile(mine, (col_count, 1))  1.61 us
    dot_general x1, matrix products, per_device(): jnp.dot(scatter, all_out.reshape(all_out.shape[0], states * leaf), precis...  1.48 us
  transfers between devices with their start and end apart: 2, of which 1 were waited for; matrix products, arithmetic and copies ran while one was open for 9% of the time, Pallas kernels for 0%

profile of v14, /device:TPU:0, one launch (start us, length us, event | category | flops | bytes accessed | tf_op | source)
XLA Modules:
  0.0 62.2 jit_solution(6179606537077983884)
XLA Ops:
  0.0 0.0 copy-start
  0.0 0.0 copy-start.1
  0.0 0.0 copy-start.2
  0.0 4.9 %shard_map.82 = bf16[4,8192]{1,0:T(4,128)(2,1)} custom-call(bf16[4,8192]{1,0:T(4,128)(2,1)} %values_ref.1, s32[64,128]{1,0:T(8,128)} %bitcast.66), custom_call_target="tpu_custom_call" | custom-call | tf_op jit(solution)/shard_map/pallas_call | solution.py:64
  4.9 1.6 %tile.2 = bf16[4,4,8192]{2,1,0:T(4,128)(2,1)} broadcast(bf16[4,8192]{1,0:T(4,128)(2,1)} %shard_map.82), dimensions={1,2} | broadcast | bytes 327680 | tf_op jit(solution)/shard_map/tile | solution.py:101
  6.5 6.3 %all-to-all-start = ((bf16[4,4,8192]{2,1,0:T(4,128)(2,1)}), bf16[4,4,8192]{2,1,0:T(4,128)(2,1)S(1)}, u32[]{:S(2)}, u32[]{:S(2)}) async-start(bf16[4,4,8192]{2,1,0:T(4,128)(2,1)} %tile.2), calls=%async_computation | async-start | bytes 524288 | tf_op jit(solution)/shard_map/all_to_all | solution.py:101
  12.8 0.8 %subtract_bitcast_fusion.2 = (s32[30]{0:T(128)S(1)}, s32[30]{0:T(128)S(1)}) fusion(s32[30,2]{0,1:T(2,128)} %param.13, s32[]{:T(128)S(6)} %mul.15), kind=kLoop, calls=%fused_computation.45 | loop fusion | flops 120 | bytes 484 | tf_op jit(solution)/shard_map/sub | solution.py:153
  13.6 10.1 %all-gather = bf16[8,4,8192]{2,1,0:T(4,128)(2,1)S(1)} all-gather(bf16[1,4,8192]{2,1,0:T(4,128)(2,1)} %bitcast.65), channel_id=1, replica_groups=mesh['row'=8,'col'=4] {'row'}, dimensions={0}, use_global_device_ids=true | all-gather | bytes 589824 | tf_op jit(solution)/shard_map/all_gather | solution.py:111
  23.7 0.4 reshape.50
  24.1 0.0 copy-start.3
  24.1 0.0 copy-done.1
  24.1 0.0 copy-done.2
  24.1 0.4 fusion.2
  24.5 1.4 %fusion.7 = f32[30,32,32]{2,1,0:T(8,128)S(1)} fusion(bf16[30,256,32]{1,2,0:T(8,128)(2,1)} %param.14, bf16[32,30,256]{2,1,0:T(8,128)(2,1)S(1)} %fusion.2), kind=kOutput, calls=%fused_computation.11 | convolution fusion | flops 15728640 | bytes 1105920 | tf_op jit(solution)/shard_map/spk,pkr->psr/dot_general | solution.py:134
  25.9 0.0 copy-done.3
  25.9 0.2 reshape.51
  26.2 0.2 convolution_convert_fusion.2
  26.4 0.0 all-to-all-done
  26.4 0.1 slice_bitcast_fusion.1
  26.5 0.2 concatenate.10
  26.7 0.8 %all_to_all.17 = bf16[8,4,4864]{2,1,0:T(4,128)(2,1)} reshape(bf16[32,4864]{1,0:T(8,128)(2,1)S(1)} %concatenate.10) | data formatting | bytes 622592 | tf_op jit(solution)/shard_map/all_to_all | solution.py:113
  27.5 4.1 %all-to-all-start.1 = ((bf16[8,4,4864]{2,1,0:T(4,128)(2,1)}), bf16[8,4,4864]{2,1,0:T(4,128)(2,1)}, u32[]{:S(2)}, u32[]{:S(2)}) async-start(bf16[8,4,4864]{2,1,0:T(4,128)(2,1)} %all_to_all.17), calls=%async_computation.1 | async-start | bytes 622592 | tf_op jit(solution)/shard_map/all_to_all | solution.py:113
  31.6 0.1 pad_add_fusion
  31.7 0.1 reshape.52
  31.8 0.6 gather_fusion
  32.4 1.4 %fusion.11 = f32[30,32,256]{2,1,0:T(8,128)S(1)} fusion(bf16[30,256,32]{1,2,0:T(8,128)(2,1)} %param.12, bf16[30,32,32]{2,1,0:T(8,128)(2,1)S(1)} %gather_fusion, pred[30]{0:T(512)(128)(4,1)S(1)} %and_bitcast_fusion), kind=kOutput, calls=%fused_computation.15 | convolution fusion | flops 15759360 | bytes 1536030 | tf_op jit(solution)/shard_map/psr,plr->psl/dot_general | solution.py:148
  33.8 5.3 %all-to-all-done.1 = bf16[8,4,4864]{2,1,0:T(4,128)(2,1)} async-done(((bf16[8,4,4864]{2,1,0:T(4,128)(2,1)}), bf16[8,4,4864]{2,1,0:T(4,128)(2,1)}, u32[]{:S(2)}, u32[]{:S(2)}) %all-to-all-start.1) | async-done | bytes 311328 | tf_op jit(solution)/shard_map/all_to_all | solution.py:113
  39.1 1.1 %reshape.49 = bf16[32,19,256]{2,1,0:T(8,128)(2,1)S(1)} reshape(bf16[8,4,4864]{2,1,0:T(4,128)(2,1)} %all-to-all-done.1) | data formatting | bytes 622592 | tf_op jit(solution)/shard_map/reshape | solution.py:113
  40.2 0.3 fusion.6
  40.5 0.0 copy-done
  40.5 0.7 %fusion.9 = f32[16,32,256]{2,1,0:T(8,128)S(1)} fusion(bf16[16,256,256]{2,1,0:T(8,128)(2,1)S(1)} %copy-done, bf16[32,16,256]{2,1,0:T(8,128)(2,1)S(1)} %fusion.6), kind=kOutput, calls=%fused_computation.13 | convolution fusion | flops 67108864 | bytes 2883584 | tf_op jit(solution)/shard_map/snk,nlk->nsl/dot_general | solution.py:123
  41.2 0.1 pad_maximum_fusion
  41.3 0.1 slice_bitcast_fusion
  41.4 1.5 %fusion.3 = f32[32,16,256]{2,1,0:T(8,128)S(1)} fusion(f32[32,256,46]{1,0,2:T(8,128)S(1)} %slice_bitcast_fusion, s32[46]{0:T(128)S(1)} %pad_add_fusion), kind=kOutput, calls=%fused_computation.7 | convolution fusion | flops 72352480 | bytes 2031800 | tf_op jit(solution)/shard_map/dot_general | solution.py:157
  42.9 0.1 all_to_all.19
  43.0 18.5 %all_to_all.24 = f32[4,8,4096]{2,1,0:T(8,128)S(1)} all-to-all(f32[4,8,4096]{2,1,0:T(8,128)S(1)} %all_to_all.19), channel_id=1, replica_groups=mesh['row'=8,'col'=4] {'col'}, dimensions={0} | all-to-all | bytes 1048576 | tf_op jit(solution)/shard_map/all_to_all | solution.py:164
  61.5 0.7 %reduce_sum.9 = f32[8,4096]{1,0:T(8,128)} reduce(f32[4,8,4096]{2,1,0:T(8,128)S(1)} %all_to_all.24, f32[]{:T(128)} %constant.52.clone.1), dimensions={0}, to_apply=%region_0.1 | reduce | flops 98304 | bytes 655364 | tf_op jit(solution)/shard_map/reduce_sum | solution.py:165
  (4 shorter events, 0.0 us)
Async XLA Ops:
  0.0 40.5 %copy-start = (bf16[16,256,256]{2,1,0:T(8,128)(2,1)S(1)}, bf16[16,256,256]{2,1,0:T(8,128)(2,1)}, u32[]{:S(2)}) copy-start(bf16[16,256,256]{2,1,0:T(8,128)(2,1)} %param.10) | copy-start | bytes 6291460
  0.0 24.1 %copy-start.1 = (s32[16,2]{0,1:T(2,128)S(1)}, s32[16,2]{0,1:T(2,128)}, u32[]{:S(2)}) copy-start(s32[16,2]{0,1:T(2,128)} %param.11) | copy-start | bytes 388
  0.0 24.1 %copy-start.2 = (s32[30,2]{0,1:T(2,128)S(1)}, s32[30,2]{0,1:T(2,128)}, u32[]{:S(2)}) copy-start(s32[30,2]{0,1:T(2,128)} %param.15) | copy-start | bytes 724
  6.5 19.9 %all-to-all-start = ((bf16[4,4,8192]{2,1,0:T(4,128)(2,1)}), bf16[4,4,8192]{2,1,0:T(4,128)(2,1)S(1)}, u32[]{:S(2)}, u32[]{:S(2)}) async-start(bf16[4,4,8192]{2,1,0:T(4,128)(2,1)} %tile.2), calls=%async_computation | async-start | bytes 524288 | tf_op jit(solution)/shard_map/all_to_all | solution.py:101
  24.1 1.9 %copy-start.3 = (s32[30,2]{0,1:T(2,128)S(1)}, s32[30,2]{0,1:T(2,128)}, u32[]{:S(2)}) copy-start(s32[30,2]{0,1:T(2,128)} %param.13) | copy-start | bytes 724
  27.5 11.5 %all-to-all-start.1 = ((bf16[8,4,4864]{2,1,0:T(4,128)(2,1)}), bf16[8,4,4864]{2,1,0:T(4,128)(2,1)}, u32[]{:S(2)}, u32[]{:S(2)}) async-start(bf16[8,4,4864]{2,1,0:T(4,128)(2,1)} %all_to_all.17), calls=%async_computation.1 | async-start | bytes 622592 | tf_op jit(solution)/shard_map/all_to_all | solution.py:113

commit v15 on v14

--- a/solution.py
+++ b/solution.py
@@ -12,7 +12,7 @@
 BATCH = 16
 
 
-def _lane_gather_kernel(values_ref, order_ref, out_ref, doubled_ref):
+def _lane_gather_kernel(values_ref, order_ref, out_ref, copies_ref, doubled_ref):
     rows, width = values_ref.shape
     group = SUBLANES // rows
     tiles = width // LANES
@@ -53,17 +53,23 @@
         for b in range(batch):
             for g in range(group):
                 column = pl.multiple_of(((base + b) * group + g) * LANES, LANES)
-                out_ref[:, pl.ds(column, LANES)] = accs[b][g * rows:(g + 1) * rows, :].astype(out_ref.dtype)
+                piece = accs[b][g * rows:(g + 1) * rows, :].astype(out_ref.dtype)
+                out_ref[:, pl.ds(column, LANES)] = piece
+                for c in range(copies_ref.shape[0]):
+                    copies_ref[c, :, pl.ds(column, LANES)] = piece
         return carry
 
     lax.fori_loop(0, groups // batch, group_body, 0)
 
 
-def reorder(values, order):
+def reorder(values, order, copies):
     rows, width = values.shape
     return pl.pallas_call(
         _lane_gather_kernel,
-        out_shape=jax.ShapeDtypeStruct((rows, width), values.dtype),
+        out_shape=(
+            jax.ShapeDtypeStruct((rows, width), values.dtype),
+            jax.ShapeDtypeStruct((copies, rows, width), values.dtype),
+        ),
         scratch_shapes=[pltpu.VMEM((SUBLANES, width), jnp.float32)],
     )(values, order.reshape(width // LANES, LANES))
 
@@ -96,11 +102,9 @@
         window = max(window, high_t - low_t)
     block_entries = 4 * BL
 
-    mine = reorder(magnetic_potential_input, node_reordering)
+    mine, stacked = reorder(magnetic_potential_input, node_reordering, col_count)
 
-    every_block = lax.all_to_all(jnp.tile(mine, (col_count, 1)), "col", 0, 0, tiled=True).reshape(
-        col_count, local_states, width
-    )
+    every_block = lax.all_to_all(stacked, "col", 0, 0, tiled=True)
     pieces = []
     for target in range(row_count):
         home_t = target * col_count // row_count

time: 62.8 us -> 61.2 us (0.975)
  local copies, waits for them, and re-layouts: 5.39 us -> 3.78 us
    another operation x1 -> x0, local copies, waits for them, and re-layouts: 1.61 us -> none  [per_device(): jnp.tile(mine, (col_count, 1))]
where the time goes in v15:
time: 61.2 us; the launch traced here: 60.7 us
  blocking collectives  28.6 us (47%)
  starting transfers between devices  10.4 us (17%)
  matrix products  5.77 us (9%)
  waiting for transfers between devices  5.3 us (9%)
  Pallas kernels  4.96 us (8%)
  local copies, waits for them, and re-layouts  3.78 us (6%)
  other arithmetic  1.68 us (3%)
    all_to_all x1, blocking collectives, per_device(): exchanged = lax.all_to_all(partial_sum, 'col', 0, 0, tiled=True)  18.5 us
    all_gather x1, blocking collectives, per_device(): ordered = lax.all_gather(mine, 'row', axis=0, tiled=True)  10.1 us
    all_to_all x1, starting transfers between devices, per_device(): every_block = lax.all_to_all(stacked, 'col', 0, 0, tiled=True)  6.32 us
    all_to_all x1, waiting for transfers between devices, per_device(): lax.all_to_all(send, 'row', 0, 0, tiled=True).reshape(states, window, leaf)  5.3 us
    pallas_call x1, Pallas kernels, reorder(): pl.pallas_call(_lane_gather_kernel, out_shape=(jax.ShapeDtypeStruct((rows...  4.96 us
    all_to_all x1, starting transfers between devices, per_device(): lax.all_to_all(send, 'row', 0, 0, tiled=True).reshape(states, window, leaf)  4.07 us
    dot_general x1, matrix products, per_device(): jnp.dot(scatter, all_out.reshape(all_out.shape[0], states * leaf), precis...  1.48 us
    dot_general x1, matrix products, per_device(): jnp.einsum('spk,pkr->psr', v_src, distant_column_factors, preferred_eleme...  1.43 us
  transfers between devices with their start and end apart: 2, of which 1 were waited for; matrix products, arithmetic and copies ran while one was open for 9% of the time, Pallas kernels for 0%

profile of v15, /device:TPU:0, one launch (start us, length us, event | category | flops | bytes accessed | tf_op | source)
XLA Modules:
  0.0 60.7 jit_solution(13879541098977284622)
XLA Ops:
  0.0 0.0 copy-start
  0.0 0.0 copy-start.1
  0.0 0.0 copy-start.2
  0.0 5.0 %shard_map.82 = (bf16[4,8192]{1,0:T(4,128)(2,1)}, bf16[4,4,8192]{2,1,0:T(4,128)(2,1)}) custom-call(bf16[4,8192]{1,0:T(4,128)(2,1)} %values_ref.1, s32[64,128]{1,0:T(8,128)} %bitcast.66), custom_call_target="tpu_custom_call" | custom-call | tf_op jit(solution)/shard_map/pallas_call | solution.py:67
  5.0 6.3 %all-to-all-start = ((bf16[4,4,8192]{2,1,0:T(4,128)(2,1)}), bf16[4,4,8192]{2,1,0:T(4,128)(2,1)S(1)}, u32[]{:S(2)}, u32[]{:S(2)}) async-start(bf16[4,4,8192]{2,1,0:T(4,128)(2,1)} %get-tuple-element.7), calls=%async_computation | async-start | bytes 524288 | tf_op jit(solution)/shard_map/all_to_all | solution.py:107
  11.3 0.8 %subtract_bitcast_fusion.2 = (s32[30]{0:T(128)S(1)}, s32[30]{0:T(128)S(1)}) fusion(s32[30,2]{0,1:T(2,128)} %param.13, s32[]{:T(128)S(6)} %mul.15), kind=kLoop, calls=%fused_computation.45 | loop fusion | flops 120 | bytes 484 | tf_op jit(solution)/shard_map/sub | solution.py:157
  12.0 10.1 %all-gather = bf16[8,4,8192]{2,1,0:T(4,128)(2,1)S(1)} all-gather(bf16[1,4,8192]{2,1,0:T(4,128)(2,1)} %bitcast.65), channel_id=1, replica_groups=mesh['row'=8,'col'=4] {'row'}, dimensions={0}, use_global_device_ids=true | all-gather | bytes 589824 | tf_op jit(solution)/shard_map/all_gather | solution.py:115
  22.2 0.4 reshape.41
  22.6 0.0 copy-start.3
  22.6 0.0 copy-done.1
  22.6 0.0 copy-done.2
  22.6 0.3 fusion.2
  23.0 1.4 %fusion.7 = f32[30,32,32]{2,1,0:T(8,128)S(1)} fusion(bf16[30,256,32]{1,2,0:T(8,128)(2,1)} %param.14, bf16[32,30,256]{2,1,0:T(8,128)(2,1)S(1)} %fusion.2), kind=kOutput, calls=%fused_computation.11 | convolution fusion | flops 15728640 | bytes 1105920 | tf_op jit(solution)/shard_map/spk,pkr->psr/dot_general | solution.py:138
  24.4 0.0 copy-done.3
  24.4 0.2 reshape.42
  24.7 0.2 convolution_convert_fusion.2
  24.8 0.0 all-to-all-done
  24.9 0.1 slice_bitcast_fusion.1
  25.0 0.2 concatenate.10
  25.2 0.8 %all_to_all.16 = bf16[8,4,4864]{2,1,0:T(4,128)(2,1)} reshape(bf16[32,4864]{1,0:T(8,128)(2,1)S(1)} %concatenate.10) | data formatting | bytes 622592 | tf_op jit(solution)/shard_map/all_to_all | solution.py:117
  26.0 4.1 %all-to-all-start.1 = ((bf16[8,4,4864]{2,1,0:T(4,128)(2,1)}), bf16[8,4,4864]{2,1,0:T(4,128)(2,1)}, u32[]{:S(2)}, u32[]{:S(2)}) async-start(bf16[8,4,4864]{2,1,0:T(4,128)(2,1)} %all_to_all.16), calls=%async_computation.1 | async-start | bytes 622592 | tf_op jit(solution)/shard_map/all_to_all | solution.py:117
  30.1 0.1 pad_add_fusion
  30.2 0.1 reshape.43
  30.3 0.6 gather_fusion
  30.9 1.4 %fusion.11 = f32[30,32,256]{2,1,0:T(8,128)S(1)} fusion(bf16[30,256,32]{1,2,0:T(8,128)(2,1)} %param.12, bf16[30,32,32]{2,1,0:T(8,128)(2,1)S(1)} %gather_fusion, pred[30]{0:T(512)(128)(4,1)S(1)} %and_bitcast_fusion), kind=kOutput, calls=%fused_computation.15 | convolution fusion | flops 15759360 | bytes 1536030 | tf_op jit(solution)/shard_map/psr,plr->psl/dot_general | solution.py:152
  32.2 5.3 %all-to-all-done.1 = bf16[8,4,4864]{2,1,0:T(4,128)(2,1)} async-done(((bf16[8,4,4864]{2,1,0:T(4,128)(2,1)}), bf16[8,4,4864]{2,1,0:T(4,128)(2,1)}, u32[]{:S(2)}, u32[]{:S(2)}) %all-to-all-start.1) | async-done | bytes 311328 | tf_op jit(solution)/shard_map/all_to_all | solution.py:117
  37.5 1.1 %reshape.40 = bf16[32,19,256]{2,1,0:T(8,128)(2,1)S(1)} reshape(bf16[8,4,4864]{2,1,0:T(4,128)(2,1)} %all-to-all-done.1) | data formatting | bytes 622592 | tf_op jit(solution)/shard_map/reshape | solution.py:117
  38.7 0.3 fusion.6
  39.0 0.0 copy-done
  39.0 0.7 %fusion.9 = f32[16,32,256]{2,1,0:T(8,128)S(1)} fusion(bf16[16,256,256]{2,1,0:T(8,128)(2,1)S(1)} %copy-done, bf16[32,16,256]{2,1,0:T(8,128)(2,1)S(1)} %fusion.6), kind=kOutput, calls=%fused_computation.13 | convolution fusion | flops 67108864 | bytes 2883584 | tf_op jit(solution)/shard_map/snk,nlk->nsl/dot_general | solution.py:127
  39.7 0.1 pad_maximum_fusion
  39.8 0.1 slice_bitcast_fusion
  39.9 1.5 %fusion.3 = f32[32,16,256]{2,1,0:T(8,128)S(1)} fusion(f32[32,256,46]{1,0,2:T(8,128)S(1)} %slice_bitcast_fusion, s32[46]{0:T(128)S(1)} %pad_add_fusion), kind=kOutput, calls=%fused_computation.7 | convolution fusion | flops 72352480 | bytes 2031800 | tf_op jit(solution)/shard_map/dot_general | solution.py:161
  41.4 0.1 all_to_all.18
  41.5 18.5 %all_to_all.23 = f32[4,8,4096]{2,1,0:T(8,128)S(1)} all-to-all(f32[4,8,4096]{2,1,0:T(8,128)S(1)} %all_to_all.18), channel_id=1, replica_groups=mesh['row'=8,'col'=4] {'col'}, dimensions={0} | all-to-all | bytes 1048576 | tf_op jit(solution)/shard_map/all_to_all | solution.py:168
  60.0 0.7 %reduce_sum.9 = f32[8,4096]{1,0:T(8,128)} reduce(f32[4,8,4096]{2,1,0:T(8,128)S(1)} %all_to_all.23, f32[]{:T(128)} %constant.52.clone.1), dimensions={0}, to_apply=%region_0.1 | reduce | flops 98304 | bytes 655364 | tf_op jit(solution)/shard_map/reduce_sum | solution.py:169
  (4 shorter events, 0.0 us)
Async XLA Ops:
  0.0 39.0 %copy-start = (bf16[16,256,256]{2,1,0:T(8,128)(2,1)S(1)}, bf16[16,256,256]{2,1,0:T(8,128)(2,1)}, u32[]{:S(2)}) copy-start(bf16[16,256,256]{2,1,0:T(8,128)(2,1)} %param.10) | copy-start | bytes 6291460
  0.0 22.6 %copy-start.1 = (s32[16,2]{0,1:T(2,128)S(1)}, s32[16,2]{0,1:T(2,128)}, u32[]{:S(2)}) copy-start(s32[16,2]{0,1:T(2,128)} %param.11) | copy-start | bytes 388
  0.0 22.6 %copy-start.2 = (s32[30,2]{0,1:T(2,128)S(1)}, s32[30,2]{0,1:T(2,128)}, u32[]{:S(2)}) copy-start(s32[30,2]{0,1:T(2,128)} %param.15) | copy-start | bytes 724
  5.0 19.9 %all-to-all-start = ((bf16[4,4,8192]{2,1,0:T(4,128)(2,1)}), bf16[4,4,8192]{2,1,0:T(4,128)(2,1)S(1)}, u32[]{:S(2)}, u32[]{:S(2)}) async-start(bf16[4,4,8192]{2,1,0:T(4,128)(2,1)} %get-tuple-element.7), calls=%async_computation | async-start | bytes 524288 | tf_op jit(solution)/shard_map/all_to_all | solution.py:107
  22.6 1.9 %copy-start.3 = (s32[30,2]{0,1:T(2,128)S(1)}, s32[30,2]{0,1:T(2,128)}, u32[]{:S(2)}) copy-start(s32[30,2]{0,1:T(2,128)} %param.13) | copy-start | bytes 724
  26.0 11.6 %all-to-all-start.1 = ((bf16[8,4,4864]{2,1,0:T(4,128)(2,1)}), bf16[8,4,4864]{2,1,0:T(4,128)(2,1)}, u32[]{:S(2)}, u32[]{:S(2)}) async-start(bf16[8,4,4864]{2,1,0:T(4,128)(2,1)} %all_to_all.16), calls=%async_computation.1 | async-start | bytes 622592 | tf_op jit(solution)/shard_map/all_to_all | solution.py:117

commit v16 on v15

--- a/solution.py
+++ b/solution.py
@@ -153,16 +153,14 @@
         "psr,plr->psl", picked, distant_row_factors, preferred_element_type=jnp.float32
     )
 
-    all_out = jnp.concatenate([near_out, far_out], axis=0)
-    all_rows = jnp.concatenate([near_rows, distant_row_factor_index[:, 0] - row_index * row_span])
-    scatter = (
-        all_rows[None, :] == jnp.arange(row_span, dtype=jnp.int32)[:, None]
-    ).astype(jnp.float32)
-    partial_sum = jnp.dot(
-        scatter,
-        all_out.reshape(all_out.shape[0], states * leaf),
-        precision=lax.Precision.HIGHEST,
-    ).reshape(row_span, states, leaf)
+    def scatter_add(pieces, targets):
+        onehot = (targets[None, :] == jnp.arange(row_span, dtype=jnp.int32)[:, None]).astype(jnp.float32)
+        return jnp.dot(
+            onehot, pieces.reshape(pieces.shape[0], states * leaf), precision=lax.Precision.HIGHEST
+        ).reshape(row_span, states, leaf)
+
+    far_sum = scatter_add(far_out, distant_row_factor_index[:, 0] - row_index * row_span)
+    partial_sum = far_sum + scatter_add(near_out, near_rows)
     partial_sum = partial_sum.transpose(1, 0, 2).reshape(states, row_span * leaf)
 
     exchanged = lax.all_to_all(partial_sum, "col", 0, 0, tiled=True)

time: 61.2 us -> 64.7 us (1.057)
  local copies, waits for them, and re-layouts: 3.78 us -> 7.23 us
  waiting for transfers between devices: 5.3 us -> 6.28 us
  other arithmetic: 1.68 us -> 0.71 us
  starting transfers between devices: 10.4 us -> 9.74 us
    concatenate x1, local copies, waits for them, and re-layouts: 0.22 us -> 2.55 us  [per_device(): send = jnp.concatenate(pieces, axis=0)]
    all_to_all x1, waiting for transfers between devices: 5.3 us -> 6.28 us  [per_device(): lax.all_to_all(send, 'row', 0, 0, tiled=True).reshape(states, window, leaf)]
    reshape x1, local copies, waits for them, and re-layouts: 1.15 us -> 0.18 us  [per_device(): lax.all_to_all(send, 'row', 0, 0, tiled=True).reshape(states, window, leaf)]
    all_to_all x1, local copies, waits for them, and re-layouts: 0.1 us -> 0.89 us  [per_device(): exchanged = lax.all_to_all(partial_sum, 'col', 0, 0, tiled=True)]
    sub x1, other arithmetic: 0.76 us -> 0.01 us  [per_device(): distant_row_factor_index[:, 0] - row_index * row_span]
    gather x1, local copies, waits for them, and re-layouts: 0.59 us -> 1.27 us  [per_device(): picked = jnp.take(summed, distant_row_factor_index[:, 1], axis=0)]
    dot_general x1 -> x2, matrix products: 1.48 us -> 1.72 us  [scatter_add(): jnp.dot(onehot, pieces.reshape(pieces.shape[0], states * leaf), precision...]
  transfers between devices with their start and end apart: 2 -> 2, of which waited for: 1 -> 1; matrix products, arithmetic and copies ran while one was open for 9% -> 10% of each run, Pallas kernels for 0% -> 0%
where the time goes in v16:
time: 64.7 us; the launch traced here: 64.1 us
  blocking collectives  28.8 us (45%)
  starting transfers between devices  9.74 us (15%)
  local copies, waits for them, and re-layouts  7.23 us (11%)
  waiting for transfers between devices  6.28 us (10%)
  matrix products  6.15 us (10%)
  Pallas kernels  4.97 us (8%)
  other arithmetic  0.71 us (1%)
    all_to_all x1, blocking collectives, per_device(): exchanged = lax.all_to_all(partial_sum, 'col', 0, 0, tiled=True)  18.7 us
    all_gather x1, blocking collectives, per_device(): ordered = lax.all_gather(mine, 'row', axis=0, tiled=True)  10.1 us
    all_to_all x1, starting transfers between devices, per_device(): every_block = lax.all_to_all(stacked, 'col', 0, 0, tiled=True)  6.32 us
    all_to_all x1, waiting for transfers between devices, per_device(): lax.all_to_all(send, 'row', 0, 0, tiled=True).reshape(states, window, leaf)  6.28 us
    pallas_call x1, Pallas kernels, reorder(): pl.pallas_call(_lane_gather_kernel, out_shape=(jax.ShapeDtypeStruct((rows...  4.97 us
    all_to_all x1, starting transfers between devices, per_device(): lax.all_to_all(send, 'row', 0, 0, tiled=True).reshape(states, window, leaf)  3.43 us
    concatenate x1, local copies, waits for them, and re-layouts, per_device(): send = jnp.concatenate(pieces, axis=0)  2.55 us
    dot_general x2, matrix products, scatter_add(): jnp.dot(onehot, pieces.reshape(pieces.shape[0], states * leaf), precision...  1.72 us
  transfers between devices with their start and end apart: 2, of which 1 were waited for; matrix products, arithmetic and copies ran while one was open for 10% of the time, Pallas kernels for 0%

profile of v16, /device:TPU:0, one launch (start us, length us, event | category | flops | bytes accessed | tf_op | source)
XLA Modules:
  0.0 64.1 jit_solution(10854591172611568276)
XLA Ops:
  0.0 0.0 copy-start
  0.0 0.0 copy-start.2
  0.0 5.0 %shard_map.82 = (bf16[4,8192]{1,0:T(4,128)(2,1)}, bf16[4,4,8192]{2,1,0:T(4,128)(2,1)}) custom-call(bf16[4,8192]{1,0:T(4,128)(2,1)} %values_ref.1, s32[64,128]{1,0:T(8,128)} %bitcast.81), custom_call_target="tpu_custom_call" | custom-call | tf_op jit(solution)/shard_map/pallas_call | solution.py:67
  5.0 6.3 %all-to-all-start = ((bf16[4,4,8192]{2,1,0:T(4,128)(2,1)}), bf16[4,4,8192]{2,1,0:T(4,128)(2,1)S(1)}, u32[]{:S(2)}, u32[]{:S(2)}) async-start(bf16[4,4,8192]{2,1,0:T(4,128)(2,1)} %get-tuple-element.8), calls=%async_computation | async-start | bytes 524288 | tf_op jit(solution)/shard_map/all_to_all | solution.py:107
  11.3 10.1 %all-gather = bf16[8,4,8192]{2,1,0:T(4,128)(2,1)S(1)} all-gather(bf16[1,4,8192]{2,1,0:T(4,128)(2,1)} %bitcast.80), channel_id=1, replica_groups=mesh['row'=8,'col'=4] {'row'}, dimensions={0}, use_global_device_ids=true | all-gather | bytes 589824 | tf_op jit(solution)/shard_map/all_gather | solution.py:115
  21.4 0.0 copy-start.3
  21.4 0.4 reshape.54
  21.8 0.0 copy-start.1
  21.8 0.0 copy-done.2
  21.8 0.3 fusion.1
  22.2 1.4 %fusion.7 = f32[30,32,32]{2,1,0:T(8,128)S(1)} fusion(bf16[30,256,32]{1,2,0:T(8,128)(2,1)} %param.14, bf16[32,30,256]{2,1,0:T(8,128)(2,1)S(1)} %fusion.1), kind=kOutput, calls=%fused_computation.13 | convolution fusion | flops 15728640 | bytes 1105920 | tf_op jit(solution)/shard_map/spk,pkr->psr/dot_general | solution.py:138
  23.6 0.2 reshape.55
  23.9 0.2 convolution_convert_fusion.2
  24.0 0.1 reshape.56
  24.2 0.0 copy-done.3
  24.2 1.3 %gather_fusion = bf16[30,32,32]{2,1,0:T(8,128)(2,1)} fusion(bf16[8,32,32]{2,1,0:T(8,128)(2,1)S(1)} %reshape.56, s32[1024]{0:T(1024)S(1)} %pad_clamp_fusion), kind=kCustom, calls=%fused_computation | custom fusion | bytes 123000 | tf_op jit(solution)/shard_map/jit(_take)/gather | solution.py:151
  25.5 0.0 copy-done.1
  25.5 1.5 %fusion.11 = f32[30,32,256]{2,1,0:T(8,128)S(1)} fusion(bf16[30,256,32]{1,2,0:T(8,128)(2,1)} %param.12, bf16[30,32,32]{2,1,0:T(8,128)(2,1)} %gather_fusion, pred[30]{0:T(512)(128)(4,1)S(1)} %and_bitcast_fusion), kind=kOutput, calls=%fused_computation.17 | convolution fusion | flops 15759360 | bytes 1536030 | tf_op jit(solution)/shard_map/psr,plr->psl/dot_general | solution.py:152
  27.0 0.0 all-to-all-done
  27.0 0.8 %slice_bitcast_fusion.1 = (bf16[4,4864]{1,0:T(4,128)(2,1)S(1)}, bf16[4,4864]{1,0:T(4,128)(2,1)S(1)}, bf16[4,4864]{1,0:T(4,128)(2,1)S(1)}, bf16[4,4864]{1,0:T(4,1...) fusion(bf16[4,4,8192]{2,1,0:T(4,128)(2,1)S(1)} %all-to-all-done), kind=kLoop, calls=%fused_computation.21 | loop fusion | bytes 622592 | tf_op jit(solution)/shard_map/squeeze | solution.py:112
  27.8 2.6 %concatenate.3 = bf16[32,4864]{1,0:T(8,128)(2,1)S(1)} concatenate(bf16[4,4864]{1,0:T(4,128)(2,1)} %get-tuple-element.16, bf16[4,4864]{1,0:T(4,128)(2,1)} %get-tuple-element.15, bf16[4,4864]{1,0:T(4,128)(2,1)} %get-tuple-element.14, bf16[4,4864]{1,0:T(4,128)(2,1)} %get-tuple-element.13, bf16[4,4864]{1,0:T(4,128)(2,1)} %get-tuple-element.12, ...), dimensions={0} | concatenate | bytes 622592 | tf_op jit(solution)/shard_map/concatenate | solution.py:113
  30.3 0.8 %all_to_all.16 = bf16[8,4,4864]{2,1,0:T(4,128)(2,1)} reshape(bf16[32,4864]{1,0:T(8,128)(2,1)S(1)} %concatenate.3) | data formatting | bytes 622592 | tf_op jit(solution)/shard_map/all_to_all | solution.py:117
  31.1 3.4 %all-to-all-start.1 = ((bf16[8,4,4864]{2,1,0:T(4,128)(2,1)}), bf16[8,4,4864]{2,1,0:T(4,128)(2,1)S(1)}, u32[]{:S(2)}, u32[]{:S(2)}) async-start(bf16[8,4,4864]{2,1,0:T(4,128)(2,1)} %all_to_all.16), calls=%async_computation.1 | async-start | bytes 622592 | tf_op jit(solution)/shard_map/all_to_all | solution.py:117
  34.6 0.1 slice_bitcast_fusion
  34.6 1.0 %fusion.3 = f32[16,32,256]{2,0,1:T(8,128)S(1)} fusion(f32[32,256,30]{1,0,2:T(8,128)S(1)} %slice_bitcast_fusion, s32[30]{0:T(128)S(1)} %get-tuple-element.19), kind=kOutput, calls=%fused_computation.8 | convolution fusion | flops 47186400 | bytes 1507448 | tf_op jit(solution)/shard_map/dot_general | solution.py:158
  35.7 6.3 %all-to-all-done.1 = bf16[8,4,4864]{2,1,0:T(4,128)(2,1)S(1)} async-done(((bf16[8,4,4864]{2,1,0:T(4,128)(2,1)}), bf16[8,4,4864]{2,1,0:T(4,128)(2,1)S(1)}, u32[]{:S(2)}, u32[]{:S(2)}) %all-to-all-start.1) | async-done | bytes 311328 | tf_op jit(solution)/shard_map/all_to_all | solution.py:117
  42.0 0.2 reshape.58
  42.1 0.3 fusion.2
  42.4 0.0 copy-done
  42.4 0.7 %fusion.9 = f32[16,32,256]{2,1,0:T(8,128)S(1)} fusion(bf16[16,256,256]{2,1,0:T(8,128)(2,1)S(1)} %copy-done, bf16[32,16,256]{2,1,0:T(8,128)(2,1)S(1)} %fusion.2), kind=kOutput, calls=%fused_computation.15 | convolution fusion | flops 67108864 | bytes 2883584 | tf_op jit(solution)/shard_map/snk,nlk->nsl/dot_general | solution.py:127
  43.2 0.7 %fusion = f32[32,16,256]{2,1,0:T(8,128)S(1)} fusion(f32[16,32,256]{2,0,1:T(8,128)S(1)} %fusion.3, s32[16]{0:T(128)S(1)} %get-tuple-element.17, f32[2,8,32,256]{3,2,1,0:T(8,128)S(1)} %bitcast.79), kind=kOutput, calls=%fused_computation.3 | convolution fusion | flops 25297152 | bytes 1572928 | tf_op jit(solution)/shard_map/dot_general | solution.py:158
  43.8 0.9 %all_to_all.18 = f32[4,8,4096]{2,1,0:T(8,128)} reshape(f32[32,16,256]{2,1,0:T(8,128)S(1)} %fusion) | data formatting | bytes 1048576 | tf_op jit(solution)/shard_map/all_to_all | solution.py:166
  44.7 18.7 %all_to_all.23 = f32[4,8,4096]{2,1,0:T(8,128)S(1)} all-to-all(f32[4,8,4096]{2,1,0:T(8,128)} %all_to_all.18), channel_id=1, replica_groups=mesh['row'=8,'col'=4] {'col'}, dimensions={0} | all-to-all | bytes 1048576 | tf_op jit(solution)/shard_map/all_to_all | solution.py:166
  63.4 0.7 %reduce_sum.9 = f32[8,4096]{1,0:T(8,128)} reduce(f32[4,8,4096]{2,1,0:T(8,128)S(1)} %all_to_all.23, f32[]{:T(128)} %constant.52.clone.1), dimensions={0}, to_apply=%region_0.1 | reduce | flops 98304 | bytes 655364 | tf_op jit(solution)/shard_map/reduce_sum | solution.py:167
  (5 shorter events, 0.0 us)
Async XLA Ops:
  0.0 42.4 %copy-start = (bf16[16,256,256]{2,1,0:T(8,128)(2,1)S(1)}, bf16[16,256,256]{2,1,0:T(8,128)(2,1)}, u32[]{:S(2)}) copy-start(bf16[16,256,256]{2,1,0:T(8,128)(2,1)} %param.10) | copy-start | bytes 6291460
  0.0 21.8 %copy-start.2 = (s32[30,2]{0,1:T(2,128)S(1)}, s32[30,2]{0,1:T(2,128)}, u32[]{:S(2)}) copy-start(s32[30,2]{0,1:T(2,128)} %param.15) | copy-start | bytes 724
  5.0 22.1 %all-to-all-start = ((bf16[4,4,8192]{2,1,0:T(4,128)(2,1)}), bf16[4,4,8192]{2,1,0:T(4,128)(2,1)S(1)}, u32[]{:S(2)}, u32[]{:S(2)}) async-start(bf16[4,4,8192]{2,1,0:T(4,128)(2,1)} %get-tuple-element.8), calls=%async_computation | async-start | bytes 524288 | tf_op jit(solution)/shard_map/all_to_all | solution.py:107
  21.4 2.7 %copy-start.3 = (s32[30,2]{0,1:T(2,128)S(1)}, s32[30,2]{0,1:T(2,128)}, u32[]{:S(2)}) copy-start(s32[30,2]{0,1:T(2,128)} %param.13) | copy-start | bytes 724
  21.8 3.7 %copy-start.1 = (s32[16,2]{0,1:T(2,128)S(1)}, s32[16,2]{0,1:T(2,128)}, u32[]{:S(2)}) copy-start(s32[16,2]{0,1:T(2,128)} %param.11) | copy-start | bytes 388
  31.1 10.8 %all-to-all-start.1 = ((bf16[8,4,4864]{2,1,0:T(4,128)(2,1)}), bf16[8,4,4864]{2,1,0:T(4,128)(2,1)S(1)}, u32[]{:S(2)}, u32[]{:S(2)}) async-start(bf16[8,4,4864]{2,1,0:T(4,128)(2,1)} %all_to_all.16), calls=%async_computation.1 | async-start | bytes 622592 | tf_op jit(solution)/shard_map/all_to_all | solution.py:117

commit v17 on v15

--- a/solution.py
+++ b/solution.py
@@ -161,7 +161,7 @@
     partial_sum = jnp.dot(
         scatter,
         all_out.reshape(all_out.shape[0], states * leaf),
-        precision=lax.Precision.HIGHEST,
+        precision=lax.Precision.HIGH,
     ).reshape(row_span, states, leaf)
     partial_sum = partial_sum.transpose(1, 0, 2).reshape(states, row_span * leaf)
 

time: 61.2 us -> 60.9 us (level)
  no operation moved by 1% of the time
where the time goes in v17:
time: 60.9 us; the launch traced here: 60.4 us
  blocking collectives  28.6 us (47%)
  starting transfers between devices  10.4 us (17%)
  matrix products  5.47 us (9%)
  waiting for transfers between devices  5.3 us (9%)
  Pallas kernels  4.96 us (8%)
  local copies, waits for them, and re-layouts  3.78 us (6%)
  other arithmetic  1.68 us (3%)
    all_to_all x1, blocking collectives, per_device(): exchanged = lax.all_to_all(partial_sum, 'col', 0, 0, tiled=True)  18.5 us
    all_gather x1, blocking collectives, per_device(): ordered = lax.all_gather(mine, 'row', axis=0, tiled=True)  10.1 us
    all_to_all x1, starting transfers between devices, per_device(): every_block = lax.all_to_all(stacked, 'col', 0, 0, tiled=True)  6.32 us
    all_to_all x1, waiting for transfers between devices, per_device(): lax.all_to_all(send, 'row', 0, 0, tiled=True).reshape(states, window, leaf)  5.3 us
    pallas_call x1, Pallas kernels, reorder(): pl.pallas_call(_lane_gather_kernel, out_shape=(jax.ShapeDtypeStruct((rows...  4.96 us
    all_to_all x1, starting transfers between devices, per_device(): lax.all_to_all(send, 'row', 0, 0, tiled=True).reshape(states, window, leaf)  4.07 us
    dot_general x1, matrix products, per_device(): jnp.einsum('spk,pkr->psr', v_src, distant_column_factors, preferred_eleme...  1.43 us
    dot_general x1, matrix products, per_device(): jnp.einsum('psr,plr->psl', picked, distant_row_factors, preferred_element...  1.37 us
  transfers between devices with their start and end apart: 2, of which 1 were waited for; matrix products, arithmetic and copies ran while one was open for 9% of the time, Pallas kernels for 0%

profile of v17, /device:TPU:0, one launch (start us, length us, event | category | flops | bytes accessed | tf_op | source)
XLA Modules:
  0.0 60.4 jit_solution(13869153759915267444)
XLA Ops:
  0.0 0.0 copy-start
  0.0 0.0 copy-start.1
  0.0 0.0 copy-start.2
  0.0 5.0 %shard_map.82 = (bf16[4,8192]{1,0:T(4,128)(2,1)}, bf16[4,4,8192]{2,1,0:T(4,128)(2,1)}) custom-call(bf16[4,8192]{1,0:T(4,128)(2,1)} %values_ref.1, s32[64,128]{1,0:T(8,128)} %bitcast.66), custom_call_target="tpu_custom_call" | custom-call | tf_op jit(solution)/shard_map/pallas_call | solution.py:67
  5.0 6.3 %all-to-all-start = ((bf16[4,4,8192]{2,1,0:T(4,128)(2,1)}), bf16[4,4,8192]{2,1,0:T(4,128)(2,1)S(1)}, u32[]{:S(2)}, u32[]{:S(2)}) async-start(bf16[4,4,8192]{2,1,0:T(4,128)(2,1)} %get-tuple-element.7), calls=%async_computation | async-start | bytes 524288 | tf_op jit(solution)/shard_map/all_to_all | solution.py:107
  11.3 0.8 %subtract_bitcast_fusion.2 = (s32[30]{0:T(128)S(1)}, s32[30]{0:T(128)S(1)}) fusion(s32[30,2]{0,1:T(2,128)} %param.13, s32[]{:T(128)S(6)} %mul.15), kind=kLoop, calls=%fused_computation.45 | loop fusion | flops 120 | bytes 484 | tf_op jit(solution)/shard_map/sub | solution.py:157
  12.0 10.1 %all-gather = bf16[8,4,8192]{2,1,0:T(4,128)(2,1)S(1)} all-gather(bf16[1,4,8192]{2,1,0:T(4,128)(2,1)} %bitcast.65), channel_id=1, replica_groups=mesh['row'=8,'col'=4] {'row'}, dimensions={0}, use_global_device_ids=true | all-gather | bytes 589824 | tf_op jit(solution)/shard_map/all_gather | solution.py:115
  22.2 0.4 reshape.41
  22.6 0.0 copy-start.3
  22.6 0.0 copy-done.1
  22.6 0.0 copy-done.2
  22.6 0.3 fusion.2
  23.0 1.4 %fusion.7 = f32[30,32,32]{2,1,0:T(8,128)S(1)} fusion(bf16[30,256,32]{1,2,0:T(8,128)(2,1)} %param.14, bf16[32,30,256]{2,1,0:T(8,128)(2,1)S(1)} %fusion.2), kind=kOutput, calls=%fused_computation.11 | convolution fusion | flops 15728640 | bytes 1105920 | tf_op jit(solution)/shard_map/spk,pkr->psr/dot_general | solution.py:138
  24.4 0.0 copy-done.3
  24.4 0.2 reshape.42
  24.7 0.2 convolution_convert_fusion.2
  24.8 0.0 all-to-all-done
  24.9 0.1 slice_bitcast_fusion.1
  25.0 0.2 concatenate.10
  25.2 0.8 %all_to_all.16 = bf16[8,4,4864]{2,1,0:T(4,128)(2,1)} reshape(bf16[32,4864]{1,0:T(8,128)(2,1)S(1)} %concatenate.10) | data formatting | bytes 622592 | tf_op jit(solution)/shard_map/all_to_all | solution.py:117
  26.0 4.1 %all-to-all-start.1 = ((bf16[8,4,4864]{2,1,0:T(4,128)(2,1)}), bf16[8,4,4864]{2,1,0:T(4,128)(2,1)}, u32[]{:S(2)}, u32[]{:S(2)}) async-start(bf16[8,4,4864]{2,1,0:T(4,128)(2,1)} %all_to_all.16), calls=%async_computation.1 | async-start | bytes 622592 | tf_op jit(solution)/shard_map/all_to_all | solution.py:117
  30.1 0.1 pad_add_fusion
  30.2 0.1 reshape.43
  30.3 0.6 gather_fusion
  30.9 1.4 %fusion.11 = f32[30,32,256]{2,1,0:T(8,128)S(1)} fusion(bf16[30,256,32]{1,2,0:T(8,128)(2,1)} %param.12, bf16[30,32,32]{2,1,0:T(8,128)(2,1)S(1)} %gather_fusion, pred[30]{0:T(512)(128)(4,1)S(1)} %and_bitcast_fusion), kind=kOutput, calls=%fused_computation.15 | convolution fusion | flops 15759360 | bytes 1536030 | tf_op jit(solution)/shard_map/psr,plr->psl/dot_general | solution.py:152
  32.2 5.3 %all-to-all-done.1 = bf16[8,4,4864]{2,1,0:T(4,128)(2,1)} async-done(((bf16[8,4,4864]{2,1,0:T(4,128)(2,1)}), bf16[8,4,4864]{2,1,0:T(4,128)(2,1)}, u32[]{:S(2)}, u32[]{:S(2)}) %all-to-all-start.1) | async-done | bytes 311328 | tf_op jit(solution)/shard_map/all_to_all | solution.py:117
  37.5 1.1 %reshape.40 = bf16[32,19,256]{2,1,0:T(8,128)(2,1)S(1)} reshape(bf16[8,4,4864]{2,1,0:T(4,128)(2,1)} %all-to-all-done.1) | data formatting | bytes 622592 | tf_op jit(solution)/shard_map/reshape | solution.py:117
  38.7 0.3 fusion.6
  39.0 0.0 copy-done
  39.0 0.7 %fusion.9 = f32[16,32,256]{2,1,0:T(8,128)S(1)} fusion(bf16[16,256,256]{2,1,0:T(8,128)(2,1)S(1)} %copy-done, bf16[32,16,256]{2,1,0:T(8,128)(2,1)S(1)} %fusion.6), kind=kOutput, calls=%fused_computation.13 | convolution fusion | flops 67108864 | bytes 2883584 | tf_op jit(solution)/shard_map/snk,nlk->nsl/dot_general | solution.py:127
  39.7 0.1 pad_maximum_fusion
  39.8 0.1 slice_bitcast_fusion
  39.9 1.2 %fusion.3 = f32[32,16,256]{2,1,0:T(8,128)S(1)} fusion(f32[32,256,46]{1,0,2:T(8,128)S(1)} %slice_bitcast_fusion, s32[46]{0:T(128)S(1)} %pad_add_fusion), kind=kOutput, calls=%fused_computation.7 | convolution fusion | flops 36176608 | bytes 2031800 | tf_op jit(solution)/shard_map/dot_general | solution.py:161
  41.1 0.1 all_to_all.18
  41.2 18.5 %all_to_all.23 = f32[4,8,4096]{2,1,0:T(8,128)S(1)} all-to-all(f32[4,8,4096]{2,1,0:T(8,128)S(1)} %all_to_all.18), channel_id=1, replica_groups=mesh['row'=8,'col'=4] {'col'}, dimensions={0} | all-to-all | bytes 1048576 | tf_op jit(solution)/shard_map/all_to_all | solution.py:168
  59.7 0.7 %reduce_sum.9 = f32[8,4096]{1,0:T(8,128)} reduce(f32[4,8,4096]{2,1,0:T(8,128)S(1)} %all_to_all.23, f32[]{:T(128)} %constant.52.clone.1), dimensions={0}, to_apply=%region_0.1 | reduce | flops 98304 | bytes 655364 | tf_op jit(solution)/shard_map/reduce_sum | solution.py:169
  (4 shorter events, 0.0 us)
Async XLA Ops:
  0.0 39.0 %copy-start = (bf16[16,256,256]{2,1,0:T(8,128)(2,1)S(1)}, bf16[16,256,256]{2,1,0:T(8,128)(2,1)}, u32[]{:S(2)}) copy-start(bf16[16,256,256]{2,1,0:T(8,128)(2,1)} %param.10) | copy-start | bytes 6291460
  0.0 22.6 %copy-start.1 = (s32[16,2]{0,1:T(2,128)S(1)}, s32[16,2]{0,1:T(2,128)}, u32[]{:S(2)}) copy-start(s32[16,2]{0,1:T(2,128)} %param.11) | copy-start | bytes 388
  0.0 22.6 %copy-start.2 = (s32[30,2]{0,1:T(2,128)S(1)}, s32[30,2]{0,1:T(2,128)}, u32[]{:S(2)}) copy-start(s32[30,2]{0,1:T(2,128)} %param.15) | copy-start | bytes 724
  5.0 19.9 %all-to-all-start = ((bf16[4,4,8192]{2,1,0:T(4,128)(2,1)}), bf16[4,4,8192]{2,1,0:T(4,128)(2,1)S(1)}, u32[]{:S(2)}, u32[]{:S(2)}) async-start(bf16[4,4,8192]{2,1,0:T(4,128)(2,1)} %get-tuple-element.7), calls=%async_computation | async-start | bytes 524288 | tf_op jit(solution)/shard_map/all_to_all | solution.py:107
  22.6 1.9 %copy-start.3 = (s32[30,2]{0,1:T(2,128)S(1)}, s32[30,2]{0,1:T(2,128)}, u32[]{:S(2)}) copy-start(s32[30,2]{0,1:T(2,128)} %param.13) | copy-start | bytes 724
  26.0 11.6 %all-to-all-start.1 = ((bf16[8,4,4864]{2,1,0:T(4,128)(2,1)}), bf16[8,4,4864]{2,1,0:T(4,128)(2,1)}, u32[]{:S(2)}, u32[]{:S(2)}) async-start(bf16[8,4,4864]{2,1,0:T(4,128)(2,1)} %all_to_all.16), calls=%async_computation.1 | async-start | bytes 622592 | tf_op jit(solution)/shard_map/all_to_all | solution.py:117

commit v18 on v17

--- a/solution.py
+++ b/solution.py
@@ -9,7 +9,7 @@
 REACH = 3
 LANES = 128
 SUBLANES = 8
-BATCH = 16
+BATCH = 8
 
 
 def _lane_gather_kernel(values_ref, order_ref, out_ref, copies_ref, doubled_ref):

time: 60.9 us -> 61 us (level)
  no operation moved by 1% of the time
where the time goes in v18:
time: 61 us; the launch traced here: 60.4 us
  blocking collectives  28.6 us (47%)
  starting transfers between devices  10.4 us (17%)
  matrix products  5.46 us (9%)
  waiting for transfers between devices  5.3 us (9%)
  Pallas kernels  5.01 us (8%)
  local copies, waits for them, and re-layouts  3.78 us (6%)
  other arithmetic  1.68 us (3%)
    all_to_all x1, blocking collectives, per_device(): exchanged = lax.all_to_all(partial_sum, 'col', 0, 0, tiled=True)  18.5 us
    all_gather x1, blocking collectives, per_device(): ordered = lax.all_gather(mine, 'row', axis=0, tiled=True)  10.1 us
    all_to_all x1, starting transfers between devices, per_device(): every_block = lax.all_to_all(stacked, 'col', 0, 0, tiled=True)  6.32 us
    all_to_all x1, waiting for transfers between devices, per_device(): lax.all_to_all(send, 'row', 0, 0, tiled=True).reshape(states, window, leaf)  5.3 us
    pallas_call x1, Pallas kernels, reorder(): pl.pallas_call(_lane_gather_kernel, out_shape=(jax.ShapeDtypeStruct((rows...  5.01 us
    all_to_all x1, starting transfers between devices, per_device(): lax.all_to_all(send, 'row', 0, 0, tiled=True).reshape(states, window, leaf)  4.07 us
    dot_general x1, matrix products, per_device(): jnp.einsum('spk,pkr->psr', v_src, distant_column_factors, preferred_eleme...  1.43 us
    dot_general x1, matrix products, per_device(): jnp.einsum('psr,plr->psl', picked, distant_row_factors, preferred_element...  1.37 us
  transfers between devices with their start and end apart: 2, of which 1 were waited for; matrix products, arithmetic and copies ran while one was open for 9% of the time, Pallas kernels for 0%

profile of v18, /device:TPU:0, one launch (start us, length us, event | category | flops | bytes accessed | tf_op | source)
XLA Modules:
  0.0 60.4 jit_solution(5144915002439314271)
XLA Ops:
  0.0 0.0 copy-start
  0.0 0.0 copy-start.1
  0.0 0.0 copy-start.2
  0.0 5.0 %shard_map.82 = (bf16[4,8192]{1,0:T(4,128)(2,1)}, bf16[4,4,8192]{2,1,0:T(4,128)(2,1)}) custom-call(bf16[4,8192]{1,0:T(4,128)(2,1)} %values_ref.1, s32[64,128]{1,0:T(8,128)} %bitcast.66), custom_call_target="tpu_custom_call" | custom-call | tf_op jit(solution)/shard_map/pallas_call | solution.py:67
  5.0 6.3 %all-to-all-start = ((bf16[4,4,8192]{2,1,0:T(4,128)(2,1)}), bf16[4,4,8192]{2,1,0:T(4,128)(2,1)S(1)}, u32[]{:S(2)}, u32[]{:S(2)}) async-start(bf16[4,4,8192]{2,1,0:T(4,128)(2,1)} %get-tuple-element.7), calls=%async_computation | async-start | bytes 524288 | tf_op jit(solution)/shard_map/all_to_all | solution.py:107
  11.3 0.8 %subtract_bitcast_fusion.2 = (s32[30]{0:T(128)S(1)}, s32[30]{0:T(128)S(1)}) fusion(s32[30,2]{0,1:T(2,128)} %param.13, s32[]{:T(128)S(6)} %mul.15), kind=kLoop, calls=%fused_computation.45 | loop fusion | flops 120 | bytes 484 | tf_op jit(solution)/shard_map/sub | solution.py:157
  12.1 10.1 %all-gather = bf16[8,4,8192]{2,1,0:T(4,128)(2,1)S(1)} all-gather(bf16[1,4,8192]{2,1,0:T(4,128)(2,1)} %bitcast.65), channel_id=1, replica_groups=mesh['row'=8,'col'=4] {'row'}, dimensions={0}, use_global_device_ids=true | all-gather | bytes 589824 | tf_op jit(solution)/shard_map/all_gather | solution.py:115
  22.2 0.4 reshape.41
  22.6 0.0 copy-start.3
  22.6 0.0 copy-done.1
  22.7 0.0 copy-done.2
  22.7 0.3 fusion.2
  23.0 1.4 %fusion.7 = f32[30,32,32]{2,1,0:T(8,128)S(1)} fusion(bf16[30,256,32]{1,2,0:T(8,128)(2,1)} %param.14, bf16[32,30,256]{2,1,0:T(8,128)(2,1)S(1)} %fusion.2), kind=kOutput, calls=%fused_computation.11 | convolution fusion | flops 15728640 | bytes 1105920 | tf_op jit(solution)/shard_map/spk,pkr->psr/dot_general | solution.py:138
  24.5 0.0 copy-done.3
  24.5 0.2 reshape.42
  24.7 0.2 convolution_convert_fusion.2
  24.9 0.0 all-to-all-done
  24.9 0.1 slice_bitcast_fusion.1
  25.0 0.2 concatenate.10
  25.3 0.8 %all_to_all.16 = bf16[8,4,4864]{2,1,0:T(4,128)(2,1)} reshape(bf16[32,4864]{1,0:T(8,128)(2,1)S(1)} %concatenate.10) | data formatting | bytes 622592 | tf_op jit(solution)/shard_map/all_to_all | solution.py:117
  26.0 4.1 %all-to-all-start.1 = ((bf16[8,4,4864]{2,1,0:T(4,128)(2,1)}), bf16[8,4,4864]{2,1,0:T(4,128)(2,1)}, u32[]{:S(2)}, u32[]{:S(2)}) async-start(bf16[8,4,4864]{2,1,0:T(4,128)(2,1)} %all_to_all.16), calls=%async_computation.1 | async-start | bytes 622592 | tf_op jit(solution)/shard_map/all_to_all | solution.py:117
  30.1 0.1 pad_add_fusion
  30.2 0.1 reshape.43
  30.3 0.6 gather_fusion
  30.9 1.4 %fusion.11 = f32[30,32,256]{2,1,0:T(8,128)S(1)} fusion(bf16[30,256,32]{1,2,0:T(8,128)(2,1)} %param.12, bf16[30,32,32]{2,1,0:T(8,128)(2,1)S(1)} %gather_fusion, pred[30]{0:T(512)(128)(4,1)S(1)} %and_bitcast_fusion), kind=kOutput, calls=%fused_computation.15 | convolution fusion | flops 15759360 | bytes 1536030 | tf_op jit(solution)/shard_map/psr,plr->psl/dot_general | solution.py:152
  32.3 5.3 %all-to-all-done.1 = bf16[8,4,4864]{2,1,0:T(4,128)(2,1)} async-done(((bf16[8,4,4864]{2,1,0:T(4,128)(2,1)}), bf16[8,4,4864]{2,1,0:T(4,128)(2,1)}, u32[]{:S(2)}, u32[]{:S(2)}) %all-to-all-start.1) | async-done | bytes 311328 | tf_op jit(solution)/shard_map/all_to_all | solution.py:117
  37.6 1.1 %reshape.40 = bf16[32,19,256]{2,1,0:T(8,128)(2,1)S(1)} reshape(bf16[8,4,4864]{2,1,0:T(4,128)(2,1)} %all-to-all-done.1) | data formatting | bytes 622592 | tf_op jit(solution)/shard_map/reshape | solution.py:117
  38.8 0.3 fusion.6
  39.0 0.0 copy-done
  39.0 0.7 %fusion.9 = f32[16,32,256]{2,1,0:T(8,128)S(1)} fusion(bf16[16,256,256]{2,1,0:T(8,128)(2,1)S(1)} %copy-done, bf16[32,16,256]{2,1,0:T(8,128)(2,1)S(1)} %fusion.6), kind=kOutput, calls=%fused_computation.13 | convolution fusion | flops 67108864 | bytes 2883584 | tf_op jit(solution)/shard_map/snk,nlk->nsl/dot_general | solution.py:127
  39.7 0.1 pad_maximum_fusion
  39.9 0.1 slice_bitcast_fusion
  40.0 1.2 %fusion.3 = f32[32,16,256]{2,1,0:T(8,128)S(1)} fusion(f32[32,256,46]{1,0,2:T(8,128)S(1)} %slice_bitcast_fusion, s32[46]{0:T(128)S(1)} %pad_add_fusion), kind=kOutput, calls=%fused_computation.7 | convolution fusion | flops 36176608 | bytes 2031800 | tf_op jit(solution)/shard_map/dot_general | solution.py:161
  41.2 0.1 all_to_all.18
  41.3 18.5 %all_to_all.23 = f32[4,8,4096]{2,1,0:T(8,128)S(1)} all-to-all(f32[4,8,4096]{2,1,0:T(8,128)S(1)} %all_to_all.18), channel_id=1, replica_groups=mesh['row'=8,'col'=4] {'col'}, dimensions={0} | all-to-all | bytes 1048576 | tf_op jit(solution)/shard_map/all_to_all | solution.py:168
  59.8 0.7 %reduce_sum.9 = f32[8,4096]{1,0:T(8,128)} reduce(f32[4,8,4096]{2,1,0:T(8,128)S(1)} %all_to_all.23, f32[]{:T(128)} %constant.52.clone.1), dimensions={0}, to_apply=%region_0.1 | reduce | flops 98304 | bytes 655364 | tf_op jit(solution)/shard_map/reduce_sum | solution.py:169
  (4 shorter events, 0.0 us)
Async XLA Ops:
  0.0 39.0 %copy-start = (bf16[16,256,256]{2,1,0:T(8,128)(2,1)S(1)}, bf16[16,256,256]{2,1,0:T(8,128)(2,1)}, u32[]{:S(2)}) copy-start(bf16[16,256,256]{2,1,0:T(8,128)(2,1)} %param.10) | copy-start | bytes 6291460
  0.0 22.6 %copy-start.1 = (s32[16,2]{0,1:T(2,128)S(1)}, s32[16,2]{0,1:T(2,128)}, u32[]{:S(2)}) copy-start(s32[16,2]{0,1:T(2,128)} %param.11) | copy-start | bytes 388
  0.0 22.7 %copy-start.2 = (s32[30,2]{0,1:T(2,128)S(1)}, s32[30,2]{0,1:T(2,128)}, u32[]{:S(2)}) copy-start(s32[30,2]{0,1:T(2,128)} %param.15) | copy-start | bytes 724
  5.0 19.9 %all-to-all-start = ((bf16[4,4,8192]{2,1,0:T(4,128)(2,1)}), bf16[4,4,8192]{2,1,0:T(4,128)(2,1)S(1)}, u32[]{:S(2)}, u32[]{:S(2)}) async-start(bf16[4,4,8192]{2,1,0:T(4,128)(2,1)} %get-tuple-element.7), calls=%async_computation | async-start | bytes 524288 | tf_op jit(solution)/shard_map/all_to_all | solution.py:107
  22.6 1.9 %copy-start.3 = (s32[30,2]{0,1:T(2,128)S(1)}, s32[30,2]{0,1:T(2,128)}, u32[]{:S(2)}) copy-start(s32[30,2]{0,1:T(2,128)} %param.13) | copy-start | bytes 724
  26.0 11.6 %all-to-all-start.1 = ((bf16[8,4,4864]{2,1,0:T(4,128)(2,1)}), bf16[8,4,4864]{2,1,0:T(4,128)(2,1)}, u32[]{:S(2)}, u32[]{:S(2)}) async-start(bf16[8,4,4864]{2,1,0:T(4,128)(2,1)} %all_to_all.16), calls=%async_computation.1 | async-start | bytes 622592 | tf_op jit(solution)/shard_map/all_to_all | solution.py:117

commit v19 on v17

--- a/solution.py
+++ b/solution.py
@@ -119,7 +119,6 @@
     home = row_index * col_count // row_count
     start = jnp.clip(row_index * row_span - home * cluster_extent - REACH, 0, cluster_extent - window)
     near_cols = adjacent_cluster_pairs[:, 1] - home * cluster_extent - start
-    near_rows = adjacent_cluster_pairs[:, 0] - row_index * row_span
     pick = (near_cols[:, None] == jnp.arange(window, dtype=jnp.int32)[None, :]).astype(near_window.dtype)
     near_src = jnp.einsum("nw,swk->snk", pick, near_window, preferred_element_type=jnp.float32).astype(
         near_window.dtype
@@ -129,8 +128,8 @@
     )
 
     v_pick = (
-        (distant_column_factor_index[:, 0] - col_index * cluster_extent)[:, None]
-        == jnp.arange(cluster_extent, dtype=jnp.int32)[None, :]
+        distant_column_factor_index[:, 0][:, None]
+        == (col_index * cluster_extent + jnp.arange(cluster_extent, dtype=jnp.int32))[None, :]
     ).astype(leaf_clusters.dtype)
     v_src = jnp.einsum("pc,sck->spk", v_pick, leaf_clusters, preferred_element_type=jnp.float32).astype(
         leaf_clusters.dtype
@@ -154,9 +153,9 @@
     )
 
     all_out = jnp.concatenate([near_out, far_out], axis=0)
-    all_rows = jnp.concatenate([near_rows, distant_row_factor_index[:, 0] - row_index * row_span])
+    all_rows = jnp.concatenate([adjacent_cluster_pairs[:, 0], distant_row_factor_index[:, 0]])
     scatter = (
-        all_rows[None, :] == jnp.arange(row_span, dtype=jnp.int32)[:, None]
+        all_rows[None, :] == (row_index * row_span + jnp.arange(row_span, dtype=jnp.int32))[:, None]
     ).astype(jnp.float32)
     partial_sum = jnp.dot(
         scatter,

time: 60.9 us -> 62.3 us (1.023)
  local copies, waits for them, and re-layouts: 3.78 us -> 4.54 us
  other arithmetic: 1.68 us -> 2.35 us
    sub x2 -> x0, other arithmetic: 0.77 us -> none  [the longest x1 0.76 us: per_device(): distant_row_factor_index[:, 0] - row_index * row_span]
    squeeze x0 -> x2, other arithmetic: none -> 0.77 us  [the longest x1 0.76 us: per_device(): distant_row_factor_index[:, 0]]
    eq x0 -> x1, local copies, waits for them, and re-layouts: none -> 0.76 us  [per_device(): distant_column_factor_index[:, 1][None, :]]
    reduce_and x1, other arithmetic: 0.02 us -> 0.69 us  [per_device(): picked = jnp.take(summed, distant_row_factor_index[:, 1], axis=0)]
  transfers between devices with their start and end apart: 2 -> 2, of which waited for: 1 -> 1; matrix products, arithmetic and copies ran while one was open for 9% -> 11% of each run, Pallas kernels for 0% -> 0%
where the time goes in v19:
time: 62.3 us; the launch traced here: 61.7 us
  blocking collectives  28.6 us (46%)
  starting transfers between devices  10.4 us (17%)
  matrix products  5.44 us (9%)
  waiting for transfers between devices  5.3 us (9%)
  Pallas kernels  4.95 us (8%)
  local copies, waits for them, and re-layouts  4.54 us (7%)
  other arithmetic  2.35 us (4%)
    all_to_all x1, blocking collectives, per_device(): exchanged = lax.all_to_all(partial_sum, 'col', 0, 0, tiled=True)  18.5 us
    all_gather x1, blocking collectives, per_device(): ordered = lax.all_gather(mine, 'row', axis=0, tiled=True)  10.1 us
    all_to_all x1, starting transfers between devices, per_device(): every_block = lax.all_to_all(stacked, 'col', 0, 0, tiled=True)  6.32 us
    all_to_all x1, waiting for transfers between devices, per_device(): lax.all_to_all(send, 'row', 0, 0, tiled=True).reshape(states, window, leaf)  5.3 us
    pallas_call x1, Pallas kernels, reorder(): pl.pallas_call(_lane_gather_kernel, out_shape=(jax.ShapeDtypeStruct((rows...  4.95 us
    all_to_all x1, starting transfers between devices, per_device(): lax.all_to_all(send, 'row', 0, 0, tiled=True).reshape(states, window, leaf)  4.06 us
    dot_general x1, matrix products, per_device(): jnp.einsum('spk,pkr->psr', v_src, distant_column_factors, preferred_eleme...  1.43 us
    dot_general x1, matrix products, per_device(): jnp.einsum('psr,plr->psl', picked, distant_row_factors, preferred_element...  1.37 us
  transfers between devices with their start and end apart: 2, of which 1 were waited for; matrix products, arithmetic and copies ran while one was open for 11% of the time, Pallas kernels for 0%

profile of v19, /device:TPU:0, one launch (start us, length us, event | category | flops | bytes accessed | tf_op | source)
XLA Modules:
  0.0 61.7 jit_solution(18342380568727397788)
XLA Ops:
  0.0 0.0 copy-start
  0.0 0.0 copy-start.1
  0.0 5.0 %shard_map.82 = (bf16[4,8192]{1,0:T(4,128)(2,1)}, bf16[4,4,8192]{2,1,0:T(4,128)(2,1)}) custom-call(bf16[4,8192]{1,0:T(4,128)(2,1)} %values_ref.1, s32[64,128]{1,0:T(8,128)} %bitcast.66), custom_call_target="tpu_custom_call" | custom-call | tf_op jit(solution)/shard_map/pallas_call | solution.py:67
  5.0 6.3 %all-to-all-start = ((bf16[4,4,8192]{2,1,0:T(4,128)(2,1)}), bf16[4,4,8192]{2,1,0:T(4,128)(2,1)S(1)}, u32[]{:S(2)}, u32[]{:S(2)}) async-start(bf16[4,4,8192]{2,1,0:T(4,128)(2,1)} %get-tuple-element.7), calls=%async_computation | async-start | bytes 524288 | tf_op jit(solution)/shard_map/all_to_all | solution.py:107
  11.3 0.7 %and_bitcast_fusion = pred[30]{0:T(512)(128)(4,1)S(1)} fusion(s32[30,2]{0,1:T(2,128)} %param.13), kind=kLoop, calls=%fused_computation.42 | loop fusion | flops 180 | bytes 150 | tf_op jit(solution)/shard_map/jit(_take)/reduce_and | solution.py:150
  12.0 0.8 %slice_bitcast_fusion.11 = (s32[30]{0:T(128)S(1)}, s32[30]{0:T(128)S(1)}) fusion(s32[30,2]{0,1:T(2,128)} %param.13), kind=kLoop, calls=%fused_computation.49 | loop fusion | flops 90 | bytes 480 | tf_op jit(solution)/shard_map/squeeze | solution.py:156
  12.7 0.8 %slice_bitcast_fusion.10 = (s32[30]{0:T(128)S(1)}, s32[30]{0:T(128)S(1)}) fusion(s32[30,2]{0,1:T(2,128)} %param.15), kind=kLoop, calls=%fused_computation.46 | loop fusion | bytes 480 | tf_op jit(solution)/shard_map/eq | solution.py:142
  13.5 10.1 %all-gather = bf16[8,4,8192]{2,1,0:T(4,128)(2,1)S(1)} all-gather(bf16[1,4,8192]{2,1,0:T(4,128)(2,1)} %bitcast.65), channel_id=1, replica_groups=mesh['row'=8,'col'=4] {'row'}, dimensions={0}, use_global_device_ids=true | all-gather | bytes 589824 | tf_op jit(solution)/shard_map/all_gather | solution.py:115
  23.6 0.4 reshape.45
  24.0 0.0 copy-done.1
  24.0 0.3 fusion.2
  24.4 1.4 %fusion.7 = f32[30,32,32]{2,1,0:T(8,128)S(1)} fusion(bf16[30,256,32]{1,2,0:T(8,128)(2,1)} %param.14, bf16[32,30,256]{2,1,0:T(8,128)(2,1)S(1)} %fusion.2), kind=kOutput, calls=%fused_computation.11 | convolution fusion | flops 15728640 | bytes 1105920 | tf_op jit(solution)/shard_map/spk,pkr->psr/dot_general | solution.py:137
  25.8 0.2 reshape.46
  26.1 0.2 convolution_convert_fusion.2
  26.2 0.0 all-to-all-done
  26.2 0.1 slice_bitcast_fusion.1
  26.4 0.2 concatenate.10
  26.6 0.8 %all_to_all.16 = bf16[8,4,4864]{2,1,0:T(4,128)(2,1)} reshape(bf16[32,4864]{1,0:T(8,128)(2,1)S(1)} %concatenate.10) | data formatting | bytes 622592 | tf_op jit(solution)/shard_map/all_to_all | solution.py:117
  27.4 4.1 %all-to-all-start.1 = ((bf16[8,4,4864]{2,1,0:T(4,128)(2,1)}), bf16[8,4,4864]{2,1,0:T(4,128)(2,1)}, u32[]{:S(2)}, u32[]{:S(2)}) async-start(bf16[8,4,4864]{2,1,0:T(4,128)(2,1)} %all_to_all.16), calls=%async_computation.1 | async-start | bytes 622592 | tf_op jit(solution)/shard_map/all_to_all | solution.py:117
  31.5 0.1 pad_add_fusion
  31.5 0.1 reshape.47
  31.6 0.6 gather_fusion
  32.2 1.4 %fusion.11 = f32[30,32,256]{2,1,0:T(8,128)S(1)} fusion(bf16[30,256,32]{1,2,0:T(8,128)(2,1)} %param.12, bf16[30,32,32]{2,1,0:T(8,128)(2,1)S(1)} %gather_fusion, pred[30]{0:T(512)(128)(4,1)S(1)} %and_bitcast_fusion), kind=kOutput, calls=%fused_computation.15 | convolution fusion | flops 15759360 | bytes 1536030 | tf_op jit(solution)/shard_map/psr,plr->psl/dot_general | solution.py:151
  33.6 5.3 %all-to-all-done.1 = bf16[8,4,4864]{2,1,0:T(4,128)(2,1)} async-done(((bf16[8,4,4864]{2,1,0:T(4,128)(2,1)}), bf16[8,4,4864]{2,1,0:T(4,128)(2,1)}, u32[]{:S(2)}, u32[]{:S(2)}) %all-to-all-start.1) | async-done | bytes 311328 | tf_op jit(solution)/shard_map/all_to_all | solution.py:117
  38.9 1.1 %reshape.44 = bf16[32,19,256]{2,1,0:T(8,128)(2,1)S(1)} reshape(bf16[8,4,4864]{2,1,0:T(4,128)(2,1)} %all-to-all-done.1) | data formatting | bytes 622592 | tf_op jit(solution)/shard_map/reshape | solution.py:117
  40.1 0.3 fusion.6
  40.4 0.0 copy-done
  40.4 0.7 %fusion.9 = f32[16,32,256]{2,1,0:T(8,128)S(1)} fusion(bf16[16,256,256]{2,1,0:T(8,128)(2,1)S(1)} %copy-done, bf16[32,16,256]{2,1,0:T(8,128)(2,1)S(1)} %fusion.6), kind=kOutput, calls=%fused_computation.13 | convolution fusion | flops 67108864 | bytes 2883584 | tf_op jit(solution)/shard_map/snk,nlk->nsl/dot_general | solution.py:126
  41.1 0.1 pad_maximum_fusion
  41.2 0.1 slice_bitcast_fusion
  41.3 1.1 %fusion.3 = f32[32,16,256]{2,1,0:T(8,128)S(1)} fusion(f32[32,256,46]{1,0,2:T(8,128)S(1)} %slice_bitcast_fusion, s32[46]{0:T(128)S(1)} %pad_add_fusion, s32[16]{0:T(128)S(1)} %iota_add_fusion.1), kind=kOutput, calls=%fused_computation.7 | convolution fusion | flops 36176608 | bytes 2031864 | tf_op jit(solution)/shard_map/dot_general | solution.py:160
  42.5 0.1 all_to_all.18
  42.6 18.5 %all_to_all.23 = f32[4,8,4096]{2,1,0:T(8,128)S(1)} all-to-all(f32[4,8,4096]{2,1,0:T(8,128)S(1)} %all_to_all.18), channel_id=1, replica_groups=mesh['row'=8,'col'=4] {'col'}, dimensions={0} | all-to-all | bytes 1048576 | tf_op jit(solution)/shard_map/all_to_all | solution.py:167
  61.0 0.7 %reduce_sum.9 = f32[8,4096]{1,0:T(8,128)} reduce(f32[4,8,4096]{2,1,0:T(8,128)S(1)} %all_to_all.23, f32[]{:T(128)} %constant.52.clone.1), dimensions={0}, to_apply=%region_0.1 | reduce | flops 98304 | bytes 655364 | tf_op jit(solution)/shard_map/reduce_sum | solution.py:168
  (4 shorter events, 0.0 us)
Async XLA Ops:
  0.0 40.4 %copy-start = (bf16[16,256,256]{2,1,0:T(8,128)(2,1)S(1)}, bf16[16,256,256]{2,1,0:T(8,128)(2,1)}, u32[]{:S(2)}) copy-start(bf16[16,256,256]{2,1,0:T(8,128)(2,1)} %param.10) | copy-start | bytes 6291460
  0.0 24.0 %copy-start.1 = (s32[16,2]{0,1:T(2,128)S(1)}, s32[16,2]{0,1:T(2,128)}, u32[]{:S(2)}) copy-start(s32[16,2]{0,1:T(2,128)} %param.11) | copy-start | bytes 388
  5.0 21.3 %all-to-all-start = ((bf16[4,4,8192]{2,1,0:T(4,128)(2,1)}), bf16[4,4,8192]{2,1,0:T(4,128)(2,1)S(1)}, u32[]{:S(2)}, u32[]{:S(2)}) async-start(bf16[4,4,8192]{2,1,0:T(4,128)(2,1)} %get-tuple-element.7), calls=%async_computation | async-start | bytes 524288 | tf_op jit(solution)/shard_map/all_to_all | solution.py:107
  27.4 11.5 %all-to-all-start.1 = ((bf16[8,4,4864]{2,1,0:T(4,128)(2,1)}), bf16[8,4,4864]{2,1,0:T(4,128)(2,1)}, u32[]{:S(2)}, u32[]{:S(2)}) async-start(bf16[8,4,4864]{2,1,0:T(4,128)(2,1)} %all_to_all.16), calls=%async_computation.1 | async-start | bytes 622592 | tf_op jit(solution)/shard_map/all_to_all | solution.py:117

commit v20 on v17

--- a/solution.py
+++ b/solution.py
@@ -12,15 +12,12 @@
 BATCH = 16
 
 
-def _lane_gather_kernel(values_ref, order_ref, out_ref, copies_ref, doubled_ref):
+def _lane_gather_kernel(values_ref, order_ref, out_ref, copies_ref):
     rows, width = values_ref.shape
     group = SUBLANES // rows
     tiles = width // LANES
     groups = tiles // group
     batch = min(BATCH, groups)
-    for v in range(tiles):
-        piece = values_ref[:, v * LANES:(v + 1) * LANES].astype(jnp.float32)
-        doubled_ref[:, v * LANES:(v + 1) * LANES] = jnp.concatenate([piece] * group, axis=0)
     sub = lax.broadcasted_iota(jnp.int32, (SUBLANES, LANES), 0) // rows
 
     def group_body(k, carry):
@@ -38,7 +35,8 @@
             highs.append(index // LANES)
 
         def tile_body(v, accs):
-            src = doubled_ref[:, pl.ds(pl.multiple_of(v * LANES, LANES), LANES)]
+            tile = values_ref[:, pl.ds(pl.multiple_of(v * LANES, LANES), LANES)].astype(jnp.float32)
+            src = jnp.concatenate([tile] * group, axis=0)
             return tuple(
                 jnp.where(
                     highs[b] == v,
@@ -70,7 +68,6 @@
             jax.ShapeDtypeStruct((rows, width), values.dtype),
             jax.ShapeDtypeStruct((copies, rows, width), values.dtype),
         ),
-        scratch_shapes=[pltpu.VMEM((SUBLANES, width), jnp.float32)],
     )(values, order.reshape(width // LANES, LANES))
 
 

time: 60.9 us -> 60.9 us (level)
  no operation moved by 1% of the time
where the time goes in v20:
time: 60.9 us; the launch traced here: 60.4 us
  blocking collectives  28.6 us (47%)
  starting transfers between devices  10.4 us (17%)
  matrix products  5.46 us (9%)
  waiting for transfers between devices  5.3 us (9%)
  Pallas kernels  4.95 us (8%)
  local copies, waits for them, and re-layouts  3.78 us (6%)
  other arithmetic  1.68 us (3%)
    all_to_all x1, blocking collectives, per_device(): exchanged = lax.all_to_all(partial_sum, 'col', 0, 0, tiled=True)  18.5 us
    all_gather x1, blocking collectives, per_device(): ordered = lax.all_gather(mine, 'row', axis=0, tiled=True)  10.1 us
    all_to_all x1, starting transfers between devices, per_device(): every_block = lax.all_to_all(stacked, 'col', 0, 0, tiled=True)  6.32 us
    all_to_all x1, waiting for transfers between devices, per_device(): lax.all_to_all(send, 'row', 0, 0, tiled=True).reshape(states, window, leaf)  5.3 us
    pallas_call x1, Pallas kernels, reorder(): pl.pallas_call(_lane_gather_kernel, out_shape=(jax.ShapeDtypeStruct((rows...  4.95 us
    all_to_all x1, starting transfers between devices, per_device(): lax.all_to_all(send, 'row', 0, 0, tiled=True).reshape(states, window, leaf)  4.07 us
    dot_general x1, matrix products, per_device(): jnp.einsum('spk,pkr->psr', v_src, distant_column_factors, preferred_eleme...  1.43 us
    dot_general x1, matrix products, per_device(): jnp.einsum('psr,plr->psl', picked, distant_row_factors, preferred_element...  1.37 us
  transfers between devices with their start and end apart: 2, of which 1 were waited for; matrix products, arithmetic and copies ran while one was open for 9% of the time, Pallas kernels for 0%

profile of v20, /device:TPU:0, one launch (start us, length us, event | category | flops | bytes accessed | tf_op | source)
XLA Modules:
  0.0 60.4 jit_solution(16984812567965221513)
XLA Ops:
  0.0 0.0 copy-start
  0.0 0.0 copy-start.1
  0.0 0.0 copy-start.2
  0.0 4.9 %shard_map.82 = (bf16[4,8192]{1,0:T(4,128)(2,1)}, bf16[4,4,8192]{2,1,0:T(4,128)(2,1)}) custom-call(bf16[4,8192]{1,0:T(4,128)(2,1)} %values_ref.1, s32[64,128]{1,0:T(8,128)} %bitcast.66), custom_call_target="tpu_custom_call" | custom-call | tf_op jit(solution)/shard_map/pallas_call | solution.py:65
  5.0 6.3 %all-to-all-start = ((bf16[4,4,8192]{2,1,0:T(4,128)(2,1)}), bf16[4,4,8192]{2,1,0:T(4,128)(2,1)S(1)}, u32[]{:S(2)}, u32[]{:S(2)}) async-start(bf16[4,4,8192]{2,1,0:T(4,128)(2,1)} %get-tuple-element.7), calls=%async_computation | async-start | bytes 524288 | tf_op jit(solution)/shard_map/all_to_all | solution.py:104
  11.3 0.8 %subtract_bitcast_fusion.2 = (s32[30]{0:T(128)S(1)}, s32[30]{0:T(128)S(1)}) fusion(s32[30,2]{0,1:T(2,128)} %param.13, s32[]{:T(128)S(6)} %mul.15), kind=kLoop, calls=%fused_computation.45 | loop fusion | flops 120 | bytes 484 | tf_op jit(solution)/shard_map/sub | solution.py:154
  12.0 10.1 %all-gather = bf16[8,4,8192]{2,1,0:T(4,128)(2,1)S(1)} all-gather(bf16[1,4,8192]{2,1,0:T(4,128)(2,1)} %bitcast.65), channel_id=1, replica_groups=mesh['row'=8,'col'=4] {'row'}, dimensions={0}, use_global_device_ids=true | all-gather | bytes 589824 | tf_op jit(solution)/shard_map/all_gather | solution.py:112
  22.2 0.4 reshape.41
  22.5 0.0 copy-start.3
  22.6 0.0 copy-done.1
  22.6 0.0 copy-done.2
  22.6 0.3 fusion.2
  23.0 1.4 %fusion.7 = f32[30,32,32]{2,1,0:T(8,128)S(1)} fusion(bf16[30,256,32]{1,2,0:T(8,128)(2,1)} %param.14, bf16[32,30,256]{2,1,0:T(8,128)(2,1)S(1)} %fusion.2), kind=kOutput, calls=%fused_computation.11 | convolution fusion | flops 15728640 | bytes 1105920 | tf_op jit(solution)/shard_map/spk,pkr->psr/dot_general | solution.py:135
  24.4 0.0 copy-done.3
  24.4 0.2 reshape.42
  24.7 0.2 convolution_convert_fusion.2
  24.8 0.0 all-to-all-done
  24.8 0.1 slice_bitcast_fusion.1
  25.0 0.2 concatenate.10
  25.2 0.8 %all_to_all.16 = bf16[8,4,4864]{2,1,0:T(4,128)(2,1)} reshape(bf16[32,4864]{1,0:T(8,128)(2,1)S(1)} %concatenate.10) | data formatting | bytes 622592 | tf_op jit(solution)/shard_map/all_to_all | solution.py:114
  26.0 4.1 %all-to-all-start.1 = ((bf16[8,4,4864]{2,1,0:T(4,128)(2,1)}), bf16[8,4,4864]{2,1,0:T(4,128)(2,1)}, u32[]{:S(2)}, u32[]{:S(2)}) async-start(bf16[8,4,4864]{2,1,0:T(4,128)(2,1)} %all_to_all.16), calls=%async_computation.1 | async-start | bytes 622592 | tf_op jit(solution)/shard_map/all_to_all | solution.py:114
  30.1 0.1 pad_add_fusion
  30.1 0.1 reshape.43
  30.3 0.6 gather_fusion
  30.9 1.4 %fusion.11 = f32[30,32,256]{2,1,0:T(8,128)S(1)} fusion(bf16[30,256,32]{1,2,0:T(8,128)(2,1)} %param.12, bf16[30,32,32]{2,1,0:T(8,128)(2,1)S(1)} %gather_fusion, pred[30]{0:T(512)(128)(4,1)S(1)} %and_bitcast_fusion), kind=kOutput, calls=%fused_computation.15 | convolution fusion | flops 15759360 | bytes 1536030 | tf_op jit(solution)/shard_map/psr,plr->psl/dot_general | solution.py:149
  32.2 5.3 %all-to-all-done.1 = bf16[8,4,4864]{2,1,0:T(4,128)(2,1)} async-done(((bf16[8,4,4864]{2,1,0:T(4,128)(2,1)}), bf16[8,4,4864]{2,1,0:T(4,128)(2,1)}, u32[]{:S(2)}, u32[]{:S(2)}) %all-to-all-start.1) | async-done | bytes 311328 | tf_op jit(solution)/shard_map/all_to_all | solution.py:114
  37.5 1.1 %reshape.40 = bf16[32,19,256]{2,1,0:T(8,128)(2,1)S(1)} reshape(bf16[8,4,4864]{2,1,0:T(4,128)(2,1)} %all-to-all-done.1) | data formatting | bytes 622592 | tf_op jit(solution)/shard_map/reshape | solution.py:114
  38.7 0.3 fusion.6
  39.0 0.0 copy-done
  39.0 0.7 %fusion.9 = f32[16,32,256]{2,1,0:T(8,128)S(1)} fusion(bf16[16,256,256]{2,1,0:T(8,128)(2,1)S(1)} %copy-done, bf16[32,16,256]{2,1,0:T(8,128)(2,1)S(1)} %fusion.6), kind=kOutput, calls=%fused_computation.13 | convolution fusion | flops 67108864 | bytes 2883584 | tf_op jit(solution)/shard_map/snk,nlk->nsl/dot_general | solution.py:124
  39.7 0.1 pad_maximum_fusion
  39.8 0.1 slice_bitcast_fusion
  39.9 1.2 %fusion.3 = f32[32,16,256]{2,1,0:T(8,128)S(1)} fusion(f32[32,256,46]{1,0,2:T(8,128)S(1)} %slice_bitcast_fusion, s32[46]{0:T(128)S(1)} %pad_add_fusion), kind=kOutput, calls=%fused_computation.7 | convolution fusion | flops 36176608 | bytes 2031800 | tf_op jit(solution)/shard_map/dot_general | solution.py:158
  41.1 0.1 all_to_all.18
  41.2 18.5 %all_to_all.23 = f32[4,8,4096]{2,1,0:T(8,128)S(1)} all-to-all(f32[4,8,4096]{2,1,0:T(8,128)S(1)} %all_to_all.18), channel_id=1, replica_groups=mesh['row'=8,'col'=4] {'col'}, dimensions={0} | all-to-all | bytes 1048576 | tf_op jit(solution)/shard_map/all_to_all | solution.py:165
  59.7 0.7 %reduce_sum.9 = f32[8,4096]{1,0:T(8,128)} reduce(f32[4,8,4096]{2,1,0:T(8,128)S(1)} %all_to_all.23, f32[]{:T(128)} %constant.52.clone.1), dimensions={0}, to_apply=%region_0.1 | reduce | flops 98304 | bytes 655364 | tf_op jit(solution)/shard_map/reduce_sum | solution.py:166
  (4 shorter events, 0.0 us)
Async XLA Ops:
  0.0 39.0 %copy-start = (bf16[16,256,256]{2,1,0:T(8,128)(2,1)S(1)}, bf16[16,256,256]{2,1,0:T(8,128)(2,1)}, u32[]{:S(2)}) copy-start(bf16[16,256,256]{2,1,0:T(8,128)(2,1)} %param.10) | copy-start | bytes 6291460
  0.0 22.6 %copy-start.1 = (s32[16,2]{0,1:T(2,128)S(1)}, s32[16,2]{0,1:T(2,128)}, u32[]{:S(2)}) copy-start(s32[16,2]{0,1:T(2,128)} %param.11) | copy-start | bytes 388
  0.0 22.6 %copy-start.2 = (s32[30,2]{0,1:T(2,128)S(1)}, s32[30,2]{0,1:T(2,128)}, u32[]{:S(2)}) copy-start(s32[30,2]{0,1:T(2,128)} %param.15) | copy-start | bytes 724
  5.0 19.9 %all-to-all-start = ((bf16[4,4,8192]{2,1,0:T(4,128)(2,1)}), bf16[4,4,8192]{2,1,0:T(4,128)(2,1)S(1)}, u32[]{:S(2)}, u32[]{:S(2)}) async-start(bf16[4,4,8192]{2,1,0:T(4,128)(2,1)} %get-tuple-element.7), calls=%async_computation | async-start | bytes 524288 | tf_op jit(solution)/shard_map/all_to_all | solution.py:104
  22.5 1.9 %copy-start.3 = (s32[30,2]{0,1:T(2,128)S(1)}, s32[30,2]{0,1:T(2,128)}, u32[]{:S(2)}) copy-start(s32[30,2]{0,1:T(2,128)} %param.13) | copy-start | bytes 724
  26.0 11.6 %all-to-all-start.1 = ((bf16[8,4,4864]{2,1,0:T(4,128)(2,1)}), bf16[8,4,4864]{2,1,0:T(4,128)(2,1)}, u32[]{:S(2)}, u32[]{:S(2)}) async-start(bf16[8,4,4864]{2,1,0:T(4,128)(2,1)} %all_to_all.16), calls=%async_computation.1 | async-start | bytes 622592 | tf_op jit(solution)/shard_map/all_to_all | solution.py:114

commit v21 on v20

--- a/solution.py
+++ b/solution.py
@@ -129,11 +129,11 @@
         (distant_column_factor_index[:, 0] - col_index * cluster_extent)[:, None]
         == jnp.arange(cluster_extent, dtype=jnp.int32)[None, :]
     ).astype(leaf_clusters.dtype)
-    v_src = jnp.einsum("pc,sck->spk", v_pick, leaf_clusters, preferred_element_type=jnp.float32).astype(
+    v_src = jnp.einsum("pc,sck->psk", v_pick, leaf_clusters, preferred_element_type=jnp.float32).astype(
         leaf_clusters.dtype
     )
     coeffs = jnp.einsum(
-        "spk,pkr->psr", v_src, distant_column_factors, preferred_element_type=jnp.float32
+        "psk,pkr->psr", v_src, distant_column_factors, preferred_element_type=jnp.float32
     )
     fragments = coeffs.shape[0]
     column_indicator = (

time: 60.9 us -> 60.9 us (level)
  no operation moved by 1% of the time
where the time goes in v21:
time: 60.9 us; the launch traced here: 60.4 us
  blocking collectives  28.6 us (47%)
  starting transfers between devices  10.4 us (17%)
  matrix products  5.46 us (9%)
  waiting for transfers between devices  5.31 us (9%)
  Pallas kernels  4.95 us (8%)
  local copies, waits for them, and re-layouts  3.78 us (6%)
  other arithmetic  1.68 us (3%)
    all_to_all x1, blocking collectives, per_device(): exchanged = lax.all_to_all(partial_sum, 'col', 0, 0, tiled=True)  18.5 us
    all_gather x1, blocking collectives, per_device(): ordered = lax.all_gather(mine, 'row', axis=0, tiled=True)  10.1 us
    all_to_all x1, starting transfers between devices, per_device(): every_block = lax.all_to_all(stacked, 'col', 0, 0, tiled=True)  6.32 us
    all_to_all x1, waiting for transfers between devices, per_device(): lax.all_to_all(send, 'row', 0, 0, tiled=True).reshape(states, window, leaf)  5.31 us
    pallas_call x1, Pallas kernels, reorder(): pl.pallas_call(_lane_gather_kernel, out_shape=(jax.ShapeDtypeStruct((rows...  4.95 us
    all_to_all x1, starting transfers between devices, per_device(): lax.all_to_all(send, 'row', 0, 0, tiled=True).reshape(states, window, leaf)  4.07 us
    dot_general x1, matrix products, per_device(): jnp.einsum('psk,pkr->psr', v_src, distant_column_factors, preferred_eleme...  1.43 us
    dot_general x1, matrix products, per_device(): jnp.einsum('psr,plr->psl', picked, distant_row_factors, preferred_element...  1.36 us
  transfers between devices with their start and end apart: 2, of which 1 were waited for; matrix products, arithmetic and copies ran while one was open for 9% of the time, Pallas kernels for 0%

profile of v21, /device:TPU:0, one launch (start us, length us, event | category | flops | bytes accessed | tf_op | source)
XLA Modules:
  0.0 60.4 jit_solution(12544159625478628875)
XLA Ops:
  0.0 0.0 copy-start
  0.0 0.0 copy-start.1
  0.0 0.0 copy-start.2
  0.0 4.9 %shard_map.82 = (bf16[4,8192]{1,0:T(4,128)(2,1)}, bf16[4,4,8192]{2,1,0:T(4,128)(2,1)}) custom-call(bf16[4,8192]{1,0:T(4,128)(2,1)} %values_ref.1, s32[64,128]{1,0:T(8,128)} %bitcast.64), custom_call_target="tpu_custom_call" | custom-call | tf_op jit(solution)/shard_map/pallas_call | solution.py:65
  5.0 6.3 %all-to-all-start = ((bf16[4,4,8192]{2,1,0:T(4,128)(2,1)}), bf16[4,4,8192]{2,1,0:T(4,128)(2,1)S(1)}, u32[]{:S(2)}, u32[]{:S(2)}) async-start(bf16[4,4,8192]{2,1,0:T(4,128)(2,1)} %get-tuple-element.7), calls=%async_computation | async-start | bytes 524288 | tf_op jit(solution)/shard_map/all_to_all | solution.py:104
  11.3 0.8 %subtract_bitcast_fusion.2 = (s32[30]{0:T(128)S(1)}, s32[30]{0:T(128)S(1)}) fusion(s32[30,2]{0,1:T(2,128)} %param.13, s32[]{:T(128)S(6)} %mul.15), kind=kLoop, calls=%fused_computation.44 | loop fusion | flops 120 | bytes 484 | tf_op jit(solution)/shard_map/sub | solution.py:154
  12.0 10.1 %all-gather = bf16[8,4,8192]{2,1,0:T(4,128)(2,1)S(1)} all-gather(bf16[1,4,8192]{2,1,0:T(4,128)(2,1)} %bitcast.63), channel_id=1, replica_groups=mesh['row'=8,'col'=4] {'row'}, dimensions={0}, use_global_device_ids=true | all-gather | bytes 589824 | tf_op jit(solution)/shard_map/all_gather | solution.py:112
  22.2 0.4 reshape.41
  22.5 0.0 copy-start.3
  22.6 0.0 copy-done.1
  22.6 0.0 copy-done.2
  22.6 0.3 convolution_convert_fusion
  23.0 1.4 %fusion.6 = f32[30,32,32]{2,1,0:T(8,128)S(1)} fusion(bf16[30,256,32]{1,2,0:T(8,128)(2,1)} %param.14, bf16[30,32,256]{2,0,1:T(8,128)(2,1)S(1)} %convolution_convert_fusion), kind=kOutput, calls=%fused_computation.10 | convolution fusion | flops 15728640 | bytes 1105920 | tf_op jit(solution)/shard_map/psk,pkr->psr/dot_general | solution.py:135
  24.4 0.0 copy-done.3
  24.4 0.2 reshape.42
  24.7 0.2 convolution_convert_fusion.2
  24.8 0.0 all-to-all-done
  24.8 0.1 slice_bitcast_fusion.1
  25.0 0.2 concatenate.10
  25.2 0.8 %all_to_all.16 = bf16[8,4,4864]{2,1,0:T(4,128)(2,1)} reshape(bf16[32,4864]{1,0:T(8,128)(2,1)S(1)} %concatenate.10) | data formatting | bytes 622592 | tf_op jit(solution)/shard_map/all_to_all | solution.py:114
  26.0 4.1 %all-to-all-start.1 = ((bf16[8,4,4864]{2,1,0:T(4,128)(2,1)}), bf16[8,4,4864]{2,1,0:T(4,128)(2,1)}, u32[]{:S(2)}, u32[]{:S(2)}) async-start(bf16[8,4,4864]{2,1,0:T(4,128)(2,1)} %all_to_all.16), calls=%async_computation.1 | async-start | bytes 622592 | tf_op jit(solution)/shard_map/all_to_all | solution.py:114
  30.1 0.1 pad_add_fusion
  30.1 0.1 reshape.43
  30.2 0.6 gather_fusion
  30.9 1.4 %fusion.10 = f32[30,32,256]{2,1,0:T(8,128)S(1)} fusion(bf16[30,256,32]{1,2,0:T(8,128)(2,1)} %param.12, bf16[30,32,32]{2,1,0:T(8,128)(2,1)S(1)} %gather_fusion, pred[30]{0:T(512)(128)(4,1)S(1)} %and_bitcast_fusion), kind=kOutput, calls=%fused_computation.14 | convolution fusion | flops 15759360 | bytes 1536030 | tf_op jit(solution)/shard_map/psr,plr->psl/dot_general | solution.py:149
  32.2 5.3 %all-to-all-done.1 = bf16[8,4,4864]{2,1,0:T(4,128)(2,1)} async-done(((bf16[8,4,4864]{2,1,0:T(4,128)(2,1)}), bf16[8,4,4864]{2,1,0:T(4,128)(2,1)}, u32[]{:S(2)}, u32[]{:S(2)}) %all-to-all-start.1) | async-done | bytes 311328 | tf_op jit(solution)/shard_map/all_to_all | solution.py:114
  37.5 1.1 %reshape.40 = bf16[32,19,256]{2,1,0:T(8,128)(2,1)S(1)} reshape(bf16[8,4,4864]{2,1,0:T(4,128)(2,1)} %all-to-all-done.1) | data formatting | bytes 622592 | tf_op jit(solution)/shard_map/reshape | solution.py:114
  38.7 0.3 fusion.5
  39.0 0.0 copy-done
  39.0 0.7 %fusion.8 = f32[16,32,256]{2,1,0:T(8,128)S(1)} fusion(bf16[16,256,256]{2,1,0:T(8,128)(2,1)S(1)} %copy-done, bf16[32,16,256]{2,1,0:T(8,128)(2,1)S(1)} %fusion.5), kind=kOutput, calls=%fused_computation.12 | convolution fusion | flops 67108864 | bytes 2883584 | tf_op jit(solution)/shard_map/snk,nlk->nsl/dot_general | solution.py:124
  39.7 0.1 pad_maximum_fusion
  39.8 0.1 slice_bitcast_fusion
  39.9 1.2 %fusion.2 = f32[32,16,256]{2,1,0:T(8,128)S(1)} fusion(f32[32,256,46]{1,0,2:T(8,128)S(1)} %slice_bitcast_fusion, s32[46]{0:T(128)S(1)} %pad_add_fusion), kind=kOutput, calls=%fused_computation.6 | convolution fusion | flops 36176608 | bytes 2031800 | tf_op jit(solution)/shard_map/dot_general | solution.py:158
  41.1 0.1 all_to_all.18
  41.2 18.5 %all_to_all.23 = f32[4,8,4096]{2,1,0:T(8,128)S(1)} all-to-all(f32[4,8,4096]{2,1,0:T(8,128)S(1)} %all_to_all.18), channel_id=1, replica_groups=mesh['row'=8,'col'=4] {'col'}, dimensions={0} | all-to-all | bytes 1048576 | tf_op jit(solution)/shard_map/all_to_all | solution.py:165
  59.7 0.7 %reduce_sum.9 = f32[8,4096]{1,0:T(8,128)} reduce(f32[4,8,4096]{2,1,0:T(8,128)S(1)} %all_to_all.23, f32[]{:T(128)} %constant.52.clone.1), dimensions={0}, to_apply=%region_0.1 | reduce | flops 98304 | bytes 655364 | tf_op jit(solution)/shard_map/reduce_sum | solution.py:166
  (4 shorter events, 0.0 us)
Async XLA Ops:
  0.0 39.0 %copy-start = (bf16[16,256,256]{2,1,0:T(8,128)(2,1)S(1)}, bf16[16,256,256]{2,1,0:T(8,128)(2,1)}, u32[]{:S(2)}) copy-start(bf16[16,256,256]{2,1,0:T(8,128)(2,1)} %param.10) | copy-start | bytes 6291460
  0.0 22.6 %copy-start.1 = (s32[16,2]{0,1:T(2,128)S(1)}, s32[16,2]{0,1:T(2,128)}, u32[]{:S(2)}) copy-start(s32[16,2]{0,1:T(2,128)} %param.11) | copy-start | bytes 388
  0.0 22.6 %copy-start.2 = (s32[30,2]{0,1:T(2,128)S(1)}, s32[30,2]{0,1:T(2,128)}, u32[]{:S(2)}) copy-start(s32[30,2]{0,1:T(2,128)} %param.15) | copy-start | bytes 724
  5.0 19.9 %all-to-all-start = ((bf16[4,4,8192]{2,1,0:T(4,128)(2,1)}), bf16[4,4,8192]{2,1,0:T(4,128)(2,1)S(1)}, u32[]{:S(2)}, u32[]{:S(2)}) async-start(bf16[4,4,8192]{2,1,0:T(4,128)(2,1)} %get-tuple-element.7), calls=%async_computation | async-start | bytes 524288 | tf_op jit(solution)/shard_map/all_to_all | solution.py:104
  22.5 1.8 %copy-start.3 = (s32[30,2]{0,1:T(2,128)S(1)}, s32[30,2]{0,1:T(2,128)}, u32[]{:S(2)}) copy-start(s32[30,2]{0,1:T(2,128)} %param.13) | copy-start | bytes 724
  26.0 11.6 %all-to-all-start.1 = ((bf16[8,4,4864]{2,1,0:T(4,128)(2,1)}), bf16[8,4,4864]{2,1,0:T(4,128)(2,1)}, u32[]{:S(2)}, u32[]{:S(2)}) async-start(bf16[8,4,4864]{2,1,0:T(4,128)(2,1)} %all_to_all.16), calls=%async_computation.1 | async-start | bytes 622592 | tf_op jit(solution)/shard_map/all_to_all | solution.py:114

commit v22 on v20

--- a/solution.py
+++ b/solution.py
@@ -118,11 +118,11 @@
     near_cols = adjacent_cluster_pairs[:, 1] - home * cluster_extent - start
     near_rows = adjacent_cluster_pairs[:, 0] - row_index * row_span
     pick = (near_cols[:, None] == jnp.arange(window, dtype=jnp.int32)[None, :]).astype(near_window.dtype)
-    near_src = jnp.einsum("nw,swk->snk", pick, near_window, preferred_element_type=jnp.float32).astype(
+    near_src = jnp.einsum("nw,swk->nsk", pick, near_window, preferred_element_type=jnp.float32).astype(
         near_window.dtype
     )
     near_out = jnp.einsum(
-        "snk,nlk->nsl", near_src, adjacent_dense_blocks, preferred_element_type=jnp.float32
+        "nsk,nlk->nsl", near_src, adjacent_dense_blocks, preferred_element_type=jnp.float32
     )
 
     v_pick = (

time: 60.9 us -> 60.9 us (level)
  no operation moved by 1% of the time
where the time goes in v22:
time: 60.9 us; the launch traced here: 60.4 us
  blocking collectives  28.6 us (47%)
  starting transfers between devices  10.4 us (17%)
  matrix products  5.46 us (9%)
  waiting for transfers between devices  5.3 us (9%)
  Pallas kernels  4.95 us (8%)
  local copies, waits for them, and re-layouts  3.78 us (6%)
  other arithmetic  1.68 us (3%)
    all_to_all x1, blocking collectives, per_device(): exchanged = lax.all_to_all(partial_sum, 'col', 0, 0, tiled=True)  18.5 us
    all_gather x1, blocking collectives, per_device(): ordered = lax.all_gather(mine, 'row', axis=0, tiled=True)  10.1 us
    all_to_all x1, starting transfers between devices, per_device(): every_block = lax.all_to_all(stacked, 'col', 0, 0, tiled=True)  6.32 us
    all_to_all x1, waiting for transfers between devices, per_device(): lax.all_to_all(send, 'row', 0, 0, tiled=True).reshape(states, window, leaf)  5.3 us
    pallas_call x1, Pallas kernels, reorder(): pl.pallas_call(_lane_gather_kernel, out_shape=(jax.ShapeDtypeStruct((rows...  4.95 us
    all_to_all x1, starting transfers between devices, per_device(): lax.all_to_all(send, 'row', 0, 0, tiled=True).reshape(states, window, leaf)  4.07 us
    dot_general x1, matrix products, per_device(): jnp.einsum('spk,pkr->psr', v_src, distant_column_factors, preferred_eleme...  1.43 us
    dot_general x1, matrix products, per_device(): jnp.einsum('psr,plr->psl', picked, distant_row_factors, preferred_element...  1.37 us
  transfers between devices with their start and end apart: 2, of which 1 were waited for; matrix products, arithmetic and copies ran while one was open for 9% of the time, Pallas kernels for 0%

profile of v22, /device:TPU:0, one launch (start us, length us, event | category | flops | bytes accessed | tf_op | source)
XLA Modules:
  0.0 60.4 jit_solution(1416888340716589448)
XLA Ops:
  0.0 0.0 copy-start
  0.0 0.0 copy-start.1
  0.0 0.0 copy-start.2
  0.0 4.9 %shard_map.82 = (bf16[4,8192]{1,0:T(4,128)(2,1)}, bf16[4,4,8192]{2,1,0:T(4,128)(2,1)}) custom-call(bf16[4,8192]{1,0:T(4,128)(2,1)} %values_ref.1, s32[64,128]{1,0:T(8,128)} %bitcast.64), custom_call_target="tpu_custom_call" | custom-call | tf_op jit(solution)/shard_map/pallas_call | solution.py:65
  5.0 6.3 %all-to-all-start = ((bf16[4,4,8192]{2,1,0:T(4,128)(2,1)}), bf16[4,4,8192]{2,1,0:T(4,128)(2,1)S(1)}, u32[]{:S(2)}, u32[]{:S(2)}) async-start(bf16[4,4,8192]{2,1,0:T(4,128)(2,1)} %get-tuple-element.7), calls=%async_computation | async-start | bytes 524288 | tf_op jit(solution)/shard_map/all_to_all | solution.py:104
  11.3 0.8 %subtract_bitcast_fusion.2 = (s32[30]{0:T(128)S(1)}, s32[30]{0:T(128)S(1)}) fusion(s32[30,2]{0,1:T(2,128)} %param.13, s32[]{:T(128)S(6)} %mul.15), kind=kLoop, calls=%fused_computation.44 | loop fusion | flops 120 | bytes 484 | tf_op jit(solution)/shard_map/sub | solution.py:154
  12.0 10.1 %all-gather = bf16[8,4,8192]{2,1,0:T(4,128)(2,1)S(1)} all-gather(bf16[1,4,8192]{2,1,0:T(4,128)(2,1)} %bitcast.63), channel_id=1, replica_groups=mesh['row'=8,'col'=4] {'row'}, dimensions={0}, use_global_device_ids=true | all-gather | bytes 589824 | tf_op jit(solution)/shard_map/all_gather | solution.py:112
  22.2 0.4 reshape.41
  22.5 0.0 copy-start.3
  22.6 0.0 copy-done.1
  22.6 0.0 copy-done.2
  22.6 0.3 fusion.2
  23.0 1.4 %fusion.6 = f32[30,32,32]{2,1,0:T(8,128)S(1)} fusion(bf16[30,256,32]{1,2,0:T(8,128)(2,1)} %param.14, bf16[32,30,256]{2,1,0:T(8,128)(2,1)S(1)} %fusion.2), kind=kOutput, calls=%fused_computation.10 | convolution fusion | flops 15728640 | bytes 1105920 | tf_op jit(solution)/shard_map/spk,pkr->psr/dot_general | solution.py:135
  24.4 0.0 copy-done.3
  24.4 0.2 reshape.42
  24.7 0.2 convolution_convert_fusion.2
  24.8 0.0 all-to-all-done
  24.8 0.1 slice_bitcast_fusion.1
  25.0 0.2 concatenate.10
  25.2 0.8 %all_to_all.16 = bf16[8,4,4864]{2,1,0:T(4,128)(2,1)} reshape(bf16[32,4864]{1,0:T(8,128)(2,1)S(1)} %concatenate.10) | data formatting | bytes 622592 | tf_op jit(solution)/shard_map/all_to_all | solution.py:114
  26.0 4.1 %all-to-all-start.1 = ((bf16[8,4,4864]{2,1,0:T(4,128)(2,1)}), bf16[8,4,4864]{2,1,0:T(4,128)(2,1)}, u32[]{:S(2)}, u32[]{:S(2)}) async-start(bf16[8,4,4864]{2,1,0:T(4,128)(2,1)} %all_to_all.16), calls=%async_computation.1 | async-start | bytes 622592 | tf_op jit(solution)/shard_map/all_to_all | solution.py:114
  30.1 0.1 pad_add_fusion
  30.1 0.1 reshape.43
  30.3 0.6 gather_fusion
  30.9 1.4 %fusion.10 = f32[30,32,256]{2,1,0:T(8,128)S(1)} fusion(bf16[30,256,32]{1,2,0:T(8,128)(2,1)} %param.12, bf16[30,32,32]{2,1,0:T(8,128)(2,1)S(1)} %gather_fusion, pred[30]{0:T(512)(128)(4,1)S(1)} %and_bitcast_fusion), kind=kOutput, calls=%fused_computation.14 | convolution fusion | flops 15759360 | bytes 1536030 | tf_op jit(solution)/shard_map/psr,plr->psl/dot_general | solution.py:149
  32.2 5.3 %all-to-all-done.1 = bf16[8,4,4864]{2,1,0:T(4,128)(2,1)} async-done(((bf16[8,4,4864]{2,1,0:T(4,128)(2,1)}), bf16[8,4,4864]{2,1,0:T(4,128)(2,1)}, u32[]{:S(2)}, u32[]{:S(2)}) %all-to-all-start.1) | async-done | bytes 311328 | tf_op jit(solution)/shard_map/all_to_all | solution.py:114
  37.5 1.1 %reshape.40 = bf16[32,19,256]{2,1,0:T(8,128)(2,1)S(1)} reshape(bf16[8,4,4864]{2,1,0:T(4,128)(2,1)} %all-to-all-done.1) | data formatting | bytes 622592 | tf_op jit(solution)/shard_map/reshape | solution.py:114
  38.7 0.3 convolution_convert_fusion.1
  39.0 0.0 copy-done
  39.0 0.7 %fusion.8 = f32[16,32,256]{2,1,0:T(8,128)S(1)} fusion(bf16[16,256,256]{2,1,0:T(8,128)(2,1)S(1)} %copy-done, bf16[16,32,256]{2,0,1:T(8,128)(2,1)S(1)} %convolution_convert_fusion.1), kind=kOutput, calls=%fused_computation.12 | convolution fusion | flops 67108864 | bytes 2883584 | tf_op jit(solution)/shard_map/nsk,nlk->nsl/dot_general | solution.py:124
  39.7 0.1 pad_maximum_fusion
  39.8 0.1 slice_bitcast_fusion
  39.9 1.2 %fusion.3 = f32[32,16,256]{2,1,0:T(8,128)S(1)} fusion(f32[32,256,46]{1,0,2:T(8,128)S(1)} %slice_bitcast_fusion, s32[46]{0:T(128)S(1)} %pad_add_fusion), kind=kOutput, calls=%fused_computation.7 | convolution fusion | flops 36176608 | bytes 2031800 | tf_op jit(solution)/shard_map/dot_general | solution.py:158
  41.1 0.1 all_to_all.18
  41.2 18.5 %all_to_all.23 = f32[4,8,4096]{2,1,0:T(8,128)S(1)} all-to-all(f32[4,8,4096]{2,1,0:T(8,128)S(1)} %all_to_all.18), channel_id=1, replica_groups=mesh['row'=8,'col'=4] {'col'}, dimensions={0} | all-to-all | bytes 1048576 | tf_op jit(solution)/shard_map/all_to_all | solution.py:165
  59.7 0.7 %reduce_sum.9 = f32[8,4096]{1,0:T(8,128)} reduce(f32[4,8,4096]{2,1,0:T(8,128)S(1)} %all_to_all.23, f32[]{:T(128)} %constant.52.clone.1), dimensions={0}, to_apply=%region_0.1 | reduce | flops 98304 | bytes 655364 | tf_op jit(solution)/shard_map/reduce_sum | solution.py:166
  (4 shorter events, 0.0 us)
Async XLA Ops:
  0.0 39.0 %copy-start = (bf16[16,256,256]{2,1,0:T(8,128)(2,1)S(1)}, bf16[16,256,256]{2,1,0:T(8,128)(2,1)}, u32[]{:S(2)}) copy-start(bf16[16,256,256]{2,1,0:T(8,128)(2,1)} %param.10) | copy-start | bytes 6291460
  0.0 22.6 %copy-start.1 = (s32[16,2]{0,1:T(2,128)S(1)}, s32[16,2]{0,1:T(2,128)}, u32[]{:S(2)}) copy-start(s32[16,2]{0,1:T(2,128)} %param.11) | copy-start | bytes 388
  0.0 22.6 %copy-start.2 = (s32[30,2]{0,1:T(2,128)S(1)}, s32[30,2]{0,1:T(2,128)}, u32[]{:S(2)}) copy-start(s32[30,2]{0,1:T(2,128)} %param.15) | copy-start | bytes 724
  5.0 19.9 %all-to-all-start = ((bf16[4,4,8192]{2,1,0:T(4,128)(2,1)}), bf16[4,4,8192]{2,1,0:T(4,128)(2,1)S(1)}, u32[]{:S(2)}, u32[]{:S(2)}) async-start(bf16[4,4,8192]{2,1,0:T(4,128)(2,1)} %get-tuple-element.7), calls=%async_computation | async-start | bytes 524288 | tf_op jit(solution)/shard_map/all_to_all | solution.py:104
  22.5 1.9 %copy-start.3 = (s32[30,2]{0,1:T(2,128)S(1)}, s32[30,2]{0,1:T(2,128)}, u32[]{:S(2)}) copy-start(s32[30,2]{0,1:T(2,128)} %param.13) | copy-start | bytes 724
  26.0 11.6 %all-to-all-start.1 = ((bf16[8,4,4864]{2,1,0:T(4,128)(2,1)}), bf16[8,4,4864]{2,1,0:T(4,128)(2,1)}, u32[]{:S(2)}, u32[]{:S(2)}) async-start(bf16[8,4,4864]{2,1,0:T(4,128)(2,1)} %all_to_all.16), calls=%async_computation.1 | async-start | bytes 622592 | tf_op jit(solution)/shard_map/all_to_all | solution.py:114

commit v23 on v20

--- a/solution.py
+++ b/solution.py
@@ -9,7 +9,7 @@
 REACH = 3
 LANES = 128
 SUBLANES = 8
-BATCH = 16
+BATCH = 32
 
 
 def _lane_gather_kernel(values_ref, order_ref, out_ref, copies_ref):

time: 60.9 us -> 60.9 us (level)
  no operation moved by 1% of the time
where the time goes in v23:
time: 60.9 us; the launch traced here: 60.3 us
  blocking collectives  28.6 us (47%)
  starting transfers between devices  10.4 us (17%)
  matrix products  5.46 us (9%)
  waiting for transfers between devices  5.31 us (9%)
  Pallas kernels  4.91 us (8%)
  local copies, waits for them, and re-layouts  3.78 us (6%)
  other arithmetic  1.68 us (3%)
    all_to_all x1, blocking collectives, per_device(): exchanged = lax.all_to_all(partial_sum, 'col', 0, 0, tiled=True)  18.5 us
    all_gather x1, blocking collectives, per_device(): ordered = lax.all_gather(mine, 'row', axis=0, tiled=True)  10.1 us
    all_to_all x1, starting transfers between devices, per_device(): every_block = lax.all_to_all(stacked, 'col', 0, 0, tiled=True)  6.32 us
    all_to_all x1, waiting for transfers between devices, per_device(): lax.all_to_all(send, 'row', 0, 0, tiled=True).reshape(states, window, leaf)  5.31 us
    pallas_call x1, Pallas kernels, reorder(): pl.pallas_call(_lane_gather_kernel, out_shape=(jax.ShapeDtypeStruct((rows...  4.91 us
    all_to_all x1, starting transfers between devices, per_device(): lax.all_to_all(send, 'row', 0, 0, tiled=True).reshape(states, window, leaf)  4.07 us
    dot_general x1, matrix products, per_device(): jnp.einsum('spk,pkr->psr', v_src, distant_column_factors, preferred_eleme...  1.43 us
    dot_general x1, matrix products, per_device(): jnp.einsum('psr,plr->psl', picked, distant_row_factors, preferred_element...  1.36 us
  transfers between devices with their start and end apart: 2, of which 1 were waited for; matrix products, arithmetic and copies ran while one was open for 9% of the time, Pallas kernels for 0%

profile of v23, /device:TPU:0, one launch (start us, length us, event | category | flops | bytes accessed | tf_op | source)
XLA Modules:
  0.0 60.3 jit_solution(14462272153788513322)
XLA Ops:
  0.0 0.0 copy-start
  0.0 0.0 copy-start.1
  0.0 0.0 copy-start.2
  0.0 4.9 %shard_map.82 = (bf16[4,8192]{1,0:T(4,128)(2,1)}, bf16[4,4,8192]{2,1,0:T(4,128)(2,1)}) custom-call(bf16[4,8192]{1,0:T(4,128)(2,1)} %values_ref.1, s32[64,128]{1,0:T(8,128)} %bitcast.66), custom_call_target="tpu_custom_call" | custom-call | tf_op jit(solution)/shard_map/pallas_call | solution.py:65
  4.9 6.3 %all-to-all-start = ((bf16[4,4,8192]{2,1,0:T(4,128)(2,1)}), bf16[4,4,8192]{2,1,0:T(4,128)(2,1)S(1)}, u32[]{:S(2)}, u32[]{:S(2)}) async-start(bf16[4,4,8192]{2,1,0:T(4,128)(2,1)} %get-tuple-element.7), calls=%async_computation | async-start | bytes 524288 | tf_op jit(solution)/shard_map/all_to_all | solution.py:104
  11.2 0.8 %subtract_bitcast_fusion.2 = (s32[30]{0:T(128)S(1)}, s32[30]{0:T(128)S(1)}) fusion(s32[30,2]{0,1:T(2,128)} %param.13, s32[]{:T(128)S(6)} %mul.15), kind=kLoop, calls=%fused_computation.45 | loop fusion | flops 120 | bytes 484 | tf_op jit(solution)/shard_map/sub | solution.py:154
  12.0 10.1 %all-gather = bf16[8,4,8192]{2,1,0:T(4,128)(2,1)S(1)} all-gather(bf16[1,4,8192]{2,1,0:T(4,128)(2,1)} %bitcast.65), channel_id=1, replica_groups=mesh['row'=8,'col'=4] {'row'}, dimensions={0}, use_global_device_ids=true | all-gather | bytes 589824 | tf_op jit(solution)/shard_map/all_gather | solution.py:112
  22.1 0.4 reshape.41
  22.5 0.0 copy-start.3
  22.5 0.0 copy-done.1
  22.5 0.0 copy-done.2
  22.6 0.3 fusion.2
  22.9 1.4 %fusion.7 = f32[30,32,32]{2,1,0:T(8,128)S(1)} fusion(bf16[30,256,32]{1,2,0:T(8,128)(2,1)} %param.14, bf16[32,30,256]{2,1,0:T(8,128)(2,1)S(1)} %fusion.2), kind=kOutput, calls=%fused_computation.11 | convolution fusion | flops 15728640 | bytes 1105920 | tf_op jit(solution)/shard_map/spk,pkr->psr/dot_general | solution.py:135
  24.3 0.0 copy-done.3
  24.4 0.2 reshape.42
  24.6 0.2 convolution_convert_fusion.2
  24.8 0.0 all-to-all-done
  24.8 0.1 slice_bitcast_fusion.1
  24.9 0.2 concatenate.10
  25.1 0.8 %all_to_all.16 = bf16[8,4,4864]{2,1,0:T(4,128)(2,1)} reshape(bf16[32,4864]{1,0:T(8,128)(2,1)S(1)} %concatenate.10) | data formatting | bytes 622592 | tf_op jit(solution)/shard_map/all_to_all | solution.py:114
  25.9 4.1 %all-to-all-start.1 = ((bf16[8,4,4864]{2,1,0:T(4,128)(2,1)}), bf16[8,4,4864]{2,1,0:T(4,128)(2,1)}, u32[]{:S(2)}, u32[]{:S(2)}) async-start(bf16[8,4,4864]{2,1,0:T(4,128)(2,1)} %all_to_all.16), calls=%async_computation.1 | async-start | bytes 622592 | tf_op jit(solution)/shard_map/all_to_all | solution.py:114
  30.0 0.1 pad_add_fusion
  30.1 0.1 reshape.43
  30.2 0.6 gather_fusion
  30.8 1.4 %fusion.11 = f32[30,32,256]{2,1,0:T(8,128)S(1)} fusion(bf16[30,256,32]{1,2,0:T(8,128)(2,1)} %param.12, bf16[30,32,32]{2,1,0:T(8,128)(2,1)S(1)} %gather_fusion, pred[30]{0:T(512)(128)(4,1)S(1)} %and_bitcast_fusion), kind=kOutput, calls=%fused_computation.15 | convolution fusion | flops 15759360 | bytes 1536030 | tf_op jit(solution)/shard_map/psr,plr->psl/dot_general | solution.py:149
  32.2 5.3 %all-to-all-done.1 = bf16[8,4,4864]{2,1,0:T(4,128)(2,1)} async-done(((bf16[8,4,4864]{2,1,0:T(4,128)(2,1)}), bf16[8,4,4864]{2,1,0:T(4,128)(2,1)}, u32[]{:S(2)}, u32[]{:S(2)}) %all-to-all-start.1) | async-done | bytes 311328 | tf_op jit(solution)/shard_map/all_to_all | solution.py:114
  37.5 1.1 %reshape.40 = bf16[32,19,256]{2,1,0:T(8,128)(2,1)S(1)} reshape(bf16[8,4,4864]{2,1,0:T(4,128)(2,1)} %all-to-all-done.1) | data formatting | bytes 622592 | tf_op jit(solution)/shard_map/reshape | solution.py:114
  38.6 0.3 fusion.6
  38.9 0.0 copy-done
  38.9 0.7 %fusion.9 = f32[16,32,256]{2,1,0:T(8,128)S(1)} fusion(bf16[16,256,256]{2,1,0:T(8,128)(2,1)S(1)} %copy-done, bf16[32,16,256]{2,1,0:T(8,128)(2,1)S(1)} %fusion.6), kind=kOutput, calls=%fused_computation.13 | convolution fusion | flops 67108864 | bytes 2883584 | tf_op jit(solution)/shard_map/snk,nlk->nsl/dot_general | solution.py:124
  39.6 0.1 pad_maximum_fusion
  39.8 0.1 slice_bitcast_fusion
  39.9 1.2 %fusion.3 = f32[32,16,256]{2,1,0:T(8,128)S(1)} fusion(f32[32,256,46]{1,0,2:T(8,128)S(1)} %slice_bitcast_fusion, s32[46]{0:T(128)S(1)} %pad_add_fusion), kind=kOutput, calls=%fused_computation.7 | convolution fusion | flops 36176608 | bytes 2031800 | tf_op jit(solution)/shard_map/dot_general | solution.py:158
  41.1 0.1 all_to_all.18
  41.2 18.5 %all_to_all.23 = f32[4,8,4096]{2,1,0:T(8,128)S(1)} all-to-all(f32[4,8,4096]{2,1,0:T(8,128)S(1)} %all_to_all.18), channel_id=1, replica_groups=mesh['row'=8,'col'=4] {'col'}, dimensions={0} | all-to-all | bytes 1048576 | tf_op jit(solution)/shard_map/all_to_all | solution.py:165
  59.6 0.7 %reduce_sum.9 = f32[8,4096]{1,0:T(8,128)} reduce(f32[4,8,4096]{2,1,0:T(8,128)S(1)} %all_to_all.23, f32[]{:T(128)} %constant.52.clone.1), dimensions={0}, to_apply=%region_0.1 | reduce | flops 98304 | bytes 655364 | tf_op jit(solution)/shard_map/reduce_sum | solution.py:166
  (4 shorter events, 0.0 us)
Async XLA Ops:
  0.0 38.9 %copy-start = (bf16[16,256,256]{2,1,0:T(8,128)(2,1)S(1)}, bf16[16,256,256]{2,1,0:T(8,128)(2,1)}, u32[]{:S(2)}) copy-start(bf16[16,256,256]{2,1,0:T(8,128)(2,1)} %param.10) | copy-start | bytes 6291460
  0.0 22.5 %copy-start.1 = (s32[16,2]{0,1:T(2,128)S(1)}, s32[16,2]{0,1:T(2,128)}, u32[]{:S(2)}) copy-start(s32[16,2]{0,1:T(2,128)} %param.11) | copy-start | bytes 388
  0.0 22.5 %copy-start.2 = (s32[30,2]{0,1:T(2,128)S(1)}, s32[30,2]{0,1:T(2,128)}, u32[]{:S(2)}) copy-start(s32[30,2]{0,1:T(2,128)} %param.15) | copy-start | bytes 724
  4.9 19.9 %all-to-all-start = ((bf16[4,4,8192]{2,1,0:T(4,128)(2,1)}), bf16[4,4,8192]{2,1,0:T(4,128)(2,1)S(1)}, u32[]{:S(2)}, u32[]{:S(2)}) async-start(bf16[4,4,8192]{2,1,0:T(4,128)(2,1)} %get-tuple-element.7), calls=%async_computation | async-start | bytes 524288 | tf_op jit(solution)/shard_map/all_to_all | solution.py:104
  22.5 1.8 %copy-start.3 = (s32[30,2]{0,1:T(2,128)S(1)}, s32[30,2]{0,1:T(2,128)}, u32[]{:S(2)}) copy-start(s32[30,2]{0,1:T(2,128)} %param.13) | copy-start | bytes 724
  25.9 11.6 %all-to-all-start.1 = ((bf16[8,4,4864]{2,1,0:T(4,128)(2,1)}), bf16[8,4,4864]{2,1,0:T(4,128)(2,1)}, u32[]{:S(2)}, u32[]{:S(2)}) async-start(bf16[8,4,4864]{2,1,0:T(4,128)(2,1)} %all_to_all.16), calls=%async_computation.1 | async-start | bytes 622592 | tf_op jit(solution)/shard_map/all_to_all | solution.py:114
